TPU v7x, 128 devices: a whole 4x4x4 slice. The times are simulated.
128 devices in a mesh: loop: 16 (over x_hi, z, core), width: 8 (over x_lo, y).
Axes of the slice: x: 4 (x_hi: 2, x_lo: 2; x = x_hi * 2 + x_lo), y: 4, z: 4, core: 2. Of those that a mesh axis runs over, the one named last changes fastest.
Arguments:
- queries: bfloat16 [16384, 4096], P('loop', 'width'), may hold values from -0.0625 to 0.0625
- passages: bfloat16 [16384, 4096], P('loop', 'width'), may hold values from -0.0625 to 0.0625
- teacher: bfloat16 [16384, 4096], P('loop'), may hold values from -5 to 12
- positives: int32 [16384], P('loop'), may hold values from 0 to 4095
Outputs:
- grad_queries: float32 [16384, 4096], P('loop', 'width')
- grad_passages: float32 [16384, 4096], P('loop', 'width')
All inputs are finite; a program needn't handle non-finite values.
Results may differ from a plain program's by a relative error of at most 0.0003.
Values may be sent and summed in bfloat16 or wider, within the bound.
No kernel may reach another device: no remote copies, remote signals or barrier semaphores. Data moves between devices by JAX's collectives and lax.ppermute only.
A program may use at most 192 MiB of HBM per device.

v0:
```python
import jax
import jax.numpy as jnp
from jax import lax
from jax.sharding import PartitionSpec as P

STEPS = 4


SCALE = 20.0


def shifted(block, axis, distance):
    devices = range(lax.axis_size(axis))
    route = [((i - distance) % len(devices), i) for i in devices]
    return lax.ppermute(block, axis, route)


def slopes_of(scores, teacher, positives):
    teach = teacher.astype(jnp.float32)
    index = positives[:, None]
    s_pos = jnp.take_along_axis(scores, index, 1)
    t_pos = jnp.take_along_axis(teach, index, 1)
    errors = s_pos - scores - (t_pos - teach)
    total = jnp.sum(errors, 1, keepdims=True)
    column = lax.broadcasted_iota(jnp.int32, scores.shape, 1)
    hit = (column == index).astype(jnp.float32)
    coef = SCALE * 2.0 / (scores.shape[1] - 1)
    return coef * (hit * total - errors)


def per_device(queries, passages, teacher, positives):
    rows = queries.shape[0]
    held = [passages]
    current = passages
    for step in range(1, STEPS):
        current = shifted(current, "loop", 1)
        held.append(current)

    def partial_value(block):
        return jnp.einsum("qd,pd->qp", queries, block, preferred_element_type=jnp.float32)

    tiles = [lax.psum(partial_value(block), "width") for block in held]
    scores = SCALE * jnp.concatenate(tiles, 1)
    slopes = slopes_of(scores, teacher, positives)
    query_wide = queries.astype(jnp.float32)
    grad_q = jnp.zeros(queries.shape, jnp.float32)
    terms = []
    for step in range(STEPS):
        block_slopes = slopes[:, step * rows : (step + 1) * rows]
        grad_q = grad_q + jnp.dot(
            block_slopes,
            held[step].astype(jnp.float32),
            precision=lax.Precision.HIGHEST,
            preferred_element_type=jnp.float32,
        )
        term = jnp.dot(
            block_slopes.T,
            query_wide,
            precision=lax.Precision.HIGHEST,
            preferred_element_type=jnp.float32,
        )
        terms.append(term)
    grad_p = terms[0]
    pending = jnp.stack(terms[1:], 0)
    for step in range(1, STEPS):
        pending = shifted(pending, "loop", -1)
        grad_p = grad_p + pending[0]
        pending = pending[1:]
    return (grad_q, grad_p)


def solution(mesh):
    in_specs = (P("loop", "width"), P("loop", "width"), P("loop", None), P("loop"))
    out_specs = (P("loop", "width"), P("loop", "width"))
    return jax.shard_map(
        per_device, mesh=mesh, in_specs=in_specs, out_specs=out_specs, check_vma=False
    )
```

profile of v0, /device:TPU:0, one launch (start us, length us, event | category | flops | bytes accessed | tf_op | source)
XLA Modules:
  0.0 632.5 jit_solution(11738128215469655900)
XLA Ops:
  7.2 0.0 copy-start
  7.2 0.0 all-reduce.3.cloned.1.call-start
  7.2 0.1 collective-permute-start
  7.3 18.7 %collective-permute-done = bf16[1024,512]{1,0:T(8,128)(2,1)S(1)} collective-permute-done((bf16[1024,512]{1,0:T(8,128)(2,1)}, bf16[1024,512]{1,0:T(8,128)(2,1)S(1)}, u32[]{:S(2)}, u32[]{:S(2)}) %collective-permute-start) | collective-permute-done | bytes 1048608 | tf_op jit(solution)/shard_map/ppermute | solution.py:15
  26.0 0.0 copy-start.3
  26.0 0.0 collective-permute-start.1
  26.0 17.8 %collective-permute-done.1 = bf16[1024,512]{1,0:T(8,128)(2,1)S(1)} collective-permute-done((bf16[1024,512]{1,0:T(8,128)(2,1)S(1)}, bf16[1024,512]{1,0:T(8,128)(2,1)S(1)}, u32[]{:S(2)}, u32[]{:S(2)}) %collective-permute-start.1) | collective-permute-done | bytes 1048608 | tf_op jit(solution)/shard_map/ppermute | solution.py:15
  43.9 0.0 copy-start.5
  43.9 0.0 collective-permute-start.2
  43.9 0.0 copy-done
  43.9 4.8 fusion.35
  48.7 3.3 fusion.36
  52.0 0.0 copy-done.3
  52.0 0.0 copy-done.5
  52.0 3.3 fusion.37
  55.3 6.4 %collective-permute-done.2 = bf16[1024,512]{1,0:T(8,128)(2,1)S(1)} collective-permute-done((bf16[1024,512]{1,0:T(8,128)(2,1)S(1)}, bf16[1024,512]{1,0:T(8,128)(2,1)S(1)}, u32[]{:S(2)}, u32[]{:S(2)}) %collective-permute-start.2) | collective-permute-done | bytes 1048608 | tf_op jit(solution)/shard_map/ppermute | solution.py:15
  61.7 0.0 copy-start.7
  61.7 1.0 copy-done.7
  62.7 3.2 fusion.38
  65.9 0.0 all-reduce.3.cloned.1.call-update
  66.0 0.0 copy-start.9
  66.0 12.0 %convert_element_type.2 = f32[1024,4096]{1,0:T(8,128)} convert(bf16[1024,4096]{1,0:T(8,128)(2,1)} %param.8) | non-fusion elementwise | flops 4194304 | bytes 25165824 | tf_op jit(solution)/shard_map/convert_element_type | solution.py:19
  78.0 0.0 copy-done.9
  78.0 13.2 %gather_fusion.1 = f32[1024]{0:T(1024)S(1)} fusion(f32[1024,4096]{1,0:T(8,128)} %convert_element_type.2, s32[1024]{0:T(1024)S(1)} %bitcast.49), kind=kCustom, calls=%fused_computation.1.clone | custom fusion | bytes 16384 | tf_op jit(solution)/shard_map/jit(take_along_axis)/gather | solution.py:22
  91.2 314.8 %all-reduce.3.cloned.1.call-done = (f32[1024,1024]{1,0:T(8,128)}, f32[1024,1024]{1,0:T(8,128)}, f32[1024,1024]{1,0:T(8,128)}, f32[1024,1024]{1,0:T(8,128)}) async-done(((f32[1024,1024]{1,0:T(8,128)}, f32[1024,1024]{1,0:T(8,128)}, f32[1024,1024]{1,0:T(8,128)}, f32[1024,1024]{1,0:T(8,128)}), (f32[1024,1024]{1,0:T(8,128)}, f32[1024,1024]{1,0:T(8,128)}, f32[1024,1024]{1,0:T(8,128)}, ...) | async-done | bytes 16777232 | tf_op jit(solution)/shard_map/psum | solution.py:42
  406.0 11.6 %maximum_multiply_fusion = f32[1024,4096]{1,0:T(8,128)} fusion(f32[1024,1024]{1,0:T(8,128)} %get-tuple-element.3, f32[1024,1024]{1,0:T(8,128)} %get-tuple-element.4, f32[1024,1024]{1,0:T(8,128)} %get-tuple-element.5, f32[1024,1024]{1,0:T(8,128)} %get-tuple-element.6), kind=kLoop, calls=%fused_computation.2 | loop fusion | flops 16777216 | bytes 33554432 | tf_op jit(solution)/shard_map/mul | solution.py:43
  417.6 13.2 %gather_fusion = f32[1024]{0:T(1024)S(1)} fusion(f32[1024,4096]{1,0:T(8,128)} %maximum_multiply_fusion, s32[1024]{0:T(1024)S(1)} %bitcast.50), kind=kCustom, calls=%fused_computation.clone | custom fusion | bytes 16384 | tf_op jit(solution)/shard_map/jit(take_along_axis)/gather | solution.py:21
  430.9 0.0 copy-start.1
  430.9 9.7 %fusion.19 = f32[1024]{0:T(1024)S(1)} fusion(bf16[1024,4096]{1,0:T(8,128)(2,1)} %param.8, f32[1024]{0:T(1024)S(1)} %bitcast.53, f32[1024]{0:T(1024)S(1)} %bitcast.51, f32[1024,1024]{1,0:T(8,128)} %get-tuple-element.3, f32[1024,1024]{1,0:T(8,128)} %get-tuple-element.4, f32[1024,1024]{1,0:T(8,128)} %get-tuple-element.5, f32[1024,1024]{1,0:T(8,128)} %get-tuple-element.6), kind=kLoop, calls=%fused_computation.29 | loop fusion | flops 37747712 | bytes 25178112 | tf_op jit(solution)/shard_map/reduce_sum | solution.py:24
  440.6 0.0 copy-done.1
  440.6 10.7 %subtract_multiply_fusion = f32[1024,4096]{1,0:T(8,128)S(1)} fusion(f32[1024]{0:T(1024)S(1)} %fusion.19, s32[1024]{0:T(1024)S(1)} %copy-done.9, bf16[1024,4096]{1,0:T(8,128)(2,1)} %param.8, f32[1024]{0:T(1024)S(1)} %bitcast.54, f32[1024]{0:T(1024)S(1)} %bitcast.52, f32[1024,1024]{1,0:T(8,128)S(1)} %copy-done.1, f32[1024,1024]{1,0:T(8,128)} %get-tuple-element.4, ...), kind=kLoop, calls=%fused_computation.3 | loop fusion | flops 50331648 | bytes 41959424 | tf_op jit(solution)/shard_map/mul | solution.py:28
  451.3 3.6 fusion.20
  454.8 3.6 fusion.23
  458.4 3.6 fusion.26
  462.0 3.4 pad_maximum_fusion
  465.3 4.4 collective-permute-start.3
  469.7 68.8 %collective-permute-done.3 = f32[3,1024,512]{2,1,0:T(8,128)S(1)} collective-permute-done((f32[3,1024,512]{2,1,0:T(8,128)}, f32[3,1024,512]{2,1,0:T(8,128)S(1)}, u32[]{:S(2)}, u32[]{:S(2)}) %collective-permute-start.3) | collective-permute-done | bytes 6291488 | tf_op jit(solution)/shard_map/ppermute | solution.py:15
  538.5 0.4 slice.47
  539.0 5.5 collective-permute-start.4
  544.5 46.0 %collective-permute-done.4 = f32[2,1024,512]{2,1,0:T(8,128)S(1)} collective-permute-done((f32[2,1024,512]{2,1,0:T(8,128)S(1)}, f32[2,1024,512]{2,1,0:T(8,128)S(1)}, u32[]{:S(2)}, u32[]{:S(2)}) %collective-permute-start.4) | collective-permute-done | bytes 4194336 | tf_op jit(solution)/shard_map/ppermute | solution.py:15
  590.5 1.5 slice.49
  592.0 0.0 copy-start.2
  592.0 5.7 collective-permute-start.5
  597.7 4.8 fusion.12
  602.5 0.0 copy-done.2
  602.5 0.0 copy-start.6
  602.5 0.0 copy-start.4
  602.5 3.4 fusion.14
  606.0 0.0 copy-done.6
  606.0 0.0 copy-start.8
  606.0 3.4 fusion.6
  609.4 0.0 copy-done.4
  609.4 3.4 fusion.10
  612.9 0.0 copy-done.8
  612.9 5.1 add_add_fusion
  618.0 3.5 collective-permute-done.5
  621.5 3.9 fusion.17
  (5 shorter events, 0.1 us)
Async XLA Ops:
  7.2 36.7 %copy-start = (bf16[1024,512]{1,0:T(8,128)(2,1)S(1)}, bf16[1024,512]{1,0:T(8,128)(2,1)}, u32[]{:S(2)}) copy-start(bf16[1024,512]{1,0:T(8,128)(2,1)} %param.6) | copy-start | bytes 3145732
  7.2 398.9 %all-reduce.3.cloned.1.call-start = ((), (), s32[]{:S(2)}) async-start(), calls=%async_computation | async-start | bytes 33554432 | tf_op jit(solution)/shard_map/psum | solution.py:42
  7.2 18.8 %collective-permute-start = (bf16[1024,512]{1,0:T(8,128)(2,1)}, bf16[1024,512]{1,0:T(8,128)(2,1)S(1)}, u32[]{:S(2)}, u32[]{:S(2)}) collective-permute-start(bf16[1024,512]{1,0:T(8,128)(2,1)} %param.7), channel_id=1, source_target_pairs={{120,0},{0,8},{8,16},{16,24},{24,32},{32,40},{40,48},{48,56},{56,6... | collective-permute-start | bytes 3145736 | tf_op jit(solution)/shard_map/ppermute | solution.py:15
  26.0 26.0 %copy-start.3 = (bf16[1024,512]{1,0:T(8,128)(2,1)}, bf16[1024,512]{1,0:T(8,128)(2,1)S(1)}, u32[]{:S(2)}) copy-start(bf16[1024,512]{1,0:T(8,128)(2,1)S(1)} %collective-permute-done) | copy-start | bytes 3145732
  26.0 17.8 %collective-permute-start.1 = (bf16[1024,512]{1,0:T(8,128)(2,1)S(1)}, bf16[1024,512]{1,0:T(8,128)(2,1)S(1)}, u32[]{:S(2)}, u32[]{:S(2)}) collective-permute-start(bf16[1024,512]{1,0:T(8,128)(2,1)S(1)} %collective-permute-done), channel_id=1, source_target_pairs={{120,0},{0,8},{8,16},{16,24},{24,32},{32,40},{40,48},{48,56},{56,6... | collective-permute-start | bytes 3145736 | tf_op jit(solution)/shard_map/ppermute | solution.py:15
  43.9 8.1 %copy-start.5 = (bf16[1024,512]{1,0:T(8,128)(2,1)}, bf16[1024,512]{1,0:T(8,128)(2,1)S(1)}, u32[]{:S(2)}) copy-start(bf16[1024,512]{1,0:T(8,128)(2,1)S(1)} %collective-permute-done.1) | copy-start | bytes 3145732
  43.9 17.8 %collective-permute-start.2 = (bf16[1024,512]{1,0:T(8,128)(2,1)S(1)}, bf16[1024,512]{1,0:T(8,128)(2,1)S(1)}, u32[]{:S(2)}, u32[]{:S(2)}) collective-permute-start(bf16[1024,512]{1,0:T(8,128)(2,1)S(1)} %collective-permute-done.1), channel_id=1, source_target_pairs={{120,0},{0,8},{8,16},{16,24},{24,32},{32,40},{40,48},{48,56},{56,6... | collective-permute-start | bytes 3145736 | tf_op jit(solution)/shard_map/ppermute | solution.py:15
  61.7 1.0 copy-start.7
  66.0 12.0 %copy-start.9 = (s32[1024]{0:T(1024)S(1)}, s32[1024]{0:T(1024)}, u32[]{:S(2)}) copy-start(s32[1024]{0:T(1024)} %param.9) | copy-start | bytes 12292
  430.9 9.7 %copy-start.1 = (f32[1024,1024]{1,0:T(8,128)S(1)}, f32[1024,1024]{1,0:T(8,128)}, u32[]{:S(2)}) copy-start(f32[1024,1024]{1,0:T(8,128)} %get-tuple-element.3) | copy-start | bytes 12582916
  465.3 73.2 %collective-permute-start.3 = (f32[3,1024,512]{2,1,0:T(8,128)}, f32[3,1024,512]{2,1,0:T(8,128)S(1)}, u32[]{:S(2)}, u32[]{:S(2)}) collective-permute-start(f32[3,1024,512]{2,1,0:T(8,128)} %pad_maximum_fusion), channel_id=1, source_target_pairs={{8,0},{16,8},{24,16},{32,24},{40,32},{48,40},{56,48},{64,56},{72,6... | collective-permute-start | bytes 18874376 | tf_op jit(solution)/shard_map/ppermute | solution.py:15
  539.0 51.5 %collective-permute-start.4 = (f32[2,1024,512]{2,1,0:T(8,128)S(1)}, f32[2,1024,512]{2,1,0:T(8,128)S(1)}, u32[]{:S(2)}, u32[]{:S(2)}) collective-permute-start(f32[2,1024,512]{2,1,0:T(8,128)S(1)} %slice.47), channel_id=1, source_target_pairs={{8,0},{16,8},{24,16},{32,24},{40,32},{48,40},{56,48},{64,56},{72,6... | collective-permute-start | bytes 12582920 | tf_op jit(solution)/shard_map/ppermute | solution.py:15
  592.0 10.5 %copy-start.2 = (bf16[1024,512]{1,0:T(8,128)(2,1)S(1)}, bf16[1024,512]{1,0:T(8,128)(2,1)}, u32[]{:S(2)}) copy-start(bf16[1024,512]{1,0:T(8,128)(2,1)} %param.7) | copy-start | bytes 3145732
  592.0 29.5 %collective-permute-start.5 = (f32[1,1024,512]{2,1,0:T(8,128)}, f32[1,1024,512]{2,1,0:T(8,128)S(1)}, u32[]{:S(2)}, u32[]{:S(2)}) collective-permute-start(f32[1,1024,512]{2,1,0:T(8,128)} %slice.49), channel_id=1, source_target_pairs={{8,0},{16,8},{24,16},{32,24},{40,32},{48,40},{56,48},{64,56},{72,6... | collective-permute-start | bytes 6291464 | tf_op jit(solution)/shard_map/ppermute | solution.py:15
  602.5 3.5 copy-start.6
  602.5 6.9 %copy-start.4 = (bf16[1024,512]{1,0:T(8,128)(2,1)S(1)}, bf16[1024,512]{1,0:T(8,128)(2,1)}, u32[]{:S(2)}) copy-start(bf16[1024,512]{1,0:T(8,128)(2,1)} %copy-done.3) | copy-start | bytes 3145732
  606.0 6.9 %copy-start.8 = (bf16[1024,512]{1,0:T(8,128)(2,1)S(1)}, bf16[1024,512]{1,0:T(8,128)(2,1)}, u32[]{:S(2)}) copy-start(bf16[1024,512]{1,0:T(8,128)(2,1)} %copy-done.7) | copy-start | bytes 3145732
Sparse Core Ops, SparseCore 0:
  66.1 339.9 all-reduce.2
where the time goes:
time: 641 us; the launch traced here: 633 us
  waiting for transfers between devices  476 us (74%)
  other arithmetic  51.3 us (8%)
  matrix products  45.7 us (7%)
  local copies, waits for them, and re-layouts  29.4 us (5%)
  starting transfers between devices  15.6 us (2%)
  between operations  14.5 us (2%)
    psum x1, waiting for transfers between devices, per_device(): tiles = [lax.psum(partial_value(block), 'width') for block in held]  315 us
    ppermute x6, waiting for transfers between devices, shifted(): return lax.ppermute(block, axis, route)  161 us
    ppermute x6, starting transfers between devices, shifted(): return lax.ppermute(block, axis, route)  15.6 us
    dot_general x4, matrix products, per_device(): jnp.dot(block_slopes.T, query_wide, precision=lax.Precision.HIGHEST, pref...  15.5 us
    dot_general x4, matrix products, per_device(): jnp.dot(block_slopes, held[step].astype(jnp.float32), precision=lax.Preci...  15.5 us
    dot_general x4, matrix products, partial_value(): jnp.einsum('qd,pd->qp', queries, block, preferred_element_type=jnp.float32)  14.7 us
    gather x1, local copies, waits for them, and re-layouts, slopes_of(): t_pos = jnp.take_along_axis(teach, index, 1)  13.2 us
    gather x1, local copies, waits for them, and re-layouts, slopes_of(): s_pos = jnp.take_along_axis(scores, index, 1)  13.2 us
  transfers between devices with their start and end apart: 7, of which 7 were waited for; matrix products, arithmetic and copies ran while one was open for 9% of the time, Pallas kernels for 0%

commit v1 on v0

v1 whole, which is shorter than its diff:
```python
import jax
import jax.numpy as jnp
from jax import lax
from jax.sharding import PartitionSpec as P

STEPS = 4


SCALE = 20.0


def shifted(block, axis, distance):
    devices = range(lax.axis_size(axis))
    route = [((i - distance) % len(devices), i) for i in devices]
    return lax.ppermute(block, axis, route)


def after(value, dep):
    return value + 0.0 * dep[:1, :1]


def per_device(queries, passages, teacher, positives):
    rows = queries.shape[0]
    window = STEPS * rows
    held = [passages]
    current = passages
    for step in range(1, STEPS):
        current = shifted(current, "loop", 1)
        held.append(current)

    index = positives[:, None]
    teach = teacher.astype(jnp.float32)
    column = lax.broadcasted_iota(jnp.int32, teach.shape, 1)
    t_pos = jnp.sum(jnp.where(column == index, teach, 0.0), 1, keepdims=True)
    t_sum = jnp.sum(teach, 1, keepdims=True)

    partials = [
        jnp.einsum("qd,pd->qp", queries, block, preferred_element_type=jnp.float32)
        for block in held
    ]
    block_col = lax.broadcasted_iota(jnp.int32, (rows, rows), 1)
    pos_part = sum(
        jnp.sum(jnp.where(block_col + k * rows == index, partials[k], 0.0), 1)
        for k in range(STEPS)
    )
    row_part = sum(jnp.sum(partials[k], 1) for k in range(STEPS))
    stats_part = jnp.stack([pos_part, row_part], 0)

    order = [0] + list(range(STEPS - 1, 0, -1))
    coef = SCALE * 2.0 / (window - 1)
    query_wide = queries.astype(jnp.float32)
    full = {}
    terms = {}
    grad_q = None
    grad_p = None

    def reduce_block(j):
        k = order[j]
        if j == 0:
            pad = jnp.zeros((8 - stats_part.shape[0], rows), jnp.float32)
            part = jnp.concatenate([partials[k], stats_part, pad], 0)
            carried = lax.psum(part, "width")
            full[k] = carried[:rows]
            return carried[rows : rows + stats_part.shape[0]]
        part = after(partials[k], full[order[j - 1]])
        if j >= 2:
            part = after(part, terms[order[j - 2]])
        full[k] = lax.psum(part, "width")
        return None

    stats = reduce_block(0)
    s_pos = SCALE * stats[0][:, None]
    s_sum = SCALE * stats[1][:, None]
    total = window * (s_pos - t_pos) - s_sum + t_sum

    for j, k in enumerate(order):
        if j + 1 < len(order):
            reduce_block(j + 1)
        scores = SCALE * full[k]
        teach_k = teach[:, k * rows : (k + 1) * rows]
        errors = (s_pos - scores) - (t_pos - teach_k)
        hit = (block_col + k * rows == index).astype(jnp.float32)
        slopes = coef * (hit * total - errors)
        gq = jnp.dot(
            slopes,
            held[k].astype(jnp.float32),
            precision=lax.Precision.HIGHEST,
            preferred_element_type=jnp.float32,
        )
        grad_q = gq if grad_q is None else grad_q + gq
        term = jnp.dot(
            slopes.T,
            query_wide,
            precision=lax.Precision.HIGHEST,
            preferred_element_type=jnp.float32,
        )
        terms[k] = term
        if k:
            term = shifted(term, "loop", -k)
        grad_p = term if grad_p is None else grad_p + term
    return (grad_q, grad_p)


def solution(mesh):
    in_specs = (P("loop", "width"), P("loop", "width"), P("loop", None), P("loop"))
    out_specs = (P("loop", "width"), P("loop", "width"))
    return jax.shard_map(
        per_device, mesh=mesh, in_specs=in_specs, out_specs=out_specs, check_vma=False
    )
```

time: 641 us -> 667 us (1.041)
  waiting for transfers between devices: 476 us -> 493 us
  starting transfers between devices: 15.6 us -> 6.65 us
  matrix products: 45.7 us -> 53.8 us
    psum x1 -> x4, waiting for transfers between devices: 315 us -> 449 us  [the longest x3 342 us: reduce_block(): full[k] = lax.psum(part, 'width')]
    ppermute x6, waiting for transfers between devices: 161 us -> 43.9 us  [shifted(): return lax.ppermute(block, axis, route)]
    gather x2 -> x0, local copies, waits for them, and re-layouts: 26.4 us -> none  [the longest x1 13.2 us: slopes_of(): t_pos = jnp.take_along_axis(teach, index, 1)]
    dot_general x0 -> x3, local copies, waits for them, and re-layouts: none -> 16 us  [per_device(): jnp.einsum('qd,pd->qp', queries, block, preferred_element_type=jnp.float32)]
    add x1 -> x9, other arithmetic: 3.94 us -> 17.3 us  [the longest x3 12.7 us: after(): return value + 0.0 * dep[:1, :1]]
    concatenate x0 -> x1, local copies, waits for them, and re-layouts: none -> 10.7 us  [reduce_block(): part = jnp.concatenate([partials[k], stats_part, pad], 0)]
    ppermute x6, starting transfers between devices: 15.6 us -> 6.1 us  [shifted(): return lax.ppermute(block, axis, route)]
    dot_general x12, matrix products: 45.7 us -> 53.8 us  [the longest x4 19.6 us: per_device(): jnp.einsum('qd,pd->qp', queries, block, preferred_element_type=jnp.float32)]
  transfers between devices with their start and end apart: 7 -> 10, of which waited for: 7 -> 8; matrix products, arithmetic and copies ran while one was open for 9% -> 12% of each run, Pallas kernels for 0% -> 0%
where the time goes in v1:
time: 667 us; the launch traced here: 658 us
  waiting for transfers between devices  493 us (74%)
  other arithmetic  53.8 us (8%)
  matrix products  53.8 us (8%)
  local copies, waits for them, and re-layouts  33.1 us (5%)
  between operations  17.7 us (3%)
    psum x3, waiting for transfers between devices, reduce_block(): full[k] = lax.psum(part, 'width')  342 us
    psum x1, waiting for transfers between devices, reduce_block(): carried = lax.psum(part, 'width')  107 us
    ppermute x6, waiting for transfers between devices, shifted(): return lax.ppermute(block, axis, route)  43.9 us
    dot_general x4, matrix products, per_device(): jnp.einsum('qd,pd->qp', queries, block, preferred_element_type=jnp.float32)  19.6 us
    dot_general x4, matrix products, per_device(): jnp.dot(slopes.T, query_wide, precision=lax.Precision.HIGHEST, preferred_...  17.4 us
    mul x3, other arithmetic, per_device(): slopes = coef * (hit * total - errors)  17.2 us
    dot_general x4, matrix products, per_device(): jnp.dot(slopes, held[k].astype(jnp.float32), precision=lax.Precision.HIGH...  16.7 us
    dot_general x3, local copies, waits for them, and re-layouts, per_device(): jnp.einsum('qd,pd->qp', queries, block, preferred_element_type=jnp.float32)  16 us
  transfers between devices with their start and end apart: 10, of which 8 were waited for; matrix products, arithmetic and copies ran while one was open for 12% of the time, Pallas kernels for 0%

profile of v1, /device:TPU:0, one launch (start us, length us, event | category | flops | bytes accessed | tf_op | source)
XLA Modules:
  0.0 658.2 jit_solution(7109032627486275314)
XLA Ops:
  7.2 0.0 copy-start
  7.2 0.0 all-reduce.5.cloned.1.call-start
  7.2 0.1 collective-permute-start
  7.3 18.7 %collective-permute-done = bf16[1024,512]{1,0:T(8,128)(2,1)S(1)} collective-permute-done((bf16[1024,512]{1,0:T(8,128)(2,1)}, bf16[1024,512]{1,0:T(8,128)(2,1)S(1)}, u32[]{:S(2)}, u32[]{:S(2)}) %collective-permute-start) | collective-permute-done | bytes 1048608 | tf_op jit(solution)/shard_map/ppermute | solution.py:15
  26.0 0.0 collective-permute-start.1
  26.0 17.8 %collective-permute-done.1 = bf16[1024,512]{1,0:T(8,128)(2,1)S(1)} collective-permute-done((bf16[1024,512]{1,0:T(8,128)(2,1)S(1)}, bf16[1024,512]{1,0:T(8,128)(2,1)S(1)}, u32[]{:S(2)}, u32[]{:S(2)}) %collective-permute-start.1) | collective-permute-done | bytes 1048608 | tf_op jit(solution)/shard_map/ppermute | solution.py:15
  43.9 0.0 collective-permute-start.2
  43.9 0.0 copy-done
  43.9 3.3 fusion.19
  47.2 5.3 copy.6
  52.5 3.3 fusion.18
  55.9 5.3 copy.7
  61.2 0.6 collective-permute-done.2
  61.8 4.5 fusion.17
  66.4 5.4 copy.8
  71.7 0.0 copy-done.10
  71.7 8.4 %fusion.16 = (f32[1024]{0:T(1024)S(1)}, f32[1024]{0:T(1024)S(1)}, f32[1024]{0:T(1024)S(1)}, f32[1024]{0:T(1024)S(1)}, f32[1024]{0:T(1024)S(1)}, /*index=5*/f32[1024,1024]{1,0:T(8,128)}) fusion(s32[1024]{0:T(1024)S(1)} %copy-done.10, f32[1024,1024]{1,0:T(8,128)} %copy.6, s32[1024]{0:T(1024)S(1)} %iota_add_fusion.2, f32[1024,1024]{1,0:T(8,128)} %copy.7, ...), kind=kOutput, calls=%fused_computation.45 | convolution fusion | flops 1087368192 | bytes 18911232 | tf_op jit(solution)/shard_map/qd,pd->qp/dot_general | solution.py:38
  80.2 10.7 %concatenate.3 = f32[1032,1024]{1,0:T(8,128)} concatenate(f32[1024,1024]{1,0:T(8,128)} %get-tuple-element.13, f32[1,1024]{1,0:T(1,128)S(1)} %bitcast.38, f32[1,1024]{1,0:T(1,128)S(1)} %bitcast.37, f32[6,1024]{1,0:T(8,128)S(1)} %broadcast_in_dim.18), dimensions={0} | concatenate | bytes 8454144 | tf_op jit(solution)/shard_map/concatenate | solution.py:61
  90.9 0.0 all-reduce.5.cloned.1.call-update
  90.9 0.0 all-reduce.7.cloned.1.call-start
  91.0 107.0 %all-reduce.5.cloned.1.call-done = f32[1032,1024]{1,0:T(8,128)} async-done(((f32[1032,1024]{1,0:T(8,128)}), f32[1032,1024]{1,0:T(8,128)}) %all-reduce.5.cloned.1.call-update) | async-done | bytes 4227088 | tf_op jit(solution)/shard_map/psum | solution.py:62
  198.0 1.2 slice.56
  199.8 5.0 broadcast_add_fusion
  204.8 0.0 all-reduce.7.cloned.1.call-update
  204.8 0.2 all-reduce.9.cloned.1.call-start
  205.0 11.6 %convert_element_type.2 = f32[1024,4096]{1,0:T(8,128)} convert(bf16[1024,4096]{1,0:T(8,128)(2,1)} %param.6) | non-fusion elementwise | flops 4194304 | bytes 25165824 | tf_op jit(solution)/shard_map/convert_element_type | solution.py:32
  216.6 6.9 %convert_reduce_fusion = (f32[1024]{0:T(1024)S(1)}, f32[1024]{0:T(1024)S(1)}) fusion(bf16[1024,4096]{1,0:T(8,128)(2,1)} %param.6, s32[1024]{0:T(1024)S(1)} %copy-done.10), kind=kLoop, calls=%fused_computation.2 | loop fusion | flops 20969472 | bytes 8400896 | tf_op jit(solution)/shard_map/reduce_sum | solution.py:35
  223.5 0.8 slice_multiply_fusion.1
  224.3 4.3 fusion.14
  228.7 3.5 fusion.21
  232.2 0.6 slice.59
  232.8 0.8 copy-done.7
  234.2 75.0 %all-reduce.7.cloned.1.call-done = f32[1024,1024]{1,0:T(8,128)} async-done(((f32[1024,1024]{1,0:T(8,128)}), f32[1024,1024]{1,0:T(8,128)}) %all-reduce.7.cloned.1.call-update) | async-done | bytes 4194320 | tf_op jit(solution)/shard_map/psum | solution.py:68
  309.2 1.2 slice.58
  311.1 5.2 add_add_fusion.1
  316.3 0.0 all-reduce.9.cloned.1.call-update
  316.3 0.3 all-reduce.11.cloned.1.call-start
  316.5 104.0 %all-reduce.9.cloned.1.call-done = f32[1024,1024]{1,0:T(8,128)} async-done(((f32[1024,1024]{1,0:T(8,128)}), f32[1024,1024]{1,0:T(8,128)}) %all-reduce.9.cloned.1.call-update) | async-done | bytes 4194320 | tf_op jit(solution)/shard_map/psum | solution.py:68
  420.6 1.2 slice.61
  422.4 8.8 %fusion.5 = (f32[1024,1024]{1,0:T(8,128)}, f32[1024,1024]{1,0:T(8,128)S(1)}) fusion(f32[1024,4096]{1,0:T(8,128)} %convert_element_type.2, f32[1024,1024]{1,0:T(8,128)} %all-reduce.9.cloned.1.call-done, f32[1024]{0:T(1024)S(1)} %get-tuple-element.3, f32[1024]{0:T(1024)S(1)} %bitcast.35, f32[1024]{0:T(1024)S(1)} %subtract_add_fusion, ...), kind=kLoop, calls=%fused_computation.14 | loop fusion | flops 16777216 | bytes 25190400 | tf_op jit(solution)/shard_map/mul | solution.py:83
  431.2 3.5 fusion.23
  434.7 0.0 copy-done.2
  434.7 0.0 copy-start.11
  434.7 0.6 slice.62
  435.3 0.7 copy-done.11
  436.7 2.6 add_add_fusion
  439.2 0.0 all-reduce.11.cloned.1.call-update
  439.3 4.6 collective-permute-start.3
  443.9 7.0 %fusion.25 = f32[1024,512]{1,0:T(8,128)} fusion(f32[1024,1024]{1,0:T(8,128)} %get-tuple-element.9, bf16[1024,512]{1,0:T(8,128)(2,1)S(1)} %copy-done), kind=kOutput, calls=%fused_computation.54 | convolution fusion | flops 6442450944 | bytes 7340032 | tf_op jit(solution)/shard_map/dot_general | solution.py:91
  450.9 1.1 collective-permute-start.4
  451.9 163.2 %all-reduce.11.cloned.1.call-done = f32[1024,1024]{1,0:T(8,128)} async-done(((f32[1024,1024]{1,0:T(8,128)}), f32[1024,1024]{1,0:T(8,128)}) %all-reduce.11.cloned.1.call-update) | async-done | bytes 4194320 | tf_op jit(solution)/shard_map/psum | solution.py:68
  615.1 4.1 fusion.2
  619.3 0.0 copy-start.9
  619.3 3.5 fusion.26
  622.8 0.3 collective-permute-start.5
  623.1 3.4 fusion.20
  626.6 3.4 fusion.22
  630.0 3.4 fusion.24
  633.5 6.4 add_add_fusion.3
  639.9 0.0 collective-permute-done.3
  639.9 0.0 collective-permute-done.4
  639.9 6.7 %collective-permute-done.5 = f32[1024,512]{1,0:T(8,128)S(1)} collective-permute-done((f32[1024,512]{1,0:T(8,128)S(1)}, f32[1024,512]{1,0:T(8,128)S(1)}, u32[]{:S(2)}, u32[]{:S(2)}) %collective-permute-start.5) | collective-permute-done | bytes 2097184 | tf_op jit(solution)/shard_map/ppermute | solution.py:15
  646.6 0.0 copy-done.8
  646.6 4.6 add_add_fusion.2
  (21 shorter events, 0.1 us)
Async XLA Ops:
  7.2 36.7 %copy-start = (bf16[1024,512]{1,0:T(8,128)(2,1)S(1)}, bf16[1024,512]{1,0:T(8,128)(2,1)}, u32[]{:S(2)}) copy-start(bf16[1024,512]{1,0:T(8,128)(2,1)} %param.4) | copy-start | bytes 3145732
  7.2 190.8 %all-reduce.5.cloned.1.call-start = ((), (), s32[]{:S(2)}) async-start(), calls=%async_computation | async-start | bytes 8454144 | tf_op jit(solution)/shard_map/psum | solution.py:62
  7.2 18.8 %collective-permute-start = (bf16[1024,512]{1,0:T(8,128)(2,1)}, bf16[1024,512]{1,0:T(8,128)(2,1)S(1)}, u32[]{:S(2)}, u32[]{:S(2)}) collective-permute-start(bf16[1024,512]{1,0:T(8,128)(2,1)} %param.5), channel_id=1, source_target_pairs={{120,0},{0,8},{8,16},{16,24},{24,32},{32,40},{40,48},{48,56},{56,6... | collective-permute-start | bytes 3145736 | tf_op jit(solution)/shard_map/ppermute | solution.py:15
  26.0 17.8 %collective-permute-start.1 = (bf16[1024,512]{1,0:T(8,128)(2,1)S(1)}, bf16[1024,512]{1,0:T(8,128)(2,1)S(1)}, u32[]{:S(2)}, u32[]{:S(2)}) collective-permute-start(bf16[1024,512]{1,0:T(8,128)(2,1)S(1)} %collective-permute-done), channel_id=1, source_target_pairs={{120,0},{0,8},{8,16},{16,24},{24,32},{32,40},{40,48},{48,56},{56,6... | collective-permute-start | bytes 3145736 | tf_op jit(solution)/shard_map/ppermute | solution.py:15
  43.9 17.9 %collective-permute-start.2 = (bf16[1024,512]{1,0:T(8,128)(2,1)S(1)}, bf16[1024,512]{1,0:T(8,128)(2,1)}, u32[]{:S(2)}, u32[]{:S(2)}) collective-permute-start(bf16[1024,512]{1,0:T(8,128)(2,1)S(1)} %collective-permute-done.1), channel_id=1, source_target_pairs={{120,0},{0,8},{8,16},{16,24},{24,32},{32,40},{40,48},{48,56},{56,6... | collective-permute-start | bytes 3145736 | tf_op jit(solution)/shard_map/ppermute | solution.py:15
  66.4 5.4 copy-start.10
  90.9 218.3 %all-reduce.7.cloned.1.call-start = ((), (), s32[]{:S(2)}) async-start(), calls=%async_computation.1 | async-start | bytes 8388608 | tf_op jit(solution)/shard_map/psum | solution.py:68
  204.8 215.8 %all-reduce.9.cloned.1.call-start = ((), (), s32[]{:S(2)}) async-start(), calls=%async_computation.2 | async-start | bytes 8388608 | tf_op jit(solution)/shard_map/psum | solution.py:68
  228.6 3.5 copy-start.4
  232.2 1.4 copy-start.7
  316.3 298.8 %all-reduce.11.cloned.1.call-start = ((), (), s32[]{:S(2)}) async-start(), calls=%async_computation.3 | async-start | bytes 8388608 | tf_op jit(solution)/shard_map/psum | solution.py:68
  431.2 3.5 copy-start.2
  431.2 5.5 copy-start.6
  434.7 1.3 copy-start.11
  439.3 200.6 %collective-permute-start.3 = (f32[1024,512]{1,0:T(8,128)}, f32[1024,512]{1,0:T(8,128)}, u32[]{:S(2)}, u32[]{:S(2)}) collective-permute-start(f32[1024,512]{1,0:T(8,128)} %copy-done.11), channel_id=1, source_target_pairs={{24,0},{32,8},{40,16},{48,24},{56,32},{64,40},{72,48},{80,56},{88,... | collective-permute-start | bytes 6291464 | tf_op jit(solution)/shard_map/ppermute | solution.py:15
  450.9 189.0 %collective-permute-start.4 = (f32[1024,512]{1,0:T(8,128)}, f32[1024,512]{1,0:T(8,128)}, u32[]{:S(2)}, u32[]{:S(2)}) collective-permute-start(f32[1024,512]{1,0:T(8,128)} %fusion.25), channel_id=1, source_target_pairs={{16,0},{24,8},{32,16},{40,24},{48,32},{56,40},{64,48},{72,56},{80,... | collective-permute-start | bytes 6291464 | tf_op jit(solution)/shard_map/ppermute | solution.py:15
  619.3 3.8 copy-start.5
  619.3 3.8 copy-start.9
  622.7 3.8 copy-start.1
  622.8 23.9 %collective-permute-start.5 = (f32[1024,512]{1,0:T(8,128)S(1)}, f32[1024,512]{1,0:T(8,128)S(1)}, u32[]{:S(2)}, u32[]{:S(2)}) collective-permute-start(f32[1024,512]{1,0:T(8,128)S(1)} %fusion.26), channel_id=1, source_target_pairs={{8,0},{16,8},{24,16},{32,24},{40,32},{48,40},{56,48},{64,56},{72,6... | collective-permute-start | bytes 6291464 | tf_op jit(solution)/shard_map/ppermute | solution.py:15
  630.0 3.5 copy-start.3
  633.5 13.2 %copy-start.8 = (f32[1024,512]{1,0:T(8,128)S(1)}, f32[1024,512]{1,0:T(8,128)}, u32[]{:S(2)}) copy-start(f32[1024,512]{1,0:T(8,128)} %copy-done.7) | copy-start | bytes 6291460
Sparse Core Ops, SparseCore 0:
  91.1 106.8 all-reduce.4
  204.9 104.2 all-reduce.6
  316.4 104.1 all-reduce.8
  439.4 175.6 all-reduce.10

commit v2 on v0

v2 whole, which is shorter than its diff:
```python
import jax
import jax.numpy as jnp
from jax import lax
from jax.sharding import PartitionSpec as P

STEPS = 4


SCALE = 20.0


def shifted(block, axis, distance):
    devices = range(lax.axis_size(axis))
    route = [((i - distance) % len(devices), i) for i in devices]
    return lax.ppermute(block, axis, route)


def wide_dot(a, b):
    return jnp.dot(a, b, precision=lax.Precision.HIGHEST, preferred_element_type=jnp.float32)


def per_device(queries, passages, teacher, positives):
    rows = queries.shape[0]
    width = lax.axis_size("width")
    me = lax.axis_index("width")
    sub = rows // width
    window = STEPS * rows

    q_full = lax.all_gather(queries, "width", axis=1, tiled=True)
    p_cols = lax.all_to_all(passages, "width", 0, 1, tiled=True)
    held_cols = [p_cols]
    held = [passages]
    for step in range(1, STEPS):
        held_cols.append(shifted(held_cols[-1], "loop", 1))
        held.append(shifted(held[-1], "loop", 1))

    cols = jnp.concatenate(held_cols, 0)
    scores = SCALE * jnp.einsum("qd,cd->qc", q_full, cols, preferred_element_type=jnp.float32)

    index = positives[:, None]
    teach = teacher.astype(jnp.float32)
    column = lax.broadcasted_iota(jnp.int32, teach.shape, 1)
    t_pos = jnp.sum(jnp.where(column == index, teach, 0.0), 1, keepdims=True)
    t_sum = jnp.sum(teach, 1, keepdims=True)

    local = lax.broadcasted_iota(jnp.int32, (1, STEPS * sub), 1)
    wcol = (local // sub) * rows + me * sub + local % sub
    hit = wcol == index
    teach_cols = lax.dynamic_slice_in_dim(
        teach.reshape(rows, STEPS, width, sub), me, 1, 2
    ).reshape(rows, STEPS * sub)

    pos_part = jnp.sum(jnp.where(hit, scores, 0.0), 1)
    row_part = jnp.sum(scores, 1)
    stats = lax.psum(jnp.stack([pos_part, row_part], 0), "width")
    s_pos = stats[0][:, None]
    s_sum = stats[1][:, None]
    total = window * (s_pos - t_pos) - s_sum + t_sum
    coef = SCALE * 2.0 / (window - 1)
    errors = (s_pos - scores) - (t_pos - teach_cols)
    slopes_cols = coef * (hit.astype(jnp.float32) * total - errors)

    slopes = lax.all_gather(slopes_cols, "width", axis=1, tiled=True)
    slopes = slopes.reshape(rows, width, STEPS, sub)

    query_wide = queries.astype(jnp.float32)
    grad_q = None
    terms = []
    for k in range(STEPS):
        block_slopes = slopes[:, :, k, :].reshape(rows, rows)
        gq = wide_dot(block_slopes, held[k].astype(jnp.float32))
        grad_q = gq if grad_q is None else grad_q + gq
        terms.append(wide_dot(block_slopes.T, query_wide))
    grad_p = terms[STEPS - 1]
    for k in range(STEPS - 2, -1, -1):
        grad_p = shifted(grad_p, "loop", -1) + terms[k]
    return (grad_q, grad_p)


def solution(mesh):
    in_specs = (P("loop", "width"), P("loop", "width"), P("loop", None), P("loop"))
    out_specs = (P("loop", "width"), P("loop", "width"))
    return jax.shard_map(
        per_device, mesh=mesh, in_specs=in_specs, out_specs=out_specs, check_vma=False
    )
```

time: 641 us -> 458 us (0.71)
  waiting for transfers between devices: 476 us -> 277 us
  blocking collectives: 0 us -> 46.2 us
  other arithmetic: 51.3 us -> 25 us
  local copies, waits for them, and re-layouts: 29.4 us -> 36.7 us
  matrix products: 45.7 us -> 38.5 us
    psum x1 -> x0, waiting for transfers between devices: 315 us -> none  [per_device(): tiles = [lax.psum(partial_value(block), 'width') for block in held]]
    all_gather x0 -> x2, waiting for transfers between devices: none -> 166 us  [the longest x1 166 us: per_device(): slopes = lax.all_gather(slopes_cols, 'width', axis=1, tiled=True)]
    ppermute x6 -> x9, waiting for transfers between devices: 161 us -> 110 us  [shifted(): return lax.ppermute(block, axis, route)]
    gather x2 -> x0, local copies, waits for them, and re-layouts: 26.4 us -> none  [the longest x1 13.2 us: slopes_of(): t_pos = jnp.take_along_axis(teach, index, 1)]
    all_to_all x0 -> x1, blocking collectives: none -> 26.1 us  [per_device(): p_cols = lax.all_to_all(passages, 'width', 0, 1, tiled=True)]
    psum x0 -> x1, blocking collectives: none -> 20.1 us  [per_device(): stats = lax.psum(jnp.stack([pos_part, row_part], 0), 'width')]
    unnamed x20 -> x12, local copies, waits for them, and re-layouts: 1.03 us -> 20 us
    mul x2 -> x1, other arithmetic: 22.3 us -> 3.73 us  [per_device(): slopes_cols = coef * (hit.astype(jnp.float32) * total - errors)]
  transfers between devices with their start and end apart: 7 -> 11, of which waited for: 7 -> 8; matrix products, arithmetic and copies ran while one was open for 9% -> 16% of each run, Pallas kernels for 0% -> 0%
where the time goes in v2:
time: 458 us; the launch traced here: 454 us
  waiting for transfers between devices  277 us (60%)
  blocking collectives  46.2 us (10%)
  matrix products  38.5 us (8%)
  local copies, waits for them, and re-layouts  36.7 us (8%)
  other arithmetic  25 us (5%)
  starting transfers between devices  16.3 us (4%)
  between operations  14.4 us (3%)
    all_gather x1, waiting for transfers between devices, per_device(): slopes = lax.all_gather(slopes_cols, 'width', axis=1, tiled=True)  166 us
    ppermute x9, waiting for transfers between devices, shifted(): return lax.ppermute(block, axis, route)  110 us
    dot_general x8, matrix products, wide_dot(): jnp.dot(a, b, precision=lax.Precision.HIGHEST, preferred_element_type=jnp...  29.6 us
    all_to_all x1, blocking collectives, per_device(): p_cols = lax.all_to_all(passages, 'width', 0, 1, tiled=True)  26.1 us
    psum x1, blocking collectives, per_device(): stats = lax.psum(jnp.stack([pos_part, row_part], 0), 'width')  20.1 us
    unnamed x12, local copies, waits for them, and re-layouts  20 us
    ppermute x9, starting transfers between devices, shifted(): return lax.ppermute(block, axis, route)  16.2 us
    unnamed x1, other arithmetic  11.8 us
  transfers between devices with their start and end apart: 11, of which 8 were waited for; matrix products, arithmetic and copies ran while one was open for 16% of the time, Pallas kernels for 0%

profile of v2, /device:TPU:0, one launch (start us, length us, event | category | flops | bytes accessed | tf_op | source)
XLA Modules:
  0.0 454.1 jit_solution(8620175439854441201)
XLA Ops:
  7.2 0.0 all-gather.3.cloned.1.call-start
  7.2 0.7 all-gather.3.cloned.1.call-update
  7.9 0.0 all-gather.5.cloned.1.call-start
  7.9 26.1 %all_to_all.19 = bf16[8,128,512]{2,1,0:T(8,128)(2,1)S(1)} all-to-all(bf16[8,128,512]{2,1,0:T(8,128)(2,1)} %bitcast.55), channel_id=1, replica_groups=mesh['loop'=16,'width'=8] {'width'}, dimensions={0} | all-to-all | bytes 2097152 | tf_op jit(solution)/shard_map/all_to_all | solution.py:30
  34.1 0.7 copy.8
  34.7 0.1 collective-permute-start
  34.8 40.4 %collective-permute-done = bf16[128,4096]{0,1:T(8,128)(2,1)S(1)} collective-permute-done((bf16[128,4096]{0,1:T(8,128)(2,1)S(1)}, bf16[128,4096]{0,1:T(8,128)(2,1)S(1)}, u32[]{:S(2)}, u32[]{:S(2)}) %collective-permute-start) | collective-permute-done | bytes 1048608 | tf_op jit(solution)/shard_map/ppermute | solution.py:15
  75.2 0.0 copy-start.4
  75.2 0.0 collective-permute-start.1
  75.2 11.8 %convert_bitcast_fusion = f32[128,8,32,128]{3,1,2,0:T(8,128)} fusion(bf16[1024,4096]{1,0:T(8,128)(2,1)} %param.6), kind=kLoop, calls=%fused_computation | loop fusion | flops 4194304 | bytes 25165824
  87.1 0.0 copy-done.4
  87.1 14.1 %copy.11 = f32[128,8,32,128]{3,2,1,0:T(8,128)} copy(f32[128,8,32,128]{3,1,2,0:T(8,128)} %convert_bitcast_fusion) | data formatting | bytes 33554432
  101.2 14.6 %collective-permute-done.1 = bf16[128,4096]{0,1:T(8,128)(2,1)} collective-permute-done((bf16[128,4096]{0,1:T(8,128)(2,1)S(1)}, bf16[128,4096]{0,1:T(8,128)(2,1)}, u32[]{:S(2)}, u32[]{:S(2)}) %collective-permute-start.1) | collective-permute-done | bytes 1048608 | tf_op jit(solution)/shard_map/ppermute | solution.py:15
  115.8 0.2 collective-permute-start.2
  115.9 0.0 copy-start.3
  115.9 9.2 %constant_dynamic-slice_fusion = f32[1024,4,1,128]{3,2,1,0:T(1,128)} fusion(f32[1024,4,8,128]{3,2,1,0:T(8,128)} %bitcast.46, s32[]{:T(128)S(6)} %select_n.37), kind=kLoop, calls=%fused_computation.40 | loop fusion | bytes 4194308 | tf_op jit(solution)/shard_map/dynamic_slice | solution.py:49
  125.2 4.6 %copy.10 = f32[1024,4,1,128]{0,3,1,2:T(8,128)S(1)} copy(f32[1024,4,1,128]{3,2,1,0:T(1,128)} %constant_dynamic-slice_fusion) | data formatting | bytes 4194304
  129.7 0.0 copy-done.3
  129.8 6.8 %convert_reduce_fusion = (f32[1024]{0:T(1024)S(1)}, f32[1024]{0:T(1024)S(1)}) fusion(bf16[1024,4096]{1,0:T(8,128)(2,1)} %param.6, s32[1024]{0:T(1024)S(1)} %copy-done.3), kind=kLoop, calls=%fused_computation.1 | loop fusion | flops 20969472 | bytes 8400896 | tf_op jit(solution)/shard_map/reduce_sum | solution.py:44
  136.6 7.4 %collective-permute-done.2 = bf16[128,4096]{0,1:T(8,128)(2,1)} collective-permute-done((bf16[128,4096]{0,1:T(8,128)(2,1)}, bf16[128,4096]{0,1:T(8,128)(2,1)}, u32[]{:S(2)}, u32[]{:S(2)}) %collective-permute-start.2) | collective-permute-done | bytes 1048608 | tf_op jit(solution)/shard_map/ppermute | solution.py:15
  144.0 0.0 all-gather.3.cloned.1.call-done
  144.0 8.9 %multiply_reduce_fusion = (f32[1024]{0:T(1024)S(1)}, f32[512,1024]{1,0:T(8,128)S(1)}) fusion(bf16[1024,4096]{1,0:T(8,128)(2,1)} %all-gather.3.cloned.1.call-done, bf16[128,4096]{0,1:T(8,128)(2,1)} %collective-permute-done.2, bf16[128,4096]{0,1:T(8,128)(2,1)} %collective-permute-done.1, bf16[128,4096]{0,1:T(8,128)(2,1)} %copy-done.4, ...), kind=kOutput, calls=%fused_computation.22 | convolution fusion | flops 4312792064 | bytes 14684160 | tf_op jit(solution)/shard_map/qd,cd->qc/dot_general | solution.py:38
  152.9 0.0 copy-start.1
  152.9 1.3 copy-done.1
  154.2 0.3 fusion.9
  154.6 20.1 %psum.7 = f32[2,1024]{1,0:T(2,128)S(1)} all-reduce(f32[2,1024]{1,0:T(2,128)S(1)} %pad_maximum_fusion), channel_id=1, replica_groups=mesh['loop'=16,'width'=8] {'width'}, use_global_device_ids=true, to_apply=%region_2.3 | all-reduce | flops 2048 | bytes 16384 | tf_op jit(solution)/shard_map/psum | solution.py:55
  174.7 3.7 fusion.11
  178.5 0.0 all-gather.5.cloned.1.call-update
  178.5 165.8 %all-gather.5.cloned.1.call-done = f32[1024,4096]{0,1:T(8,128)} async-done(((f32[1024,512]{0,1:T(8,128)}), f32[1024,4096]{0,1:T(8,128)}) %all-gather.5.cloned.1.call-update) | async-done | bytes 16777232 | tf_op jit(solution)/shard_map/all_gather | solution.py:63
  344.3 0.0 copy-start
  344.3 6.8 %fusion.24 = (f32[1024,8,1,128]{0,3,2,1:T(8,128)S(1)}, f32[1024,8,1,128]{0,3,2,1:T(8,128)S(1)}, f32[1024,8,1,128]{0,3,2,1:T(8,128)S(1)}, f32[1024,8,1,128]{0,3,2,1:T(8,128)S(1)}) fusion(f32[1024,8,4,128]{0,3,2,1:T(8,128)} %bitcast.47), kind=kLoop, calls=%fused_computation.42 | loop fusion | bytes 33554432 | tf_op jit(solution)/shard_map/slice | solution.py:70
  351.2 0.0 copy-start.2
  351.2 0.0 copy-done
  351.2 3.5 fusion.29
  354.6 4.4 collective-permute-start.6
  359.1 0.0 copy-done.2
  359.1 0.0 collective-permute-start.3
  359.1 23.5 %collective-permute-done.6 = f32[1024,512]{1,0:T(8,128)S(1)} collective-permute-done((f32[1024,512]{1,0:T(8,128)S(1)}, f32[1024,512]{1,0:T(8,128)S(1)}, u32[]{:S(2)}, u32[]{:S(2)}) %collective-permute-start.6) | collective-permute-done | bytes 2097184 | tf_op jit(solution)/shard_map/ppermute | solution.py:15
  382.6 3.5 convolution_add_fusion
  386.1 5.6 %collective-permute-start.7 = (f32[1024,512]{1,0:T(8,128)S(1)}, f32[1024,512]{1,0:T(8,128)S(1)}, u32[]{:S(2)}, u32[]{:S(2)}) collective-permute-start(f32[1024,512]{1,0:T(8,128)S(1)} %convolution_add_fusion), channel_id=1, source_target_pairs={{8,0},{16,8},{24,16},{32,24},{40,32},{48,40},{56,48},{64,56},{72,6... | collective-permute-start | bytes 6291464 | tf_op jit(solution)/shard_map/ppermute | solution.py:15
  391.7 0.0 collective-permute-done.3
  391.7 0.0 collective-permute-start.4
  391.7 17.8 %collective-permute-done.4 = bf16[1024,512]{1,0:T(8,128)(2,1)S(1)} collective-permute-done((bf16[1024,512]{1,0:T(8,128)(2,1)S(1)}, bf16[1024,512]{1,0:T(8,128)(2,1)S(1)}, u32[]{:S(2)}, u32[]{:S(2)}) %collective-permute-start.4) | collective-permute-done | bytes 1048608 | tf_op jit(solution)/shard_map/ppermute | solution.py:15
  409.5 0.0 collective-permute-start.5
  409.5 3.5 fusion.30
  413.0 2.2 collective-permute-done.7
  415.2 0.5 add.77
  415.7 6.0 %collective-permute-start.8 = (f32[1024,512]{1,0:T(8,128)S(1)}, f32[1024,512]{1,0:T(8,128)S(1)}, u32[]{:S(2)}, u32[]{:S(2)}) collective-permute-start(f32[1024,512]{1,0:T(8,128)S(1)} %add.77), channel_id=1, source_target_pairs={{8,0},{16,8},{24,16},{32,24},{40,32},{48,40},{56,48},{64,56},{72,6... | collective-permute-start | bytes 6291464 | tf_op jit(solution)/shard_map/ppermute | solution.py:15
  421.7 3.5 fusion.26
  425.2 3.4 fusion.31
  428.7 3.5 fusion.28
  432.2 3.7 fusion.27
  435.9 0.0 collective-permute-done.5
  435.9 5.0 %add_add_fusion = f32[1024,512]{1,0:T(8,128)} fusion(f32[1024,512]{1,0:T(8,128)S(1)} %fusion.28, f32[1024,512]{1,0:T(8,128)S(1)} %fusion.26, f32[1024,512]{1,0:T(8,128)S(1)} %fusion.27, f32[1024,1024]{0,1:T(8,128)S(1)} %bitcast.45, bf16[1024,512]{1,0:T(8,128)(2,1)S(1)} %collective-permute-done.5), kind=kOutput, calls=%fused_computation.21 | convolution fusion | flops 6444023808 | bytes 13631488 | tf_op jit(solution)/shard_map/dot_general | solution.py:19
  440.9 4.3 collective-permute-done.8
  445.3 1.8 add.78
  (4 shorter events, 0.0 us)
Async XLA Ops:
  7.2 136.8 %all-gather.3.cloned.1.call-start = ((), (), s32[]{:S(2)}) async-start(), calls=%async_computation.1 | async-start | bytes 9437184 | tf_op jit(solution)/shard_map/all_gather | solution.py:29
  7.9 336.4 %all-gather.5.cloned.1.call-start = ((), (), s32[]{:S(2)}) async-start(), calls=%async_computation.2 | async-start | bytes 18874368 | tf_op jit(solution)/shard_map/all_gather | solution.py:63
  34.7 40.5 %collective-permute-start = (bf16[128,4096]{0,1:T(8,128)(2,1)S(1)}, bf16[128,4096]{0,1:T(8,128)(2,1)S(1)}, u32[]{:S(2)}, u32[]{:S(2)}) collective-permute-start(bf16[128,4096]{0,1:T(8,128)(2,1)S(1)} %bitcast.56), channel_id=1, source_target_pairs={{120,0},{0,8},{8,16},{16,24},{24,32},{32,40},{40,48},{48,56},{56,6... | collective-permute-start | bytes 3145736 | tf_op jit(solution)/shard_map/ppermute | solution.py:15
  75.2 11.8 %copy-start.4 = (bf16[128,4096]{0,1:T(8,128)(2,1)}, bf16[128,4096]{0,1:T(8,128)(2,1)S(1)}, u32[]{:S(2)}) copy-start(bf16[128,4096]{0,1:T(8,128)(2,1)S(1)} %collective-permute-done) | copy-start | bytes 3145732
  75.2 40.5 %collective-permute-start.1 = (bf16[128,4096]{0,1:T(8,128)(2,1)S(1)}, bf16[128,4096]{0,1:T(8,128)(2,1)}, u32[]{:S(2)}, u32[]{:S(2)}) collective-permute-start(bf16[128,4096]{0,1:T(8,128)(2,1)S(1)} %collective-permute-done), channel_id=1, source_target_pairs={{120,0},{0,8},{8,16},{16,24},{24,32},{32,40},{40,48},{48,56},{56,6... | collective-permute-start | bytes 3145736 | tf_op jit(solution)/shard_map/ppermute | solution.py:15
  115.8 28.2 %collective-permute-start.2 = (bf16[128,4096]{0,1:T(8,128)(2,1)}, bf16[128,4096]{0,1:T(8,128)(2,1)}, u32[]{:S(2)}, u32[]{:S(2)}) collective-permute-start(bf16[128,4096]{0,1:T(8,128)(2,1)} %collective-permute-done.1), channel_id=1, source_target_pairs={{120,0},{0,8},{8,16},{16,24},{24,32},{32,40},{40,48},{48,56},{56,6... | collective-permute-start | bytes 3145736 | tf_op jit(solution)/shard_map/ppermute | solution.py:15
  115.9 13.8 %copy-start.3 = (s32[1024]{0:T(1024)S(1)}, s32[1024]{0:T(1024)}, u32[]{:S(2)}) copy-start(s32[1024]{0:T(1024)} %param.7) | copy-start | bytes 12292
  152.9 1.3 copy-start.1
  344.3 6.8 %copy-start = (bf16[1024,512]{1,0:T(8,128)(2,1)S(1)}, bf16[1024,512]{1,0:T(8,128)(2,1)}, u32[]{:S(2)}) copy-start(bf16[1024,512]{1,0:T(8,128)(2,1)} %param.4) | copy-start | bytes 3145732
  351.2 7.9 %copy-start.2 = (bf16[1024,512]{1,0:T(8,128)(2,1)S(1)}, bf16[1024,512]{1,0:T(8,128)(2,1)}, u32[]{:S(2)}) copy-start(bf16[1024,512]{1,0:T(8,128)(2,1)} %param.5) | copy-start | bytes 3145732
  354.6 28.0 %collective-permute-start.6 = (f32[1024,512]{1,0:T(8,128)S(1)}, f32[1024,512]{1,0:T(8,128)S(1)}, u32[]{:S(2)}, u32[]{:S(2)}) collective-permute-start(f32[1024,512]{1,0:T(8,128)S(1)} %fusion.29), channel_id=1, source_target_pairs={{8,0},{16,8},{24,16},{32,24},{40,32},{48,40},{56,48},{64,56},{72,6... | collective-permute-start | bytes 6291464 | tf_op jit(solution)/shard_map/ppermute | solution.py:15
  359.1 32.6 %collective-permute-start.3 = (bf16[1024,512]{1,0:T(8,128)(2,1)S(1)}, bf16[1024,512]{1,0:T(8,128)(2,1)S(1)}, u32[]{:S(2)}, u32[]{:S(2)}) collective-permute-start(bf16[1024,512]{1,0:T(8,128)(2,1)S(1)} %copy-done.2), channel_id=1, source_target_pairs={{120,0},{0,8},{8,16},{16,24},{24,32},{32,40},{40,48},{48,56},{56,6... | collective-permute-start | bytes 3145736 | tf_op jit(solution)/shard_map/ppermute | solution.py:15
  386.1 29.1 %collective-permute-start.7 = (f32[1024,512]{1,0:T(8,128)S(1)}, f32[1024,512]{1,0:T(8,128)S(1)}, u32[]{:S(2)}, u32[]{:S(2)}) collective-permute-start(f32[1024,512]{1,0:T(8,128)S(1)} %convolution_add_fusion), channel_id=1, source_target_pairs={{8,0},{16,8},{24,16},{32,24},{40,32},{48,40},{56,48},{64,56},{72,6... | collective-permute-start | bytes 6291464 | tf_op jit(solution)/shard_map/ppermute | solution.py:15
  391.7 17.8 %collective-permute-start.4 = (bf16[1024,512]{1,0:T(8,128)(2,1)S(1)}, bf16[1024,512]{1,0:T(8,128)(2,1)S(1)}, u32[]{:S(2)}, u32[]{:S(2)}) collective-permute-start(bf16[1024,512]{1,0:T(8,128)(2,1)S(1)} %collective-permute-done.3), channel_id=1, source_target_pairs={{120,0},{0,8},{8,16},{16,24},{24,32},{32,40},{40,48},{48,56},{56,6... | collective-permute-start | bytes 3145736 | tf_op jit(solution)/shard_map/ppermute | solution.py:15
  409.5 26.4 %collective-permute-start.5 = (bf16[1024,512]{1,0:T(8,128)(2,1)S(1)}, bf16[1024,512]{1,0:T(8,128)(2,1)S(1)}, u32[]{:S(2)}, u32[]{:S(2)}) collective-permute-start(bf16[1024,512]{1,0:T(8,128)(2,1)S(1)} %collective-permute-done.4), channel_id=1, source_target_pairs={{120,0},{0,8},{8,16},{16,24},{24,32},{32,40},{40,48},{48,56},{56,6... | collective-permute-start | bytes 3145736 | tf_op jit(solution)/shard_map/ppermute | solution.py:15
  415.7 29.6 %collective-permute-start.8 = (f32[1024,512]{1,0:T(8,128)S(1)}, f32[1024,512]{1,0:T(8,128)S(1)}, u32[]{:S(2)}, u32[]{:S(2)}) collective-permute-start(f32[1024,512]{1,0:T(8,128)S(1)} %add.77), channel_id=1, source_target_pairs={{8,0},{16,8},{24,16},{32,24},{40,32},{48,40},{56,48},{64,56},{72,6... | collective-permute-start | bytes 6291464 | tf_op jit(solution)/shard_map/ppermute | solution.py:15
Sparse Core Ops, SparseCore 0:
  9.6 98.8 all-gather.2
  178.6 165.6 all-gather.4

commit v3 on v2

--- a/solution.py
+++ b/solution.py
@@ -15,6 +15,11 @@
     return lax.ppermute(block, axis, route)
 
 
+def after(value, dep):
+    zero = 0.0 * dep[:1, :1]
+    return value + zero.astype(value.dtype)
+
+
 def wide_dot(a, b):
     return jnp.dot(a, b, precision=lax.Precision.HIGHEST, preferred_element_type=jnp.float32)
 
@@ -29,10 +34,8 @@
     q_full = lax.all_gather(queries, "width", axis=1, tiled=True)
     p_cols = lax.all_to_all(passages, "width", 0, 1, tiled=True)
     held_cols = [p_cols]
-    held = [passages]
     for step in range(1, STEPS):
         held_cols.append(shifted(held_cols[-1], "loop", 1))
-        held.append(shifted(held[-1], "loop", 1))
 
     cols = jnp.concatenate(held_cols, 0)
     scores = SCALE * jnp.einsum("qd,cd->qc", q_full, cols, preferred_element_type=jnp.float32)
@@ -60,20 +63,26 @@
     errors = (s_pos - scores) - (t_pos - teach_cols)
     slopes_cols = coef * (hit.astype(jnp.float32) * total - errors)
 
-    slopes = lax.all_gather(slopes_cols, "width", axis=1, tiled=True)
-    slopes = slopes.reshape(rows, width, STEPS, sub)
+    held = [after(passages, stats)]
+    for step in range(1, STEPS):
+        held.append(shifted(held[-1], "loop", 1))
 
     query_wide = queries.astype(jnp.float32)
     grad_q = None
-    terms = []
-    for k in range(STEPS):
-        block_slopes = slopes[:, :, k, :].reshape(rows, rows)
+    grad_p = None
+    done = []
+    for j, k in enumerate(range(STEPS - 1, -1, -1)):
+        piece = slopes_cols[:, k * sub : (k + 1) * sub]
+        if j >= 1:
+            piece = after(piece, done[j - 1][0])
+        if j >= 2:
+            piece = after(after(piece, done[j - 2][1]), held[STEPS - 1])
+        block_slopes = lax.all_gather(piece, "width", axis=1, tiled=True)
         gq = wide_dot(block_slopes, held[k].astype(jnp.float32))
         grad_q = gq if grad_q is None else grad_q + gq
-        terms.append(wide_dot(block_slopes.T, query_wide))
-    grad_p = terms[STEPS - 1]
-    for k in range(STEPS - 2, -1, -1):
-        grad_p = shifted(grad_p, "loop", -1) + terms[k]
+        term = wide_dot(block_slopes.T, query_wide)
+        grad_p = term if grad_p is None else shifted(grad_p, "loop", -1) + term
+        done.append((block_slopes, grad_p))
     return (grad_q, grad_p)
 
 

time: 458 us -> 551 us (1.20)
  waiting for transfers between devices: 277 us -> 325 us
  blocking collectives: 46.2 us -> 65.9 us
  matrix products: 38.5 us -> 51.7 us
  local copies, waits for them, and re-layouts: 36.7 us -> 43.7 us
    ppermute x9, waiting for transfers between devices: 110 us -> 276 us  [shifted(): return lax.ppermute(block, axis, route)]
    all_gather x1 -> x4, waiting for transfers between devices: 166 us -> 47.9 us  [per_device(): block_slopes = lax.all_gather(piece, 'width', axis=1, tiled=True)]
    psum x1, blocking collectives: 20.1 us -> 39.8 us  [per_device(): stats = lax.psum(jnp.stack([pos_part, row_part], 0), 'width')]
    dot_general x8, matrix products: 29.6 us -> 43.1 us  [wide_dot(): jnp.dot(a, b, precision=lax.Precision.HIGHEST, preferred_element_type=jnp...]
    unnamed x12 -> x49, local copies, waits for them, and re-layouts: 20 us -> 27.2 us
  transfers between devices with their start and end apart: 11 -> 14, of which waited for: 8 -> 10; matrix products, arithmetic and copies ran while one was open for 16% -> 15% of each run, Pallas kernels for 0% -> 0%
where the time goes in v3:
time: 551 us; the launch traced here: 546 us
  waiting for transfers between devices  325 us (59%)
  blocking collectives  65.9 us (12%)
  matrix products  51.7 us (9%)
  local copies, waits for them, and re-layouts  43.7 us (8%)
  other arithmetic  28.4 us (5%)
  between operations  18.9 us (3%)
  starting transfers between devices  12.2 us (2%)
    ppermute x9, waiting for transfers between devices, shifted(): return lax.ppermute(block, axis, route)  276 us
    all_gather x4, waiting for transfers between devices, per_device(): block_slopes = lax.all_gather(piece, 'width', axis=1, tiled=True)  47.9 us
    dot_general x8, matrix products, wide_dot(): jnp.dot(a, b, precision=lax.Precision.HIGHEST, preferred_element_type=jnp...  43.1 us
    psum x1, blocking collectives, per_device(): stats = lax.psum(jnp.stack([pos_part, row_part], 0), 'width')  39.8 us
    unnamed x49, local copies, waits for them, and re-layouts  27.2 us
    all_to_all x1, blocking collectives, per_device(): p_cols = lax.all_to_all(passages, 'width', 0, 1, tiled=True)  26.1 us
    ppermute x9, starting transfers between devices, shifted(): return lax.ppermute(block, axis, route)  12 us
    unnamed x1, other arithmetic  11.8 us
  transfers between devices with their start and end apart: 14, of which 10 were waited for; matrix products, arithmetic and copies ran while one was open for 15% of the time, Pallas kernels for 0%

profile of v3, /device:TPU:0, one launch (start us, length us, event | category | flops | bytes accessed | tf_op | source)
XLA Modules:
  0.0 545.8 jit_solution(3646251461143239241)
XLA Ops:
  7.2 0.0 all-gather.6.cloned.1.call-start
  7.2 0.7 all-gather.6.cloned.1.call-update
  7.9 0.0 all-gather.8.cloned.1.call-start
  7.9 26.1 %all_to_all.19 = bf16[8,128,512]{2,1,0:T(8,128)(2,1)S(1)} all-to-all(bf16[8,128,512]{2,1,0:T(8,128)(2,1)} %bitcast.46), channel_id=1, replica_groups=mesh['loop'=16,'width'=8] {'width'}, dimensions={0} | all-to-all | bytes 2097152 | tf_op jit(solution)/shard_map/all_to_all | solution.py:35
  34.1 0.7 copy.32
  34.7 0.1 collective-permute-start
  34.8 40.4 %collective-permute-done = bf16[128,4096]{0,1:T(8,128)(2,1)S(1)} collective-permute-done((bf16[128,4096]{0,1:T(8,128)(2,1)S(1)}, bf16[128,4096]{0,1:T(8,128)(2,1)S(1)}, u32[]{:S(2)}, u32[]{:S(2)}) %collective-permute-start) | collective-permute-done | bytes 1048608 | tf_op jit(solution)/shard_map/ppermute | solution.py:15
  75.2 11.8 %convert_bitcast_fusion = f32[128,8,32,128]{3,1,2,0:T(8,128)} fusion(bf16[1024,4096]{1,0:T(8,128)(2,1)} %param.6), kind=kLoop, calls=%fused_computation | loop fusion | flops 4194304 | bytes 25165824
  87.1 14.1 %copy.46 = f32[128,8,32,128]{3,2,1,0:T(8,128)} copy(f32[128,8,32,128]{3,1,2,0:T(8,128)} %convert_bitcast_fusion) | data formatting | bytes 33554432
  101.2 14.6 %collective-permute-done.1 = bf16[128,4096]{0,1:T(8,128)(2,1)} collective-permute-done((bf16[128,4096]{0,1:T(8,128)(2,1)S(1)}, bf16[128,4096]{0,1:T(8,128)(2,1)}, u32[]{:S(2)}, u32[]{:S(2)}) %collective-permute-start.1) | collective-permute-done | bytes 1048608 | tf_op jit(solution)/shard_map/ppermute | solution.py:15
  115.8 0.5 collective-permute-start.2
  116.3 7.9 %constant_dynamic-slice_fusion = f32[1024,4,1,128]{3,2,1,0:T(1,128)S(1)} fusion(f32[1024,4,8,128]{3,2,1,0:T(8,128)} %bitcast.45, s32[]{:T(128)S(6)} %select_n.37), kind=kLoop, calls=%fused_computation.50 | loop fusion | bytes 4194308 | tf_op jit(solution)/shard_map/dynamic_slice | solution.py:52
  124.2 4.4 copy.45
  128.6 7.0 %convert_reduce_fusion = (f32[1024]{0:T(1024)S(1)}, f32[1024]{0:T(1024)S(1)}) fusion(bf16[1024,4096]{1,0:T(8,128)(2,1)} %param.6, s32[1024]{0:T(1024)S(1)} %copy-done.16), kind=kLoop, calls=%fused_computation.1 | loop fusion | flops 20969472 | bytes 8400896 | tf_op jit(solution)/shard_map/reduce_sum | solution.py:47
  135.6 8.3 %collective-permute-done.2 = bf16[128,4096]{0,1:T(8,128)(2,1)} collective-permute-done((bf16[128,4096]{0,1:T(8,128)(2,1)}, bf16[128,4096]{0,1:T(8,128)(2,1)}, u32[]{:S(2)}, u32[]{:S(2)}) %collective-permute-start.2) | collective-permute-done | bytes 1048608 | tf_op jit(solution)/shard_map/ppermute | solution.py:15
  144.0 8.6 %multiply_reduce_fusion = (f32[1024]{0:T(1024)S(1)}, f32[512,1024]{1,0:T(8,128)S(1)}) fusion(bf16[1024,4096]{1,0:T(8,128)(2,1)} %all-gather.6.cloned.1.call-done, bf16[128,4096]{0,1:T(8,128)(2,1)} %collective-permute-done.2, bf16[128,4096]{0,1:T(8,128)(2,1)} %collective-permute-done.1, bf16[128,4096]{0,1:T(8,128)(2,1)S(1)} %copy-done.22, ...), kind=kOutput, calls=%fused_computation.22 | convolution fusion | flops 4312792064 | bytes 14684160 | tf_op jit(solution)/shard_map/qd,cd->qc/dot_general | solution.py:41
  152.6 1.3 copy-done.2
  153.9 0.3 fusion.9
  154.3 0.2 copy.33
  154.5 39.8 %psum.7 = f32[2,1024]{0,1:T(8,128)S(1)} all-reduce(f32[2,1024]{0,1:T(8,128)S(1)} %copy.33), channel_id=1, replica_groups=mesh['loop'=16,'width'=8] {'width'}, use_global_device_ids=true, to_apply=%region_2.3 | all-reduce | flops 2048 | bytes 16384 | tf_op jit(solution)/shard_map/psum | solution.py:58
  194.3 0.5 slice_reduce_fusion
  194.8 2.8 fusion.11
  197.6 0.8 slice.55
  198.5 0.0 all-gather.10.cloned.1.call-start
  198.5 47.8 %all-gather.8.cloned.1.call-done = f32[1024,1024]{0,1:T(8,128)} async-done(((f32[1024,128]{0,1:T(8,128)}), f32[1024,1024]{0,1:T(8,128)}) %all-gather.8.cloned.1.call-update) | async-done | bytes 4194320 | tf_op jit(solution)/shard_map/all_gather | solution.py:80
  246.3 1.2 slice.58
  248.2 0.9 slice_add_fusion.2
  249.1 0.0 all-gather.12.cloned.1.call-start
  249.2 1.2 slice.56
  251.0 1.3 broadcast_add_fusion
  252.3 1.0 copy-done.10
  253.3 35.2 %collective-permute-done.3 = bf16[1024,512]{1,0:T(8,128)(2,1)S(1)} collective-permute-done((bf16[1024,512]{1,0:T(8,128)(2,1)S(1)}, bf16[1024,512]{1,0:T(8,128)(2,1)S(1)}, u32[]{:S(2)}, u32[]{:S(2)}) %collective-permute-start.3) | collective-permute-done | bytes 1048608 | tf_op jit(solution)/shard_map/ppermute | solution.py:15
  288.5 33.2 %collective-permute-done.4 = bf16[1024,512]{1,0:T(8,128)(2,1)S(1)} collective-permute-done((bf16[1024,512]{1,0:T(8,128)(2,1)S(1)}, bf16[1024,512]{1,0:T(8,128)(2,1)S(1)}, u32[]{:S(2)}, u32[]{:S(2)}) %collective-permute-start.4) | collective-permute-done | bytes 1048608 | tf_op jit(solution)/shard_map/ppermute | solution.py:15
  321.7 0.2 collective-permute-start.5
  321.9 0.8 copy-done.19
  322.7 17.0 %collective-permute-done.5 = bf16[1024,512]{1,0:T(8,128)(2,1)S(1)} collective-permute-done((bf16[1024,512]{1,0:T(8,128)(2,1)S(1)}, bf16[1024,512]{1,0:T(8,128)(2,1)S(1)}, u32[]{:S(2)}, u32[]{:S(2)}) %collective-permute-start.5) | collective-permute-done | bytes 1048608 | tf_op jit(solution)/shard_map/ppermute | solution.py:15
  339.7 1.0 copy-done.14
  340.7 0.5 slice.62
  341.9 5.7 %fusion.29 = f32[1024,512]{0,1:T(8,128)S(1)} fusion(f32[1024,1024]{0,1:T(8,128)} %all-gather.8.cloned.1.call-done, bf16[1024,512]{1,0:T(8,128)(2,1)S(1)} %copy-done), kind=kOutput, calls=%fused_computation.53 | convolution fusion | flops 6442450944 | bytes 7340032 | tf_op jit(solution)/shard_map/dot_general | solution.py:24
  347.6 1.3 copy-done.6
  348.9 0.6 slice.61
  350.2 1.3 slice.60
  352.2 0.9 fusion.16
  353.1 0.0 all-gather.14.cloned.1.call-start
  353.2 0.1 collective-permute-start.6
  353.2 62.2 %collective-permute-done.6 = f32[1024,512]{0,1:T(8,128)S(1)} collective-permute-done((f32[1024,512]{0,1:T(8,128)}, f32[1024,512]{0,1:T(8,128)S(1)}, u32[]{:S(2)}, u32[]{:S(2)}) %collective-permute-start.6) | collective-permute-done | bytes 2097184 | tf_op jit(solution)/shard_map/ppermute | solution.py:15
  415.4 5.8 %convolution_add_fusion = f32[1024,512]{0,1:T(8,128)S(1)} fusion(f32[1024,512]{0,1:T(8,128)S(1)} %collective-permute-done.6, f32[1024,1024]{0,1:T(8,128)} %all-gather.10.cloned.1.call-done, bf16[1024,512]{1,0:T(8,128)(2,1)S(1)} %copy-done), kind=kOutput, calls=%fused_computation.23 | convolution fusion | flops 6442975232 | bytes 9437184 | tf_op jit(solution)/shard_map/dot_general | solution.py:24
  421.3 1.3 copy-done.7
  422.6 0.5 slice.65
  423.8 1.2 slice.64
  425.5 0.9 fusion.14
  426.4 5.5 %collective-permute-start.7 = (f32[1024,512]{0,1:T(8,128)}, f32[1024,512]{0,1:T(8,128)S(1)}, u32[]{:S(2)}, u32[]{:S(2)}) collective-permute-start(f32[1024,512]{0,1:T(8,128)} %copy-done.7), channel_id=1, source_target_pairs={{8,0},{16,8},{24,16},{32,24},{40,32},{48,40},{56,48},{64,56},{72,6... | collective-permute-start | bytes 6291464 | tf_op jit(solution)/shard_map/ppermute | solution.py:15
  431.9 5.7 %fusion.32 = f32[1024,512]{0,1:T(8,128)S(1)} fusion(f32[1024,1024]{0,1:T(8,128)} %all-gather.12.cloned.1.call-done, bf16[1024,512]{1,0:T(8,128)(2,1)S(1)} %copy-done), kind=kOutput, calls=%fused_computation.56 | convolution fusion | flops 6442450944 | bytes 7340032 | tf_op jit(solution)/shard_map/dot_general | solution.py:24
  437.6 57.5 %collective-permute-done.7 = f32[1024,512]{0,1:T(8,128)S(1)} collective-permute-done((f32[1024,512]{0,1:T(8,128)}, f32[1024,512]{0,1:T(8,128)S(1)}, u32[]{:S(2)}, u32[]{:S(2)}) %collective-permute-start.7) | collective-permute-done | bytes 2097184 | tf_op jit(solution)/shard_map/ppermute | solution.py:15
  495.1 0.4 add.179
  495.5 5.7 %collective-permute-start.8 = (f32[1024,512]{0,1:T(8,128)S(1)}, f32[1024,512]{0,1:T(8,128)}, u32[]{:S(2)}, u32[]{:S(2)}) collective-permute-start(f32[1024,512]{0,1:T(8,128)S(1)} %add.179), channel_id=1, source_target_pairs={{8,0},{16,8},{24,16},{32,24},{40,32},{48,40},{56,48},{64,56},{72,6... | collective-permute-start | bytes 6291464 | tf_op jit(solution)/shard_map/ppermute | solution.py:15
  501.2 4.8 fusion.28
  506.1 4.8 fusion.30
  510.8 5.9 %fusion.33 = f32[1024,512]{0,1:T(8,128)S(1)} fusion(f32[1024,1024]{0,1:T(8,128)} %all-gather.14.cloned.1.call-done, bf16[1024,512]{1,0:T(8,128)(2,1)S(1)} %copy-done), kind=kOutput, calls=%fused_computation.57 | convolution fusion | flops 6442450944 | bytes 7340032 | tf_op jit(solution)/shard_map/dot_general | solution.py:24
  516.8 8.0 %collective-permute-done.8 = f32[1024,512]{0,1:T(8,128)} collective-permute-done((f32[1024,512]{0,1:T(8,128)S(1)}, f32[1024,512]{0,1:T(8,128)}, u32[]{:S(2)}, u32[]{:S(2)}) %collective-permute-start.8) | collective-permute-done | bytes 2097184 | tf_op jit(solution)/shard_map/ppermute | solution.py:15
  524.8 2.0 add.180
  526.8 1.8 copy.40
  528.6 5.4 fusion.31
  534.1 4.9 add_add_fusion
  (54 shorter events, 0.2 us)
Async XLA Ops:
  7.2 136.8 %all-gather.6.cloned.1.call-start = ((), (), s32[]{:S(2)}) async-start(), calls=%async_computation.1 | async-start | bytes 9437184 | tf_op jit(solution)/shard_map/all_gather | solution.py:34
  7.9 238.4 %all-gather.8.cloned.1.call-start = ((), (), s32[]{:S(2)}) async-start(), calls=%async_computation.2 | async-start | bytes 4718592 | tf_op jit(solution)/shard_map/all_gather | solution.py:80
  34.7 52.4 %copy-start.12 = (bf16[128,8,512]{0,2,1:T(8,128)(2,1)}, bf16[128,8,512]{0,2,1:T(8,128)(2,1)S(1)}, u32[]{:S(2)}) copy-start(bf16[128,8,512]{0,2,1:T(8,128)(2,1)S(1)} %copy.32) | copy-start | bytes 3145732
  34.7 40.5 %collective-permute-start = (bf16[128,4096]{0,1:T(8,128)(2,1)S(1)}, bf16[128,4096]{0,1:T(8,128)(2,1)S(1)}, u32[]{:S(2)}, u32[]{:S(2)}) collective-permute-start(bf16[128,4096]{0,1:T(8,128)(2,1)S(1)} %bitcast.48), channel_id=1, source_target_pairs={{120,0},{0,8},{8,16},{16,24},{24,32},{32,40},{40,48},{48,56},{56,6... | collective-permute-start | bytes 3145736 | tf_op jit(solution)/shard_map/ppermute | solution.py:15
  75.2 11.8 %copy-start.21 = (bf16[128,4096]{0,1:T(8,128)(2,1)}, bf16[128,4096]{0,1:T(8,128)(2,1)S(1)}, u32[]{:S(2)}) copy-start(bf16[128,4096]{0,1:T(8,128)(2,1)S(1)} %collective-permute-done) | copy-start | bytes 3145732
  75.2 40.5 %collective-permute-start.1 = (bf16[128,4096]{0,1:T(8,128)(2,1)S(1)}, bf16[128,4096]{0,1:T(8,128)(2,1)}, u32[]{:S(2)}, u32[]{:S(2)}) collective-permute-start(bf16[128,4096]{0,1:T(8,128)(2,1)S(1)} %collective-permute-done), channel_id=1, source_target_pairs={{120,0},{0,8},{8,16},{16,24},{24,32},{32,40},{40,48},{48,56},{56,6... | collective-permute-start | bytes 3145736 | tf_op jit(solution)/shard_map/ppermute | solution.py:15
  115.8 28.2 %collective-permute-start.2 = (bf16[128,4096]{0,1:T(8,128)(2,1)}, bf16[128,4096]{0,1:T(8,128)(2,1)}, u32[]{:S(2)}, u32[]{:S(2)}) collective-permute-start(bf16[128,4096]{0,1:T(8,128)(2,1)} %collective-permute-done.1), channel_id=1, source_target_pairs={{120,0},{0,8},{8,16},{16,24},{24,32},{32,40},{40,48},{48,56},{56,6... | collective-permute-start | bytes 3145736 | tf_op jit(solution)/shard_map/ppermute | solution.py:15
  124.2 4.4 copy-start.16
  128.6 15.3 %copy-start.13 = (bf16[128,8,512]{0,2,1:T(8,128)(2,1)S(1)}, bf16[128,8,512]{0,2,1:T(8,128)(2,1)}, u32[]{:S(2)}) copy-start(bf16[128,8,512]{0,2,1:T(8,128)(2,1)} %copy-done.12) | copy-start | bytes 3145732
  128.6 15.3 %copy-start.22 = (bf16[128,4096]{0,1:T(8,128)(2,1)S(1)}, bf16[128,4096]{0,1:T(8,128)(2,1)}, u32[]{:S(2)}) copy-start(bf16[128,4096]{0,1:T(8,128)(2,1)} %copy-done.21) | copy-start | bytes 3145732
  152.6 1.3 copy-start.2
  194.3 3.3 copy-start.3
  198.4 143.4 %copy-start = (bf16[1024,512]{1,0:T(8,128)(2,1)S(1)}, bf16[1024,512]{1,0:T(8,128)(2,1)}, u32[]{:S(2)}) copy-start(bf16[1024,512]{1,0:T(8,128)(2,1)} %param.4) | copy-start | bytes 3145732
  198.5 151.7 %all-gather.10.cloned.1.call-start = ((), (), s32[]{:S(2)}) async-start(), calls=%async_computation.3 | async-start | bytes 4718592 | tf_op jit(solution)/shard_map/all_gather | solution.py:80
  249.1 174.6 %all-gather.12.cloned.1.call-start = ((), (), s32[]{:S(2)}) async-start(), calls=%async_computation.4 | async-start | bytes 4718592 | tf_op jit(solution)/shard_map/all_gather | solution.py:80
  252.3 1.0 copy-start.10
  253.3 35.2 %collective-permute-start.3 = (bf16[1024,512]{1,0:T(8,128)(2,1)S(1)}, bf16[1024,512]{1,0:T(8,128)(2,1)S(1)}, u32[]{:S(2)}, u32[]{:S(2)}) collective-permute-start(bf16[1024,512]{1,0:T(8,128)(2,1)S(1)} %broadcast_add_fusion), channel_id=1, source_target_pairs={{120,0},{0,8},{8,16},{16,24},{24,32},{32,40},{40,48},{48,56},{56,6... | collective-permute-start | bytes 3145736 | tf_op jit(solution)/shard_map/ppermute | solution.py:15
  288.5 33.2 %copy-start.17 = (bf16[1024,512]{1,0:T(8,128)(2,1)}, bf16[1024,512]{1,0:T(8,128)(2,1)S(1)}, u32[]{:S(2)}) copy-start(bf16[1024,512]{1,0:T(8,128)(2,1)S(1)} %collective-permute-done.3) | copy-start | bytes 3145732
  288.5 33.2 %collective-permute-start.4 = (bf16[1024,512]{1,0:T(8,128)(2,1)S(1)}, bf16[1024,512]{1,0:T(8,128)(2,1)S(1)}, u32[]{:S(2)}, u32[]{:S(2)}) collective-permute-start(bf16[1024,512]{1,0:T(8,128)(2,1)S(1)} %collective-permute-done.3), channel_id=1, source_target_pairs={{120,0},{0,8},{8,16},{16,24},{24,32},{32,40},{40,48},{48,56},{56,6... | collective-permute-start | bytes 3145736 | tf_op jit(solution)/shard_map/ppermute | solution.py:15
  321.7 1.0 copy-start.19
  321.7 18.0 %collective-permute-start.5 = (bf16[1024,512]{1,0:T(8,128)(2,1)S(1)}, bf16[1024,512]{1,0:T(8,128)(2,1)S(1)}, u32[]{:S(2)}, u32[]{:S(2)}) collective-permute-start(bf16[1024,512]{1,0:T(8,128)(2,1)S(1)} %collective-permute-done.4), channel_id=1, source_target_pairs={{120,0},{0,8},{8,16},{16,24},{24,32},{32,40},{40,48},{48,56},{56,6... | collective-permute-start | bytes 3145736 | tf_op jit(solution)/shard_map/ppermute | solution.py:15
  339.7 1.0 copy-start.14
  347.6 1.3 copy-start.6
  353.1 157.7 %all-gather.14.cloned.1.call-start = ((), (), s32[]{:S(2)}) async-start(), calls=%async_computation.5 | async-start | bytes 4718592 | tf_op jit(solution)/shard_map/all_gather | solution.py:80
  353.2 62.3 %collective-permute-start.6 = (f32[1024,512]{0,1:T(8,128)}, f32[1024,512]{0,1:T(8,128)S(1)}, u32[]{:S(2)}, u32[]{:S(2)}) collective-permute-start(f32[1024,512]{0,1:T(8,128)} %copy-done.6), channel_id=1, source_target_pairs={{8,0},{16,8},{24,16},{32,24},{40,32},{48,40},{56,48},{64,56},{72,6... | collective-permute-start | bytes 6291464 | tf_op jit(solution)/shard_map/ppermute | solution.py:15
  421.3 1.3 copy-start.7
  426.4 68.7 %collective-permute-start.7 = (f32[1024,512]{0,1:T(8,128)}, f32[1024,512]{0,1:T(8,128)S(1)}, u32[]{:S(2)}, u32[]{:S(2)}) collective-permute-start(f32[1024,512]{0,1:T(8,128)} %copy-done.7), channel_id=1, source_target_pairs={{8,0},{16,8},{24,16},{32,24},{40,32},{48,40},{56,48},{64,56},{72,6... | collective-permute-start | bytes 6291464 | tf_op jit(solution)/shard_map/ppermute | solution.py:15
  437.6 63.6 %copy-start.5 = (f32[1024,1024]{0,1:T(8,128)S(1)}, f32[1024,1024]{0,1:T(8,128)}, u32[]{:S(2)}) copy-start(f32[1024,1024]{0,1:T(8,128)} %all-gather.10.cloned.1.call-done) | copy-start | bytes 12582916
  437.6 63.6 %copy-start.20 = (bf16[1024,512]{1,0:T(8,128)(2,1)S(1)}, bf16[1024,512]{1,0:T(8,128)(2,1)}, u32[]{:S(2)}) copy-start(bf16[1024,512]{1,0:T(8,128)(2,1)} %copy-done.19) | copy-start | bytes 3145732
  495.5 10.6 %copy-start.4 = (f32[1024,1024]{0,1:T(8,128)S(1)}, f32[1024,1024]{0,1:T(8,128)}, u32[]{:S(2)}) copy-start(f32[1024,1024]{0,1:T(8,128)} %all-gather.12.cloned.1.call-done) | copy-start | bytes 12582916
  495.5 10.5 %copy-start.18 = (bf16[1024,512]{1,0:T(8,128)(2,1)S(1)}, bf16[1024,512]{1,0:T(8,128)(2,1)}, u32[]{:S(2)}) copy-start(bf16[1024,512]{1,0:T(8,128)(2,1)} %copy-done.17) | copy-start | bytes 3145732
  495.5 29.2 %collective-permute-start.8 = (f32[1024,512]{0,1:T(8,128)S(1)}, f32[1024,512]{0,1:T(8,128)}, u32[]{:S(2)}, u32[]{:S(2)}) collective-permute-start(f32[1024,512]{0,1:T(8,128)S(1)} %add.179), channel_id=1, source_target_pairs={{8,0},{16,8},{24,16},{32,24},{40,32},{48,40},{56,48},{64,56},{72,6... | collective-permute-start | bytes 6291464 | tf_op jit(solution)/shard_map/ppermute | solution.py:15
  526.8 1.8 copy-start.11
  528.6 5.5 %copy-start.1 = (f32[1024,1024]{0,1:T(8,128)S(1)}, f32[1024,1024]{0,1:T(8,128)}, u32[]{:S(2)}) copy-start(f32[1024,1024]{0,1:T(8,128)} %all-gather.8.cloned.1.call-done) | copy-start | bytes 12582916
  528.6 5.5 %copy-start.8 = (f32[1024,512]{1,0:T(8,128)S(1)}, f32[1024,512]{1,0:T(8,128)}, u32[]{:S(2)}) copy-start(f32[1024,512]{1,0:T(8,128)} %fusion.28) | copy-start | bytes 6291460
  528.6 5.5 %copy-start.9 = (f32[1024,512]{1,0:T(8,128)S(1)}, f32[1024,512]{1,0:T(8,128)}, u32[]{:S(2)}) copy-start(f32[1024,512]{1,0:T(8,128)} %fusion.30) | copy-start | bytes 6291460
  528.6 5.5 %copy-start.15 = (bf16[1024,512]{1,0:T(8,128)(2,1)S(1)}, bf16[1024,512]{1,0:T(8,128)(2,1)}, u32[]{:S(2)}) copy-start(bf16[1024,512]{1,0:T(8,128)(2,1)} %copy-done.14) | copy-start | bytes 3145732
Sparse Core Ops, SparseCore 0:
  9.6 98.8 all-gather.5
  198.6 47.7 all-gather.7
  249.2 51.2 all-gather.9
  353.2 65.4 all-gather.11
  426.6 67.2 all-gather.13

commit v4 on v2

--- a/solution.py
+++ b/solution.py
@@ -27,12 +27,10 @@
     window = STEPS * rows
 
     q_full = lax.all_gather(queries, "width", axis=1, tiled=True)
-    p_cols = lax.all_to_all(passages, "width", 0, 1, tiled=True)
-    held_cols = [p_cols]
     held = [passages]
     for step in range(1, STEPS):
-        held_cols.append(shifted(held_cols[-1], "loop", 1))
         held.append(shifted(held[-1], "loop", 1))
+    held_cols = [lax.all_to_all(block, "width", 0, 1, tiled=True) for block in held]
 
     cols = jnp.concatenate(held_cols, 0)
     scores = SCALE * jnp.einsum("qd,cd->qc", q_full, cols, preferred_element_type=jnp.float32)

time: 458 us -> 501 us (1.094)
  waiting for transfers between devices: 277 us -> 312 us
  blocking collectives: 46.2 us -> 20.3 us
  starting transfers between devices: 16.3 us -> 37.1 us
  local copies, waits for them, and re-layouts: 36.7 us -> 44.3 us
    all_to_all x1 -> x0, blocking collectives: 26.1 us -> none  [per_device(): p_cols = lax.all_to_all(passages, 'width', 0, 1, tiled=True)]
    ppermute x9 -> x6, waiting for transfers between devices: 110 us -> 134 us  [shifted(): return lax.ppermute(block, axis, route)]
    all_to_all x0 -> x4, starting transfers between devices: none -> 20.4 us  [per_device(): lax.all_to_all(block, 'width', 0, 1, tiled=True)]
    all_gather x1, waiting for transfers between devices: 166 us -> 177 us  [per_device(): slopes = lax.all_gather(slopes_cols, 'width', axis=1, tiled=True)]
    all_to_all x1 -> x4, local copies, waits for them, and re-layouts: 0.65 us -> 8.2 us  [per_device(): lax.all_to_all(block, 'width', 0, 1, tiled=True)]
    ppermute x9 -> x6, starting transfers between devices: 16.2 us -> 16.4 us  [shifted(): return lax.ppermute(block, axis, route)]
    unnamed x12 -> x14, local copies, waits for them, and re-layouts: 20 us -> 20.1 us
  transfers between devices with their start and end apart: 11 -> 12, of which waited for: 8 -> 7; matrix products, arithmetic and copies ran while one was open for 16% -> 16% of each run, Pallas kernels for 0% -> 0%
where the time goes in v4:
time: 501 us; the launch traced here: 495 us
  waiting for transfers between devices  312 us (62%)
  local copies, waits for them, and re-layouts  44.3 us (9%)
  matrix products  42.2 us (8%)
  starting transfers between devices  37.1 us (7%)
  other arithmetic  24.7 us (5%)
  blocking collectives  20.3 us (4%)
  between operations  14.5 us (3%)
    all_gather x1, waiting for transfers between devices, per_device(): slopes = lax.all_gather(slopes_cols, 'width', axis=1, tiled=True)  177 us
    ppermute x6, waiting for transfers between devices, shifted(): return lax.ppermute(block, axis, route)  134 us
    dot_general x8, matrix products, wide_dot(): jnp.dot(a, b, precision=lax.Precision.HIGHEST, preferred_element_type=jnp...  33.3 us
    all_to_all x4, starting transfers between devices, per_device(): lax.all_to_all(block, 'width', 0, 1, tiled=True)  20.4 us
    psum x1, blocking collectives, per_device(): stats = lax.psum(jnp.stack([pos_part, row_part], 0), 'width')  20.3 us
    unnamed x14, local copies, waits for them, and re-layouts  20.1 us
    ppermute x6, starting transfers between devices, shifted(): return lax.ppermute(block, axis, route)  16.4 us
    unnamed x1, other arithmetic  11.5 us
  transfers between devices with their start and end apart: 12, of which 7 were waited for; matrix products, arithmetic and copies ran while one was open for 16% of the time, Pallas kernels for 0%

profile of v4, /device:TPU:0, one launch (start us, length us, event | category | flops | bytes accessed | tf_op | source)
XLA Modules:
  0.0 495.2 jit_solution(7302572149417628085)
XLA Ops:
  7.2 0.0 all-gather.3.cloned.1.call-start
  7.2 0.7 all-gather.3.cloned.1.call-update
  7.9 0.1 collective-permute-start
  8.0 5.5 %all-to-all-start = ((bf16[8,128,512]{2,1,0:T(8,128)(2,1)}), bf16[8,128,512]{2,1,0:T(8,128)(2,1)S(1)}, u32[]{:S(2)}, u32[]{:S(2)}) async-start(bf16[8,128,512]{2,1,0:T(8,128)(2,1)} %bitcast.65), calls=%async_computation | async-start | bytes 2097152 | tf_op jit(solution)/shard_map/all_to_all | solution.py:33
  13.5 24.0 %collective-permute-done = bf16[1024,512]{1,0:T(8,128)(2,1)} collective-permute-done((bf16[1024,512]{1,0:T(8,128)(2,1)}, bf16[1024,512]{1,0:T(8,128)(2,1)}, u32[]{:S(2)}, u32[]{:S(2)}) %collective-permute-start) | collective-permute-done | bytes 1048608 | tf_op jit(solution)/shard_map/ppermute | solution.py:15
  37.5 0.0 collective-permute-start.1
  37.5 0.0 all-to-all-done
  37.5 4.9 all-to-all-start.1
  42.4 51.6 %collective-permute-done.1 = bf16[1024,512]{1,0:T(8,128)(2,1)} collective-permute-done((bf16[1024,512]{1,0:T(8,128)(2,1)}, bf16[1024,512]{1,0:T(8,128)(2,1)}, u32[]{:S(2)}, u32[]{:S(2)}) %collective-permute-start.1) | collective-permute-done | bytes 1048608 | tf_op jit(solution)/shard_map/ppermute | solution.py:15
  94.1 0.0 collective-permute-start.2
  94.1 0.0 all-to-all-done.1
  94.1 0.0 copy-start.2
  94.1 5.3 %all-to-all-start.2 = ((bf16[8,128,512]{2,1,0:T(8,128)(2,1)}), bf16[8,128,512]{2,1,0:T(8,128)(2,1)}, u32[]{:S(2)}, u32[]{:S(2)}) async-start(bf16[8,128,512]{2,1,0:T(8,128)(2,1)} %bitcast.6), calls=%async_computation.2 | async-start | bytes 2097152 | tf_op jit(solution)/shard_map/all_to_all | solution.py:33
  99.3 11.5 %convert_bitcast_fusion = f32[128,8,32,128]{3,1,2,0:T(8,128)} fusion(bf16[1024,4096]{1,0:T(8,128)(2,1)} %param.6), kind=kLoop, calls=%fused_computation | loop fusion | flops 4194304 | bytes 25165824
  110.8 0.0 copy-done.2
  110.8 14.2 %copy.14 = f32[128,8,32,128]{3,2,1,0:T(8,128)} copy(f32[128,8,32,128]{3,1,2,0:T(8,128)} %convert_bitcast_fusion) | data formatting | bytes 33554432
  125.0 9.2 %constant_dynamic-slice_fusion = f32[1024,4,1,128]{3,2,1,0:T(1,128)} fusion(f32[1024,4,8,128]{3,2,1,0:T(8,128)} %bitcast.55, s32[]{:T(128)S(6)} %select_n.37), kind=kLoop, calls=%fused_computation.40 | loop fusion | bytes 4194308 | tf_op jit(solution)/shard_map/dynamic_slice | solution.py:47
  134.2 0.0 copy-start.5
  134.2 4.6 copy.13
  138.8 0.0 all-to-all-done.2
  138.8 14.5 %collective-permute-done.2 = bf16[1024,512]{1,0:T(8,128)(2,1)} collective-permute-done((bf16[1024,512]{1,0:T(8,128)(2,1)}, bf16[1024,512]{1,0:T(8,128)(2,1)}, u32[]{:S(2)}, u32[]{:S(2)}) %collective-permute-start.2) | collective-permute-done | bytes 1048608 | tf_op jit(solution)/shard_map/ppermute | solution.py:15
  153.3 4.7 all-to-all-start.3
  158.0 0.3 all-gather.5.cloned.1.call-start
  158.4 0.0 copy-done.5
  158.4 6.8 %convert_reduce_fusion = (f32[1024]{0:T(1024)S(1)}, f32[1024]{0:T(1024)S(1)}) fusion(bf16[1024,4096]{1,0:T(8,128)(2,1)} %param.6, s32[1024]{0:T(1024)S(1)} %copy-done.5), kind=kLoop, calls=%fused_computation.1 | loop fusion | flops 20969472 | bytes 8400896 | tf_op jit(solution)/shard_map/reduce_sum | solution.py:42
  165.2 1.3 copy.8
  166.6 0.0 copy-start.4
  166.6 2.4 copy.9
  168.9 2.3 copy.10
  171.2 0.0 all-to-all-done.3
  171.2 2.3 copy.11
  173.4 0.0 all-gather.3.cloned.1.call-done
  173.4 0.0 copy-done.4
  173.4 8.9 %multiply_reduce_fusion = (f32[1024]{0:T(1024)S(1)}, f32[512,1024]{1,0:T(8,128)S(1)}) fusion(bf16[1024,4096]{1,0:T(8,128)(2,1)} %all-gather.3.cloned.1.call-done, bf16[128,4096]{0,1:T(8,128)(2,1)} %bitcast.69, bf16[128,4096]{0,1:T(8,128)(2,1)} %bitcast.68, bf16[128,4096]{0,1:T(8,128)(2,1)} %bitcast.67, bf16[128,4096]{0,1:T(8,128)(2,1)S(1)} %bitcast.66), kind=kOutput, calls=%fused_computation.22 | convolution fusion | flops 4312792064 | bytes 14684160 | tf_op jit(solution)/shard_map/qd,cd->qc/dot_general | solution.py:36
  182.3 0.0 copy-start.1
  182.4 1.3 copy-done.1
  183.7 0.3 fusion.9
  184.0 20.3 %psum.7 = f32[2,1024]{1,0:T(2,128)S(1)} all-reduce(f32[2,1024]{1,0:T(2,128)S(1)} %pad_maximum_fusion), channel_id=1, replica_groups=mesh['loop'=16,'width'=8] {'width'}, use_global_device_ids=true, to_apply=%region_2.3 | all-reduce | flops 2048 | bytes 16384 | tf_op jit(solution)/shard_map/psum | solution.py:53
  204.4 3.7 fusion.11
  208.1 0.0 all-gather.5.cloned.1.call-update
  208.1 177.0 %all-gather.5.cloned.1.call-done = f32[1024,4096]{0,1:T(8,128)} async-done(((f32[1024,512]{0,1:T(8,128)}), f32[1024,4096]{0,1:T(8,128)}) %all-gather.5.cloned.1.call-update) | async-done | bytes 16777232 | tf_op jit(solution)/shard_map/all_gather | solution.py:61
  385.1 0.0 copy-start
  385.1 6.8 %fusion.24 = (f32[1024,8,1,128]{0,3,2,1:T(8,128)S(1)}, f32[1024,8,1,128]{0,3,2,1:T(8,128)S(1)}, f32[1024,8,1,128]{0,3,2,1:T(8,128)S(1)}, f32[1024,8,1,128]{0,3,2,1:T(8,128)S(1)}) fusion(f32[1024,8,4,128]{0,3,2,1:T(8,128)} %bitcast.56), kind=kLoop, calls=%fused_computation.42 | loop fusion | bytes 33554432 | tf_op jit(solution)/shard_map/slice | solution.py:68
  392.0 0.0 copy-done
  392.0 3.5 fusion.29
  395.4 4.9 collective-permute-start.3
  400.4 23.6 %collective-permute-done.3 = f32[1024,512]{1,0:T(8,128)S(1)} collective-permute-done((f32[1024,512]{1,0:T(8,128)S(1)}, f32[1024,512]{1,0:T(8,128)S(1)}, u32[]{:S(2)}, u32[]{:S(2)}) %collective-permute-start.3) | collective-permute-done | bytes 2097184 | tf_op jit(solution)/shard_map/ppermute | solution.py:15
  423.9 3.5 convolution_add_fusion
  427.4 5.6 %collective-permute-start.4 = (f32[1024,512]{1,0:T(8,128)S(1)}, f32[1024,512]{1,0:T(8,128)S(1)}, u32[]{:S(2)}, u32[]{:S(2)}) collective-permute-start(f32[1024,512]{1,0:T(8,128)S(1)} %convolution_add_fusion), channel_id=1, source_target_pairs={{8,0},{16,8},{24,16},{32,24},{40,32},{48,40},{56,48},{64,56},{72,6... | collective-permute-start | bytes 6291464 | tf_op jit(solution)/shard_map/ppermute | solution.py:15
  433.0 3.5 fusion.30
  436.5 0.0 copy-start.3
  436.5 20.1 %collective-permute-done.4 = f32[1024,512]{1,0:T(8,128)S(1)} collective-permute-done((f32[1024,512]{1,0:T(8,128)S(1)}, f32[1024,512]{1,0:T(8,128)S(1)}, u32[]{:S(2)}, u32[]{:S(2)}) %collective-permute-start.4) | collective-permute-done | bytes 2097184 | tf_op jit(solution)/shard_map/ppermute | solution.py:15
  456.5 0.5 add.77
  457.0 5.8 %collective-permute-start.5 = (f32[1024,512]{1,0:T(8,128)S(1)}, f32[1024,512]{1,0:T(8,128)S(1)}, u32[]{:S(2)}, u32[]{:S(2)}) collective-permute-start(f32[1024,512]{1,0:T(8,128)S(1)} %add.77), channel_id=1, source_target_pairs={{8,0},{16,8},{24,16},{32,24},{40,32},{48,40},{56,48},{64,56},{72,6... | collective-permute-start | bytes 6291464 | tf_op jit(solution)/shard_map/ppermute | solution.py:15
  462.8 0.0 copy-done.3
  462.8 3.5 fusion.26
  466.3 3.4 fusion.31
  469.8 4.7 fusion.28
  474.5 5.0 %fusion.27 = f32[1024,512]{1,0:T(8,128)S(1)} fusion(f32[1024,1024]{0,1:T(8,128)S(1)} %bitcast.58, bf16[1024,512]{1,0:T(8,128)(2,1)} %collective-permute-done), kind=kOutput, calls=%fused_computation.45 | convolution fusion | flops 6442450944 | bytes 7340032 | tf_op jit(solution)/shard_map/dot_general | solution.py:19
  479.5 6.2 %add_add_fusion = f32[1024,512]{1,0:T(8,128)} fusion(f32[1024,512]{1,0:T(8,128)S(1)} %fusion.28, f32[1024,512]{1,0:T(8,128)S(1)} %fusion.26, f32[1024,512]{1,0:T(8,128)S(1)} %fusion.27, f32[1024,1024]{0,1:T(8,128)S(1)} %bitcast.54, bf16[1024,512]{1,0:T(8,128)(2,1)} %collective-permute-done.2), kind=kOutput, calls=%fused_computation.21 | convolution fusion | flops 6444023808 | bytes 13631488 | tf_op jit(solution)/shard_map/dot_general | solution.py:19
  485.7 0.6 collective-permute-done.5
  486.3 1.8 add.78
  (4 shorter events, 0.0 us)
Async XLA Ops:
  7.2 166.3 %all-gather.3.cloned.1.call-start = ((), (), s32[]{:S(2)}) async-start(), calls=%async_computation.4 | async-start | bytes 9437184 | tf_op jit(solution)/shard_map/all_gather | solution.py:29
  7.9 29.6 %collective-permute-start = (bf16[1024,512]{1,0:T(8,128)(2,1)}, bf16[1024,512]{1,0:T(8,128)(2,1)}, u32[]{:S(2)}, u32[]{:S(2)}) collective-permute-start(bf16[1024,512]{1,0:T(8,128)(2,1)} %param.5), channel_id=1, source_target_pairs={{120,0},{0,8},{8,16},{16,24},{24,32},{32,40},{40,48},{48,56},{56,6... | collective-permute-start | bytes 3145736 | tf_op jit(solution)/shard_map/ppermute | solution.py:15
  8.0 29.5 %all-to-all-start = ((bf16[8,128,512]{2,1,0:T(8,128)(2,1)}), bf16[8,128,512]{2,1,0:T(8,128)(2,1)S(1)}, u32[]{:S(2)}, u32[]{:S(2)}) async-start(bf16[8,128,512]{2,1,0:T(8,128)(2,1)} %bitcast.65), calls=%async_computation | async-start | bytes 2097152 | tf_op jit(solution)/shard_map/all_to_all | solution.py:33
  37.5 56.5 %collective-permute-start.1 = (bf16[1024,512]{1,0:T(8,128)(2,1)}, bf16[1024,512]{1,0:T(8,128)(2,1)}, u32[]{:S(2)}, u32[]{:S(2)}) collective-permute-start(bf16[1024,512]{1,0:T(8,128)(2,1)} %collective-permute-done), channel_id=1, source_target_pairs={{120,0},{0,8},{8,16},{16,24},{24,32},{32,40},{40,48},{48,56},{56,6... | collective-permute-start | bytes 3145736 | tf_op jit(solution)/shard_map/ppermute | solution.py:15
  37.5 56.5 %all-to-all-start.1 = ((bf16[8,128,512]{2,1,0:T(8,128)(2,1)}), bf16[8,128,512]{2,1,0:T(8,128)(2,1)S(1)}, u32[]{:S(2)}, u32[]{:S(2)}) async-start(bf16[8,128,512]{2,1,0:T(8,128)(2,1)} %bitcast.3), calls=%async_computation.1 | async-start | bytes 2097152 | tf_op jit(solution)/shard_map/all_to_all | solution.py:33
  94.1 59.3 %collective-permute-start.2 = (bf16[1024,512]{1,0:T(8,128)(2,1)}, bf16[1024,512]{1,0:T(8,128)(2,1)}, u32[]{:S(2)}, u32[]{:S(2)}) collective-permute-start(bf16[1024,512]{1,0:T(8,128)(2,1)} %collective-permute-done.1), channel_id=1, source_target_pairs={{120,0},{0,8},{8,16},{16,24},{24,32},{32,40},{40,48},{48,56},{56,6... | collective-permute-start | bytes 3145736 | tf_op jit(solution)/shard_map/ppermute | solution.py:15
  94.1 16.7 %copy-start.2 = (bf16[8,128,512]{2,1,0:T(8,128)(2,1)}, bf16[8,128,512]{2,1,0:T(8,128)(2,1)S(1)}, u32[]{:S(2)}) copy-start(bf16[8,128,512]{2,1,0:T(8,128)(2,1)S(1)} %all-to-all-done.1) | copy-start | bytes 3145732
  94.1 44.7 %all-to-all-start.2 = ((bf16[8,128,512]{2,1,0:T(8,128)(2,1)}), bf16[8,128,512]{2,1,0:T(8,128)(2,1)}, u32[]{:S(2)}, u32[]{:S(2)}) async-start(bf16[8,128,512]{2,1,0:T(8,128)(2,1)} %bitcast.6), calls=%async_computation.2 | async-start | bytes 2097152 | tf_op jit(solution)/shard_map/all_to_all | solution.py:33
  134.2 24.2 %copy-start.5 = (s32[1024]{0:T(1024)S(1)}, s32[1024]{0:T(1024)}, u32[]{:S(2)}) copy-start(s32[1024]{0:T(1024)} %param.7) | copy-start | bytes 12292
  153.3 17.8 %all-to-all-start.3 = ((bf16[8,128,512]{2,1,0:T(8,128)(2,1)}), bf16[8,128,512]{2,1,0:T(8,128)(2,1)}, u32[]{:S(2)}, u32[]{:S(2)}) async-start(bf16[8,128,512]{2,1,0:T(8,128)(2,1)} %bitcast.9), calls=%async_computation.3 | async-start | bytes 2097152 | tf_op jit(solution)/shard_map/all_to_all | solution.py:33
  158.0 227.1 %all-gather.5.cloned.1.call-start = ((), (), s32[]{:S(2)}) async-start(), calls=%async_computation.5 | async-start | bytes 18874368 | tf_op jit(solution)/shard_map/all_gather | solution.py:61
  166.6 6.9 %copy-start.4 = (bf16[128,8,512]{0,2,1:T(8,128)(2,1)S(1)}, bf16[128,8,512]{0,2,1:T(8,128)(2,1)}, u32[]{:S(2)}) copy-start(bf16[128,8,512]{0,2,1:T(8,128)(2,1)} %copy.8) | copy-start | bytes 3145732
  182.3 1.3 copy-start.1
  385.1 6.8 %copy-start = (bf16[1024,512]{1,0:T(8,128)(2,1)S(1)}, bf16[1024,512]{1,0:T(8,128)(2,1)}, u32[]{:S(2)}) copy-start(bf16[1024,512]{1,0:T(8,128)(2,1)} %param.4) | copy-start | bytes 3145732
  395.4 28.5 %collective-permute-start.3 = (f32[1024,512]{1,0:T(8,128)S(1)}, f32[1024,512]{1,0:T(8,128)S(1)}, u32[]{:S(2)}, u32[]{:S(2)}) collective-permute-start(f32[1024,512]{1,0:T(8,128)S(1)} %fusion.29), channel_id=1, source_target_pairs={{8,0},{16,8},{24,16},{32,24},{40,32},{48,40},{56,48},{64,56},{72,6... | collective-permute-start | bytes 6291464 | tf_op jit(solution)/shard_map/ppermute | solution.py:15
  427.4 29.1 %collective-permute-start.4 = (f32[1024,512]{1,0:T(8,128)S(1)}, f32[1024,512]{1,0:T(8,128)S(1)}, u32[]{:S(2)}, u32[]{:S(2)}) collective-permute-start(f32[1024,512]{1,0:T(8,128)S(1)} %convolution_add_fusion), channel_id=1, source_target_pairs={{8,0},{16,8},{24,16},{32,24},{40,32},{48,40},{56,48},{64,56},{72,6... | collective-permute-start | bytes 6291464 | tf_op jit(solution)/shard_map/ppermute | solution.py:15
  436.5 26.3 %copy-start.3 = (bf16[1024,512]{1,0:T(8,128)(2,1)S(1)}, bf16[1024,512]{1,0:T(8,128)(2,1)}, u32[]{:S(2)}) copy-start(bf16[1024,512]{1,0:T(8,128)(2,1)} %param.5) | copy-start | bytes 3145732
  457.0 29.3 %collective-permute-start.5 = (f32[1024,512]{1,0:T(8,128)S(1)}, f32[1024,512]{1,0:T(8,128)S(1)}, u32[]{:S(2)}, u32[]{:S(2)}) collective-permute-start(f32[1024,512]{1,0:T(8,128)S(1)} %add.77), channel_id=1, source_target_pairs={{8,0},{16,8},{24,16},{32,24},{40,32},{48,40},{56,48},{64,56},{72,6... | collective-permute-start | bytes 6291464 | tf_op jit(solution)/shard_map/ppermute | solution.py:15
Sparse Core Ops, SparseCore 0:
  9.6 130.1 all-gather.2
  208.2 176.8 all-gather.4

commit v5 on v2

--- a/solution.py
+++ b/solution.py
@@ -35,32 +35,24 @@
         held.append(shifted(held[-1], "loop", 1))
 
     cols = jnp.concatenate(held_cols, 0)
-    scores = SCALE * jnp.einsum("qd,cd->qc", q_full, cols, preferred_element_type=jnp.float32)
+    raw = jnp.einsum("qd,cd->qc", q_full, cols, preferred_element_type=jnp.float32)
+    scores = SCALE * lax.all_gather(raw, "width", axis=1, tiled=True)
 
     index = positives[:, None]
     teach = teacher.astype(jnp.float32)
     column = lax.broadcasted_iota(jnp.int32, teach.shape, 1)
     t_pos = jnp.sum(jnp.where(column == index, teach, 0.0), 1, keepdims=True)
-    t_sum = jnp.sum(teach, 1, keepdims=True)
-
-    local = lax.broadcasted_iota(jnp.int32, (1, STEPS * sub), 1)
-    wcol = (local // sub) * rows + me * sub + local % sub
+    teach_perm = (
+        teach.reshape(rows, STEPS, width, sub).transpose(0, 2, 1, 3).reshape(rows, window)
+    )
+    place = lax.broadcasted_iota(jnp.int32, (1, window), 1)
+    wcol = ((place // sub) % STEPS) * rows + (place // (STEPS * sub)) * sub + place % sub
     hit = wcol == index
-    teach_cols = lax.dynamic_slice_in_dim(
-        teach.reshape(rows, STEPS, width, sub), me, 1, 2
-    ).reshape(rows, STEPS * sub)
-
-    pos_part = jnp.sum(jnp.where(hit, scores, 0.0), 1)
-    row_part = jnp.sum(scores, 1)
-    stats = lax.psum(jnp.stack([pos_part, row_part], 0), "width")
-    s_pos = stats[0][:, None]
-    s_sum = stats[1][:, None]
-    total = window * (s_pos - t_pos) - s_sum + t_sum
+    s_pos = jnp.sum(jnp.where(hit, scores, 0.0), 1, keepdims=True)
+    errors = (s_pos - scores) - (t_pos - teach_perm)
+    total = jnp.sum(errors, 1, keepdims=True)
     coef = SCALE * 2.0 / (window - 1)
-    errors = (s_pos - scores) - (t_pos - teach_cols)
-    slopes_cols = coef * (hit.astype(jnp.float32) * total - errors)
-
-    slopes = lax.all_gather(slopes_cols, "width", axis=1, tiled=True)
+    slopes = coef * (hit.astype(jnp.float32) * total - errors)
     slopes = slopes.reshape(rows, width, STEPS, sub)
 
     query_wide = queries.astype(jnp.float32)

time: 458 us -> 470 us (1.026)
  blocking collectives: 46.2 us -> 26.1 us
  other arithmetic: 25 us -> 44.5 us
  waiting for transfers between devices: 277 us -> 290 us
    ppermute x9, waiting for transfers between devices: 110 us -> 157 us  [shifted(): return lax.ppermute(block, axis, route)]
    all_gather x1, waiting for transfers between devices: 166 us -> 133 us  [per_device(): scores = SCALE * lax.all_gather(raw, 'width', axis=1, tiled=True)]
    psum x1 -> x0, blocking collectives: 20.1 us -> none  [per_device(): stats = lax.psum(jnp.stack([pos_part, row_part], 0), 'width')]
    transpose x0 -> x1, local copies, waits for them, and re-layouts: none -> 12 us  [per_device(): teach.reshape(rows, STEPS, width, sub).transpose(0, 2, 1, 3)]
    unnamed x1 -> x0, other arithmetic: 11.8 us -> none
    convert_element_type x0 -> x1, other arithmetic: none -> 11.3 us  [per_device(): teach = teacher.astype(jnp.float32)]
    reduce_sum x2, other arithmetic: 7.17 us -> 18.1 us  [the longest x1 10.5 us: per_device(): s_pos = jnp.sum(jnp.where(hit, scores, 0.0), 1, keepdims=True)]
    dynamic_slice x1 -> x0, local copies, waits for them, and re-layouts: 9.23 us -> none  [per_device(): lax.dynamic_slice_in_dim(teach.reshape(rows, STEPS, width, sub), me, 1, 2)]
  transfers between devices with their start and end apart: 11 -> 11, of which waited for: 8 -> 8; matrix products, arithmetic and copies ran while one was open for 16% -> 14% of each run, Pallas kernels for 0% -> 0%
where the time goes in v5:
time: 470 us; the launch traced here: 465 us
  waiting for transfers between devices  290 us (62%)
  other arithmetic  44.5 us (9%)
  matrix products  39.4 us (8%)
  local copies, waits for them, and re-layouts  34.2 us (7%)
  blocking collectives  26.1 us (6%)
  starting transfers between devices  16.2 us (3%)
  between operations  14.7 us (3%)
    ppermute x9, waiting for transfers between devices, shifted(): return lax.ppermute(block, axis, route)  157 us
    all_gather x1, waiting for transfers between devices, per_device(): scores = SCALE * lax.all_gather(raw, 'width', axis=1, tiled=True)  133 us
    dot_general x8, matrix products, wide_dot(): jnp.dot(a, b, precision=lax.Precision.HIGHEST, preferred_element_type=jnp...  29.8 us
    all_to_all x1, blocking collectives, per_device(): p_cols = lax.all_to_all(passages, 'width', 0, 1, tiled=True)  26.1 us
    ppermute x9, starting transfers between devices, shifted(): return lax.ppermute(block, axis, route)  16.1 us
    unnamed x9, local copies, waits for them, and re-layouts  14.7 us
    mul x1, other arithmetic, per_device(): slopes = coef * (hit.astype(jnp.float32) * total - errors)  12.9 us
    transpose x1, local copies, waits for them, and re-layouts, per_device(): teach.reshape(rows, STEPS, width, sub).transpose(0, 2, 1, 3)  12 us
  transfers between devices with their start and end apart: 11, of which 8 were waited for; matrix products, arithmetic and copies ran while one was open for 14% of the time, Pallas kernels for 0%

profile of v5, /device:TPU:0, one launch (start us, length us, event | category | flops | bytes accessed | tf_op | source)
XLA Modules:
  0.0 465.1 jit_solution(4112318248874401599)
XLA Ops:
  7.2 0.0 all-gather.3.cloned.1.call-start
  7.2 0.7 all-gather.3.cloned.1.call-update
  7.9 0.0 all-gather.5.cloned.1.call-start
  7.9 26.1 %all_to_all.19 = bf16[8,128,512]{2,1,0:T(8,128)(2,1)S(1)} all-to-all(bf16[8,128,512]{2,1,0:T(8,128)(2,1)} %bitcast.49), channel_id=1, replica_groups=mesh['loop'=16,'width'=8] {'width'}, dimensions={0} | all-to-all | bytes 2097152 | tf_op jit(solution)/shard_map/all_to_all | solution.py:30
  34.1 0.7 copy.10
  34.7 0.1 collective-permute-start
  34.8 40.4 %collective-permute-done = bf16[128,4096]{0,1:T(8,128)(2,1)S(1)} collective-permute-done((bf16[128,4096]{0,1:T(8,128)(2,1)S(1)}, bf16[128,4096]{0,1:T(8,128)(2,1)S(1)}, u32[]{:S(2)}, u32[]{:S(2)}) %collective-permute-start) | collective-permute-done | bytes 1048608 | tf_op jit(solution)/shard_map/ppermute | solution.py:15
  75.2 0.0 collective-permute-start.1
  75.2 40.4 %collective-permute-done.1 = bf16[128,4096]{0,1:T(8,128)(2,1)S(1)} collective-permute-done((bf16[128,4096]{0,1:T(8,128)(2,1)S(1)}, bf16[128,4096]{0,1:T(8,128)(2,1)S(1)}, u32[]{:S(2)}, u32[]{:S(2)}) %collective-permute-start.1) | collective-permute-done | bytes 1048608 | tf_op jit(solution)/shard_map/ppermute | solution.py:15
  115.6 0.0 collective-permute-start.2
  115.7 28.3 %collective-permute-done.2 = bf16[128,4096]{0,1:T(8,128)(2,1)} collective-permute-done((bf16[128,4096]{0,1:T(8,128)(2,1)S(1)}, bf16[128,4096]{0,1:T(8,128)(2,1)}, u32[]{:S(2)}, u32[]{:S(2)}) %collective-permute-start.2) | collective-permute-done | bytes 1048608 | tf_op jit(solution)/shard_map/ppermute | solution.py:15
  144.0 0.0 all-gather.3.cloned.1.call-done
  144.0 9.6 %fusion.13 = f32[1024,512]{0,1:T(8,128)} fusion(bf16[1024,4096]{1,0:T(8,128)(2,1)} %all-gather.3.cloned.1.call-done, bf16[128,4096]{0,1:T(8,128)(2,1)} %collective-permute-done.2, bf16[128,4096]{0,1:T(8,128)(2,1)S(1)} %collective-permute-done.1, bf16[128,4096]{0,1:T(8,128)(2,1)S(1)} %collective-permute-done, bf16[128,4096]{0,1:T(8,128)(2,1)S(1)} %bitcast.51), kind=kOutput, calls=%fused_computation.19 | convolution fusion | flops 4311744512 | bytes 14680064 | tf_op jit(solution)/shard_map/qd,cd->qc/dot_general | solution.py:38
  153.6 0.0 all-gather.5.cloned.1.call-update
  153.6 12.2 %copy.11 = bf16[1024,4096]{0,1:T(8,128)(2,1)} copy(bf16[1024,4096]{1,0:T(8,128)(2,1)} %param.6) | data formatting | bytes 16777216 | tf_op args[2]
  165.8 11.3 %convert_element_type.2 = f32[1024,4096]{0,1:T(8,128)} convert(bf16[1024,4096]{0,1:T(8,128)(2,1)} %copy.11) | non-fusion elementwise | flops 4194304 | bytes 25165824 | tf_op jit(solution)/shard_map/convert_element_type | solution.py:42
  177.1 0.0 copy-start.3
  177.1 12.0 %copy.12 = f32[1024,8,4,128]{0,3,2,1:T(8,128)} copy(f32[1024,8,4,128]{0,3,1,2:T(8,128)} %bitcast.38) | data formatting | bytes 33554432 | tf_op jit(solution)/shard_map/transpose | solution.py:46
  189.1 132.6 %all-gather.5.cloned.1.call-done = f32[1024,4096]{0,1:T(8,128)} async-done(((f32[1024,512]{0,1:T(8,128)}), f32[1024,4096]{0,1:T(8,128)}) %all-gather.5.cloned.1.call-update) | async-done | bytes 16777232 | tf_op jit(solution)/shard_map/all_gather | solution.py:39
  321.7 0.0 copy-done.3
  321.7 0.0 copy-start
  321.7 10.5 %fusion = (f32[1024]{0:T(1024)S(1)}, f32[1024]{0:T(1024)S(1)}) fusion(f32[1024,4096]{0,1:T(8,128)} %all-gather.5.cloned.1.call-done, s32[1024]{0:T(1024)S(1)} %copy-done.3, s32[4096]{0:T(1024)S(1)} %fusion.25, bf16[1024,4096]{0,1:T(8,128)(2,1)} %copy.11), kind=kLoop, calls=%fused_computation.2 | loop fusion | flops 33552384 | bytes 25194496 | tf_op jit(solution)/shard_map/reduce_sum | solution.py:51
  332.2 2.5 copy-done
  334.7 7.6 %fusion.4 = f32[1024]{0:T(1024)S(1)} fusion(f32[1024,8,4,128]{0,3,2,1:T(8,128)} %copy.12, f32[1024]{0:T(1024)S(1)} %get-tuple-element.3, f32[1024,4096]{0,1:T(8,128)S(1)} %copy-done, f32[1024]{0:T(1024)S(1)} %get-tuple-element.2), kind=kLoop, calls=%fused_computation.9 | loop fusion | flops 20970496 | bytes 33566720 | tf_op jit(solution)/shard_map/reduce_sum | solution.py:53
  342.3 12.9 %fusion.2 = f32[1024,4096]{0,1:T(8,128)} fusion(f32[1024]{0:T(1024)S(1)} %fusion.4, s32[1024]{0:T(1024)S(1)} %copy-done.3, s32[4096]{0:T(1024)S(1)} %fusion.25, f32[1024,8,4,128]{0,3,2,1:T(8,128)} %copy.12, f32[1024]{0:T(1024)S(1)} %get-tuple-element.3, f32[1024,4096]{0,1:T(8,128)S(1)} %copy-done, f32[1024]{0:T(1024)S(1)} %get-tuple-element.2), kind=kLoop, calls=%fused_computation.4 | loop fusion | flops 33554432 | bytes 50364416 | tf_op jit(solution)/shard_map/mul | solution.py:55
  355.2 0.0 copy-start.1
  355.2 6.8 %fusion.31 = (f32[1024,8,1,128]{0,3,2,1:T(8,128)S(1)}, f32[1024,8,1,128]{0,3,2,1:T(8,128)S(1)}, f32[1024,8,1,128]{0,3,2,1:T(8,128)S(1)}, f32[1024,8,1,128]{0,3,2,1:T(8,128)S(1)}) fusion(f32[1024,8,4,128]{0,3,2,1:T(8,128)} %bitcast.39), kind=kLoop, calls=%fused_computation.46 | loop fusion | bytes 33554432 | tf_op jit(solution)/shard_map/slice | solution.py:62
  362.0 0.0 copy-start.2
  362.0 0.0 copy-done.1
  362.0 3.5 fusion.35
  365.5 4.4 collective-permute-start.6
  369.9 0.0 copy-done.2
  369.9 0.2 collective-permute-start.3
  370.1 23.3 %collective-permute-done.6 = f32[1024,512]{1,0:T(8,128)S(1)} collective-permute-done((f32[1024,512]{1,0:T(8,128)S(1)}, f32[1024,512]{1,0:T(8,128)S(1)}, u32[]{:S(2)}, u32[]{:S(2)}) %collective-permute-start.6) | collective-permute-done | bytes 2097184 | tf_op jit(solution)/shard_map/ppermute | solution.py:15
  393.4 3.5 convolution_add_fusion
  396.9 5.6 %collective-permute-start.7 = (f32[1024,512]{1,0:T(8,128)S(1)}, f32[1024,512]{1,0:T(8,128)S(1)}, u32[]{:S(2)}, u32[]{:S(2)}) collective-permute-start(f32[1024,512]{1,0:T(8,128)S(1)} %convolution_add_fusion), channel_id=1, source_target_pairs={{8,0},{16,8},{24,16},{32,24},{40,32},{48,40},{56,48},{64,56},{72,6... | collective-permute-start | bytes 6291464 | tf_op jit(solution)/shard_map/ppermute | solution.py:15
  402.5 0.0 collective-permute-done.3
  402.5 0.0 collective-permute-start.4
  402.5 17.8 %collective-permute-done.4 = bf16[1024,512]{1,0:T(8,128)(2,1)S(1)} collective-permute-done((bf16[1024,512]{1,0:T(8,128)(2,1)S(1)}, bf16[1024,512]{1,0:T(8,128)(2,1)S(1)}, u32[]{:S(2)}, u32[]{:S(2)}) %collective-permute-start.4) | collective-permute-done | bytes 1048608 | tf_op jit(solution)/shard_map/ppermute | solution.py:15
  420.3 0.0 collective-permute-start.5
  420.3 3.5 fusion.36
  423.8 2.2 collective-permute-done.7
  426.0 0.5 add.74
  426.5 5.8 %collective-permute-start.8 = (f32[1024,512]{1,0:T(8,128)S(1)}, f32[1024,512]{1,0:T(8,128)S(1)}, u32[]{:S(2)}, u32[]{:S(2)}) collective-permute-start(f32[1024,512]{1,0:T(8,128)S(1)} %add.74), channel_id=1, source_target_pairs={{8,0},{16,8},{24,16},{32,24},{40,32},{48,40},{56,48},{64,56},{72,6... | collective-permute-start | bytes 6291464 | tf_op jit(solution)/shard_map/ppermute | solution.py:15
  432.4 3.4 fusion.37
  435.8 3.5 fusion.32
  439.3 3.5 fusion.34
  442.9 3.8 fusion.33
  446.7 0.0 collective-permute-done.5
  446.7 5.1 %add_add_fusion = f32[1024,512]{1,0:T(8,128)} fusion(f32[1024,512]{1,0:T(8,128)S(1)} %fusion.34, f32[1024,512]{1,0:T(8,128)S(1)} %fusion.32, f32[1024,512]{1,0:T(8,128)S(1)} %fusion.33, f32[1024,1024]{0,1:T(8,128)S(1)} %bitcast.41, bf16[1024,512]{1,0:T(8,128)(2,1)S(1)} %collective-permute-done.5), kind=kOutput, calls=%fused_computation.18 | convolution fusion | flops 6444023808 | bytes 13631488 | tf_op jit(solution)/shard_map/dot_general | solution.py:19
  451.9 4.1 collective-permute-done.8
  455.9 1.8 add.75
  (1 shorter events, 0.0 us)
Async XLA Ops:
  7.2 136.8 %all-gather.3.cloned.1.call-start = ((), (), s32[]{:S(2)}) async-start(), calls=%async_computation.1 | async-start | bytes 9437184 | tf_op jit(solution)/shard_map/all_gather | solution.py:29
  7.9 313.8 %all-gather.5.cloned.1.call-start = ((), (), s32[]{:S(2)}) async-start(), calls=%async_computation.2 | async-start | bytes 18874368 | tf_op jit(solution)/shard_map/all_gather | solution.py:39
  34.7 40.5 %collective-permute-start = (bf16[128,4096]{0,1:T(8,128)(2,1)S(1)}, bf16[128,4096]{0,1:T(8,128)(2,1)S(1)}, u32[]{:S(2)}, u32[]{:S(2)}) collective-permute-start(bf16[128,4096]{0,1:T(8,128)(2,1)S(1)} %bitcast.50), channel_id=1, source_target_pairs={{120,0},{0,8},{8,16},{16,24},{24,32},{32,40},{40,48},{48,56},{56,6... | collective-permute-start | bytes 3145736 | tf_op jit(solution)/shard_map/ppermute | solution.py:15
  75.2 40.4 %collective-permute-start.1 = (bf16[128,4096]{0,1:T(8,128)(2,1)S(1)}, bf16[128,4096]{0,1:T(8,128)(2,1)S(1)}, u32[]{:S(2)}, u32[]{:S(2)}) collective-permute-start(bf16[128,4096]{0,1:T(8,128)(2,1)S(1)} %collective-permute-done), channel_id=1, source_target_pairs={{120,0},{0,8},{8,16},{16,24},{24,32},{32,40},{40,48},{48,56},{56,6... | collective-permute-start | bytes 3145736 | tf_op jit(solution)/shard_map/ppermute | solution.py:15
  115.6 28.3 %collective-permute-start.2 = (bf16[128,4096]{0,1:T(8,128)(2,1)S(1)}, bf16[128,4096]{0,1:T(8,128)(2,1)}, u32[]{:S(2)}, u32[]{:S(2)}) collective-permute-start(bf16[128,4096]{0,1:T(8,128)(2,1)S(1)} %collective-permute-done.1), channel_id=1, source_target_pairs={{120,0},{0,8},{8,16},{16,24},{24,32},{32,40},{40,48},{48,56},{56,6... | collective-permute-start | bytes 3145736 | tf_op jit(solution)/shard_map/ppermute | solution.py:15
  177.1 144.6 %copy-start.3 = (s32[1024]{0:T(1024)S(1)}, s32[1024]{0:T(1024)}, u32[]{:S(2)}) copy-start(s32[1024]{0:T(1024)} %param.7) | copy-start | bytes 12292
  321.7 13.0 %copy-start = (f32[1024,4096]{0,1:T(8,128)S(1)}, f32[1024,4096]{0,1:T(8,128)}, u32[]{:S(2)}) copy-start(f32[1024,4096]{0,1:T(8,128)} %all-gather.5.cloned.1.call-done) | copy-start | bytes 50331652
  355.2 6.8 %copy-start.1 = (bf16[1024,512]{1,0:T(8,128)(2,1)S(1)}, bf16[1024,512]{1,0:T(8,128)(2,1)}, u32[]{:S(2)}) copy-start(bf16[1024,512]{1,0:T(8,128)(2,1)} %param.4) | copy-start | bytes 3145732
  362.0 7.9 %copy-start.2 = (bf16[1024,512]{1,0:T(8,128)(2,1)S(1)}, bf16[1024,512]{1,0:T(8,128)(2,1)}, u32[]{:S(2)}) copy-start(bf16[1024,512]{1,0:T(8,128)(2,1)} %param.5) | copy-start | bytes 3145732
  365.5 28.0 %collective-permute-start.6 = (f32[1024,512]{1,0:T(8,128)S(1)}, f32[1024,512]{1,0:T(8,128)S(1)}, u32[]{:S(2)}, u32[]{:S(2)}) collective-permute-start(f32[1024,512]{1,0:T(8,128)S(1)} %fusion.35), channel_id=1, source_target_pairs={{8,0},{16,8},{24,16},{32,24},{40,32},{48,40},{56,48},{64,56},{72,6... | collective-permute-start | bytes 6291464 | tf_op jit(solution)/shard_map/ppermute | solution.py:15
  369.9 32.6 %collective-permute-start.3 = (bf16[1024,512]{1,0:T(8,128)(2,1)S(1)}, bf16[1024,512]{1,0:T(8,128)(2,1)S(1)}, u32[]{:S(2)}, u32[]{:S(2)}) collective-permute-start(bf16[1024,512]{1,0:T(8,128)(2,1)S(1)} %copy-done.2), channel_id=1, source_target_pairs={{120,0},{0,8},{8,16},{16,24},{24,32},{32,40},{40,48},{48,56},{56,6... | collective-permute-start | bytes 3145736 | tf_op jit(solution)/shard_map/ppermute | solution.py:15
  396.9 29.1 %collective-permute-start.7 = (f32[1024,512]{1,0:T(8,128)S(1)}, f32[1024,512]{1,0:T(8,128)S(1)}, u32[]{:S(2)}, u32[]{:S(2)}) collective-permute-start(f32[1024,512]{1,0:T(8,128)S(1)} %convolution_add_fusion), channel_id=1, source_target_pairs={{8,0},{16,8},{24,16},{32,24},{40,32},{48,40},{56,48},{64,56},{72,6... | collective-permute-start | bytes 6291464 | tf_op jit(solution)/shard_map/ppermute | solution.py:15
  402.5 17.8 %collective-permute-start.4 = (bf16[1024,512]{1,0:T(8,128)(2,1)S(1)}, bf16[1024,512]{1,0:T(8,128)(2,1)S(1)}, u32[]{:S(2)}, u32[]{:S(2)}) collective-permute-start(bf16[1024,512]{1,0:T(8,128)(2,1)S(1)} %collective-permute-done.3), channel_id=1, source_target_pairs={{120,0},{0,8},{8,16},{16,24},{24,32},{32,40},{40,48},{48,56},{56,6... | collective-permute-start | bytes 3145736 | tf_op jit(solution)/shard_map/ppermute | solution.py:15
  420.3 26.4 %collective-permute-start.5 = (bf16[1024,512]{1,0:T(8,128)(2,1)S(1)}, bf16[1024,512]{1,0:T(8,128)(2,1)S(1)}, u32[]{:S(2)}, u32[]{:S(2)}) collective-permute-start(bf16[1024,512]{1,0:T(8,128)(2,1)S(1)} %collective-permute-done.4), channel_id=1, source_target_pairs={{120,0},{0,8},{8,16},{16,24},{24,32},{32,40},{40,48},{48,56},{56,6... | collective-permute-start | bytes 3145736 | tf_op jit(solution)/shard_map/ppermute | solution.py:15
  426.5 29.4 %collective-permute-start.8 = (f32[1024,512]{1,0:T(8,128)S(1)}, f32[1024,512]{1,0:T(8,128)S(1)}, u32[]{:S(2)}, u32[]{:S(2)}) collective-permute-start(f32[1024,512]{1,0:T(8,128)S(1)} %add.74), channel_id=1, source_target_pairs={{8,0},{16,8},{24,16},{32,24},{40,32},{48,40},{56,48},{64,56},{72,6... | collective-permute-start | bytes 6291464 | tf_op jit(solution)/shard_map/ppermute | solution.py:15
Sparse Core Ops, SparseCore 0:
  9.6 98.8 all-gather.2
  153.7 167.9 all-gather.4

commit v6 on v2

--- a/solution.py
+++ b/solution.py
@@ -15,6 +15,11 @@
     return lax.ppermute(block, axis, route)
 
 
+def after(value, dep):
+    zero = 0.0 * dep[:1, :1]
+    return value + zero.astype(value.dtype)
+
+
 def wide_dot(a, b):
     return jnp.dot(a, b, precision=lax.Precision.HIGHEST, preferred_element_type=jnp.float32)
 
@@ -29,10 +34,13 @@
     q_full = lax.all_gather(queries, "width", axis=1, tiled=True)
     p_cols = lax.all_to_all(passages, "width", 0, 1, tiled=True)
     held_cols = [p_cols]
-    held = [passages]
     for step in range(1, STEPS):
         held_cols.append(shifted(held_cols[-1], "loop", 1))
-        held.append(shifted(held[-1], "loop", 1))
+    held = [passages]
+    current = after(passages, q_full)
+    for step in range(1, STEPS):
+        current = shifted(current, "loop", 1)
+        held.append(current)
 
     cols = jnp.concatenate(held_cols, 0)
     scores = SCALE * jnp.einsum("qd,cd->qc", q_full, cols, preferred_element_type=jnp.float32)
@@ -60,7 +68,7 @@
     errors = (s_pos - scores) - (t_pos - teach_cols)
     slopes_cols = coef * (hit.astype(jnp.float32) * total - errors)
 
-    slopes = lax.all_gather(slopes_cols, "width", axis=1, tiled=True)
+    slopes = lax.all_gather(after(slopes_cols, held[-1]), "width", axis=1, tiled=True)
     slopes = slopes.reshape(rows, width, STEPS, sub)
 
     query_wide = queries.astype(jnp.float32)

time: 458 us -> 507 us (1.11)
  waiting for transfers between devices: 277 us -> 316 us
    all_gather x1, waiting for transfers between devices: 0.01 us -> 33.2 us  [per_device(): q_full = lax.all_gather(queries, 'width', axis=1, tiled=True)]
    unnamed x12 -> x14, local copies, waits for them, and re-layouts: 20 us -> 20 us
  transfers between devices with their start and end apart: 11 -> 11, of which waited for: 8 -> 8; matrix products, arithmetic and copies ran while one was open for 16% -> 17% of each run, Pallas kernels for 0% -> 0%
where the time goes in v6:
time: 507 us; the launch traced here: 499 us
  waiting for transfers between devices  316 us (62%)
  matrix products  42.4 us (8%)
  blocking collectives  42.3 us (8%)
  local copies, waits for them, and re-layouts  39 us (8%)
  other arithmetic  24.8 us (5%)
  starting transfers between devices  18.9 us (4%)
  between operations  15.9 us (3%)
    all_gather x1, waiting for transfers between devices, per_device(): lax.all_gather(after(slopes_cols, held[-1]), 'width', axis=1, tiled=True)  168 us
    ppermute x9, waiting for transfers between devices, shifted(): return lax.ppermute(block, axis, route)  114 us
    dot_general x8, matrix products, wide_dot(): jnp.dot(a, b, precision=lax.Precision.HIGHEST, preferred_element_type=jnp...  33.5 us
    all_gather x1, waiting for transfers between devices, per_device(): q_full = lax.all_gather(queries, 'width', axis=1, tiled=True)  33.2 us
    all_to_all x1, blocking collectives, per_device(): p_cols = lax.all_to_all(passages, 'width', 0, 1, tiled=True)  26.1 us
    unnamed x14, local copies, waits for them, and re-layouts  20 us
    ppermute x9, starting transfers between devices, shifted(): return lax.ppermute(block, axis, route)  18.8 us
    psum x1, blocking collectives, per_device(): stats = lax.psum(jnp.stack([pos_part, row_part], 0), 'width')  16.2 us
  transfers between devices with their start and end apart: 11, of which 8 were waited for; matrix products, arithmetic and copies ran while one was open for 17% of the time, Pallas kernels for 0%

profile of v6, /device:TPU:0, one launch (start us, length us, event | category | flops | bytes accessed | tf_op | source)
XLA Modules:
  0.0 498.9 jit_solution(6046526519442271374)
XLA Ops:
  7.2 0.0 copy-start.2
  7.2 0.0 all-gather.3.cloned.1.call-start
  7.2 0.7 all-gather.3.cloned.1.call-update
  7.9 0.0 all-gather.5.cloned.1.call-start
  8.0 26.1 %all_to_all.19 = bf16[8,128,512]{2,1,0:T(8,128)(2,1)S(1)} all-to-all(bf16[8,128,512]{2,1,0:T(8,128)(2,1)} %bitcast.57), channel_id=1, replica_groups=mesh['loop'=16,'width'=8] {'width'}, dimensions={0} | all-to-all | bytes 2097152 | tf_op jit(solution)/shard_map/all_to_all | solution.py:35
  34.1 0.7 copy.8
  34.7 0.0 copy-start.3
  34.7 0.1 collective-permute-start
  34.8 40.5 %collective-permute-done = bf16[128,4096]{0,1:T(8,128)(2,1)} collective-permute-done((bf16[128,4096]{0,1:T(8,128)(2,1)S(1)}, bf16[128,4096]{0,1:T(8,128)(2,1)}, u32[]{:S(2)}, u32[]{:S(2)}) %collective-permute-start) | collective-permute-done | bytes 1048608 | tf_op jit(solution)/shard_map/ppermute | solution.py:15
  75.3 0.0 collective-permute-start.1
  75.4 33.2 %all-gather.3.cloned.1.call-done = bf16[1024,4096]{1,0:T(8,128)(2,1)} async-done(((bf16[1024,512]{1,0:T(8,128)(2,1)}), bf16[1024,4096]{1,0:T(8,128)(2,1)}) %all-gather.3.cloned.1.call-update) | async-done | bytes 8388624 | tf_op jit(solution)/shard_map/all_gather | solution.py:34
  108.5 1.1 slice.34
  110.3 0.0 copy-done.2
  110.3 0.1 broadcast_add_fusion
  110.4 0.1 collective-permute-start.3
  110.5 11.4 %convert_bitcast_fusion = f32[128,8,32,128]{3,1,2,0:T(8,128)} fusion(bf16[1024,4096]{1,0:T(8,128)(2,1)} %param.6), kind=kLoop, calls=%fused_computation | loop fusion | flops 4194304 | bytes 25165824
  121.9 0.0 copy-done.3
  121.9 14.1 %copy.11 = f32[128,8,32,128]{3,2,1,0:T(8,128)} copy(f32[128,8,32,128]{3,1,2,0:T(8,128)} %convert_bitcast_fusion) | data formatting | bytes 33554432
  136.0 0.0 collective-permute-done.1
  136.0 2.3 collective-permute-start.2
  138.2 13.4 %collective-permute-done.3 = bf16[1024,512]{1,0:T(8,128)(2,1)} collective-permute-done((bf16[1024,512]{1,0:T(8,128)(2,1)S(1)}, bf16[1024,512]{1,0:T(8,128)(2,1)}, u32[]{:S(2)}, u32[]{:S(2)}) %collective-permute-start.3) | collective-permute-done | bytes 1048608 | tf_op jit(solution)/shard_map/ppermute | solution.py:15
  151.7 0.0 collective-permute-start.4
  151.7 0.0 copy-start.5
  151.7 9.2 %constant_dynamic-slice_fusion = f32[1024,4,1,128]{3,2,1,0:T(1,128)} fusion(f32[1024,4,8,128]{3,2,1,0:T(8,128)} %bitcast.49, s32[]{:T(128)S(6)} %select_n.37), kind=kLoop, calls=%fused_computation.42 | loop fusion | bytes 4194308 | tf_op jit(solution)/shard_map/dynamic_slice | solution.py:57
  160.9 4.6 copy.10
  165.5 0.0 copy-done.5
  165.5 0.0 copy-start.4
  165.5 6.9 %convert_reduce_fusion = (f32[1024]{0:T(1024)S(1)}, f32[1024]{0:T(1024)S(1)}) fusion(bf16[1024,4096]{1,0:T(8,128)(2,1)} %param.6, s32[1024]{0:T(1024)S(1)} %copy-done.5), kind=kLoop, calls=%fused_computation.1 | loop fusion | flops 20969472 | bytes 8400896 | tf_op jit(solution)/shard_map/reduce_sum | solution.py:52
  172.4 16.2 %collective-permute-done.4 = bf16[1024,512]{1,0:T(8,128)(2,1)} collective-permute-done((bf16[1024,512]{1,0:T(8,128)(2,1)}, bf16[1024,512]{1,0:T(8,128)(2,1)}, u32[]{:S(2)}, u32[]{:S(2)}) %collective-permute-start.4) | collective-permute-done | bytes 1048608 | tf_op jit(solution)/shard_map/ppermute | solution.py:15
  188.6 0.2 collective-permute-start.5
  188.8 0.0 collective-permute-done.2
  188.8 0.0 copy-done.4
  188.8 8.9 %multiply_reduce_fusion = (f32[1024]{0:T(1024)S(1)}, f32[512,1024]{1,0:T(8,128)S(1)}) fusion(bf16[1024,4096]{1,0:T(8,128)(2,1)} %all-gather.3.cloned.1.call-done, bf16[128,4096]{0,1:T(8,128)(2,1)} %collective-permute-done.2, bf16[128,4096]{0,1:T(8,128)(2,1)} %collective-permute-done.1, bf16[128,4096]{0,1:T(8,128)(2,1)} %collective-permute-done, ...), kind=kOutput, calls=%fused_computation.23 | convolution fusion | flops 4312792064 | bytes 14684160 | tf_op jit(solution)/shard_map/qd,cd->qc/dot_general | solution.py:46
  197.8 0.0 copy-start.1
  197.8 1.3 copy-done.1
  199.1 0.3 fusion.9
  199.5 16.2 %psum.7 = f32[2,1024]{1,0:T(2,128)S(1)} all-reduce(f32[2,1024]{1,0:T(2,128)S(1)} %pad_maximum_fusion), channel_id=1, replica_groups=mesh['loop'=16,'width'=8] {'width'}, use_global_device_ids=true, to_apply=%region_2.3 | all-reduce | flops 2048 | bytes 16384 | tf_op jit(solution)/shard_map/psum | solution.py:63
  215.7 0.0 collective-permute-done.5
  215.7 1.2 slice.35
  217.6 3.8 fusion.12
  221.4 0.0 all-gather.5.cloned.1.call-update
  221.4 167.5 %all-gather.5.cloned.1.call-done = f32[1024,4096]{0,1:T(8,128)} async-done(((f32[1024,512]{0,1:T(8,128)}), f32[1024,4096]{0,1:T(8,128)}) %all-gather.5.cloned.1.call-update) | async-done | bytes 16777232 | tf_op jit(solution)/shard_map/all_gather | solution.py:71
  388.9 0.0 copy-start
  388.9 6.8 %fusion.25 = (f32[1024,8,1,128]{0,3,2,1:T(8,128)S(1)}, f32[1024,8,1,128]{0,3,2,1:T(8,128)S(1)}, f32[1024,8,1,128]{0,3,2,1:T(8,128)S(1)}, f32[1024,8,1,128]{0,3,2,1:T(8,128)S(1)}) fusion(f32[1024,8,4,128]{0,3,2,1:T(8,128)} %bitcast.50), kind=kLoop, calls=%fused_computation.44 | loop fusion | bytes 33554432 | tf_op jit(solution)/shard_map/slice | solution.py:78
  395.7 0.0 copy-done
  395.7 3.4 fusion.30
  399.2 4.8 collective-permute-start.6
  404.0 23.6 %collective-permute-done.6 = f32[1024,512]{1,0:T(8,128)S(1)} collective-permute-done((f32[1024,512]{1,0:T(8,128)S(1)}, f32[1024,512]{1,0:T(8,128)S(1)}, u32[]{:S(2)}, u32[]{:S(2)}) %collective-permute-start.6) | collective-permute-done | bytes 2097184 | tf_op jit(solution)/shard_map/ppermute | solution.py:15
  427.6 3.5 convolution_add_fusion
  431.1 5.6 %collective-permute-start.7 = (f32[1024,512]{1,0:T(8,128)S(1)}, f32[1024,512]{1,0:T(8,128)S(1)}, u32[]{:S(2)}, u32[]{:S(2)}) collective-permute-start(f32[1024,512]{1,0:T(8,128)S(1)} %convolution_add_fusion), channel_id=1, source_target_pairs={{8,0},{16,8},{24,16},{32,24},{40,32},{48,40},{56,48},{64,56},{72,6... | collective-permute-start | bytes 6291464 | tf_op jit(solution)/shard_map/ppermute | solution.py:15
  436.7 3.5 fusion.31
  440.1 20.1 %collective-permute-done.7 = f32[1024,512]{1,0:T(8,128)S(1)} collective-permute-done((f32[1024,512]{1,0:T(8,128)S(1)}, f32[1024,512]{1,0:T(8,128)S(1)}, u32[]{:S(2)}, u32[]{:S(2)}) %collective-permute-start.7) | collective-permute-done | bytes 2097184 | tf_op jit(solution)/shard_map/ppermute | solution.py:15
  460.2 0.5 add.107
  460.7 5.8 %collective-permute-start.8 = (f32[1024,512]{1,0:T(8,128)S(1)}, f32[1024,512]{1,0:T(8,128)S(1)}, u32[]{:S(2)}, u32[]{:S(2)}) collective-permute-start(f32[1024,512]{1,0:T(8,128)S(1)} %add.107), channel_id=1, source_target_pairs={{8,0},{16,8},{24,16},{32,24},{40,32},{48,40},{56,48},{64,56},{72,6... | collective-permute-start | bytes 6291464 | tf_op jit(solution)/shard_map/ppermute | solution.py:15
  466.5 3.5 fusion.27
  470.0 3.4 fusion.32
  473.4 4.7 fusion.29
  478.2 5.0 fusion.28
  483.2 6.4 %add_add_fusion = f32[1024,512]{1,0:T(8,128)} fusion(f32[1024,512]{1,0:T(8,128)S(1)} %fusion.29, f32[1024,512]{1,0:T(8,128)S(1)} %fusion.27, f32[1024,512]{1,0:T(8,128)S(1)} %fusion.28, f32[1024,1024]{0,1:T(8,128)S(1)} %bitcast.48, bf16[1024,512]{1,0:T(8,128)(2,1)} %collective-permute-done.5), kind=kOutput, calls=%fused_computation.22 | convolution fusion | flops 6444023808 | bytes 13631488 | tf_op jit(solution)/shard_map/dot_general | solution.py:24
  489.6 0.5 collective-permute-done.8
  490.0 1.8 add.108
  (4 shorter events, 0.0 us)
Async XLA Ops:
  7.2 103.1 %copy-start.2 = (bf16[1024,512]{1,0:T(8,128)(2,1)S(1)}, bf16[1024,512]{1,0:T(8,128)(2,1)}, u32[]{:S(2)}) copy-start(bf16[1024,512]{1,0:T(8,128)(2,1)} %param.5) | copy-start | bytes 3145732
  7.2 101.3 %all-gather.3.cloned.1.call-start = ((), (), s32[]{:S(2)}) async-start(), calls=%async_computation.1 | async-start | bytes 9437184 | tf_op jit(solution)/shard_map/all_gather | solution.py:34
  7.9 381.0 %all-gather.5.cloned.1.call-start = ((), (), s32[]{:S(2)}) async-start(), calls=%async_computation.2 | async-start | bytes 18874368 | tf_op jit(solution)/shard_map/all_gather | solution.py:71
  34.7 87.1 %copy-start.3 = (bf16[128,8,512]{0,2,1:T(8,128)(2,1)}, bf16[128,8,512]{0,2,1:T(8,128)(2,1)S(1)}, u32[]{:S(2)}) copy-start(bf16[128,8,512]{0,2,1:T(8,128)(2,1)S(1)} %copy.8) | copy-start | bytes 3145732
  34.7 40.6 %collective-permute-start = (bf16[128,4096]{0,1:T(8,128)(2,1)S(1)}, bf16[128,4096]{0,1:T(8,128)(2,1)}, u32[]{:S(2)}, u32[]{:S(2)}) collective-permute-start(bf16[128,4096]{0,1:T(8,128)(2,1)S(1)} %bitcast.59), channel_id=1, source_target_pairs={{120,0},{0,8},{8,16},{16,24},{24,32},{32,40},{40,48},{48,56},{56,6... | collective-permute-start | bytes 3145736 | tf_op jit(solution)/shard_map/ppermute | solution.py:15
  75.3 60.6 %collective-permute-start.1 = (bf16[128,4096]{0,1:T(8,128)(2,1)}, bf16[128,4096]{0,1:T(8,128)(2,1)}, u32[]{:S(2)}, u32[]{:S(2)}) collective-permute-start(bf16[128,4096]{0,1:T(8,128)(2,1)} %collective-permute-done), channel_id=1, source_target_pairs={{120,0},{0,8},{8,16},{16,24},{24,32},{32,40},{40,48},{48,56},{56,6... | collective-permute-start | bytes 3145736 | tf_op jit(solution)/shard_map/ppermute | solution.py:15
  110.4 41.3 %collective-permute-start.3 = (bf16[1024,512]{1,0:T(8,128)(2,1)S(1)}, bf16[1024,512]{1,0:T(8,128)(2,1)}, u32[]{:S(2)}, u32[]{:S(2)}) collective-permute-start(bf16[1024,512]{1,0:T(8,128)(2,1)S(1)} %broadcast_add_fusion), channel_id=1, source_target_pairs={{120,0},{0,8},{8,16},{16,24},{24,32},{32,40},{40,48},{48,56},{56,6... | collective-permute-start | bytes 3145736 | tf_op jit(solution)/shard_map/ppermute | solution.py:15
  136.0 52.8 %collective-permute-start.2 = (bf16[128,4096]{0,1:T(8,128)(2,1)}, bf16[128,4096]{0,1:T(8,128)(2,1)}, u32[]{:S(2)}, u32[]{:S(2)}) collective-permute-start(bf16[128,4096]{0,1:T(8,128)(2,1)} %collective-permute-done.1), channel_id=1, source_target_pairs={{120,0},{0,8},{8,16},{16,24},{24,32},{32,40},{40,48},{48,56},{56,6... | collective-permute-start | bytes 3145736 | tf_op jit(solution)/shard_map/ppermute | solution.py:15
  151.7 36.9 %collective-permute-start.4 = (bf16[1024,512]{1,0:T(8,128)(2,1)}, bf16[1024,512]{1,0:T(8,128)(2,1)}, u32[]{:S(2)}, u32[]{:S(2)}) collective-permute-start(bf16[1024,512]{1,0:T(8,128)(2,1)} %collective-permute-done.3), channel_id=1, source_target_pairs={{120,0},{0,8},{8,16},{16,24},{24,32},{32,40},{40,48},{48,56},{56,6... | collective-permute-start | bytes 3145736 | tf_op jit(solution)/shard_map/ppermute | solution.py:15
  151.7 13.8 %copy-start.5 = (s32[1024]{0:T(1024)S(1)}, s32[1024]{0:T(1024)}, u32[]{:S(2)}) copy-start(s32[1024]{0:T(1024)} %param.7) | copy-start | bytes 12292
  165.5 23.3 %copy-start.4 = (bf16[128,8,512]{0,2,1:T(8,128)(2,1)S(1)}, bf16[128,8,512]{0,2,1:T(8,128)(2,1)}, u32[]{:S(2)}) copy-start(bf16[128,8,512]{0,2,1:T(8,128)(2,1)} %copy-done.3) | copy-start | bytes 3145732
  188.6 27.1 %collective-permute-start.5 = (bf16[1024,512]{1,0:T(8,128)(2,1)}, bf16[1024,512]{1,0:T(8,128)(2,1)}, u32[]{:S(2)}, u32[]{:S(2)}) collective-permute-start(bf16[1024,512]{1,0:T(8,128)(2,1)} %collective-permute-done.4), channel_id=1, source_target_pairs={{120,0},{0,8},{8,16},{16,24},{24,32},{32,40},{40,48},{48,56},{56,6... | collective-permute-start | bytes 3145736 | tf_op jit(solution)/shard_map/ppermute | solution.py:15
  197.8 1.3 copy-start.1
  388.9 6.8 %copy-start = (bf16[1024,512]{1,0:T(8,128)(2,1)S(1)}, bf16[1024,512]{1,0:T(8,128)(2,1)}, u32[]{:S(2)}) copy-start(bf16[1024,512]{1,0:T(8,128)(2,1)} %param.4) | copy-start | bytes 3145732
  399.2 28.4 %collective-permute-start.6 = (f32[1024,512]{1,0:T(8,128)S(1)}, f32[1024,512]{1,0:T(8,128)S(1)}, u32[]{:S(2)}, u32[]{:S(2)}) collective-permute-start(f32[1024,512]{1,0:T(8,128)S(1)} %fusion.30), channel_id=1, source_target_pairs={{8,0},{16,8},{24,16},{32,24},{40,32},{48,40},{56,48},{64,56},{72,6... | collective-permute-start | bytes 6291464 | tf_op jit(solution)/shard_map/ppermute | solution.py:15
  431.1 29.1 %collective-permute-start.7 = (f32[1024,512]{1,0:T(8,128)S(1)}, f32[1024,512]{1,0:T(8,128)S(1)}, u32[]{:S(2)}, u32[]{:S(2)}) collective-permute-start(f32[1024,512]{1,0:T(8,128)S(1)} %convolution_add_fusion), channel_id=1, source_target_pairs={{8,0},{16,8},{24,16},{32,24},{40,32},{48,40},{56,48},{64,56},{72,6... | collective-permute-start | bytes 6291464 | tf_op jit(solution)/shard_map/ppermute | solution.py:15
  460.7 29.3 %collective-permute-start.8 = (f32[1024,512]{1,0:T(8,128)S(1)}, f32[1024,512]{1,0:T(8,128)S(1)}, u32[]{:S(2)}, u32[]{:S(2)}) collective-permute-start(f32[1024,512]{1,0:T(8,128)S(1)} %add.107), channel_id=1, source_target_pairs={{8,0},{16,8},{24,16},{32,24},{40,32},{48,40},{56,48},{64,56},{72,6... | collective-permute-start | bytes 6291464 | tf_op jit(solution)/shard_map/ppermute | solution.py:15
Sparse Core Ops, SparseCore 0:
  9.6 98.8 all-gather.2
  221.5 167.3 all-gather.4

commit v7 on v2

--- a/solution.py
+++ b/solution.py
@@ -13,6 +13,11 @@
     devices = range(lax.axis_size(axis))
     route = [((i - distance) % len(devices), i) for i in devices]
     return lax.ppermute(block, axis, route)
+
+
+def after(value, dep):
+    zero = 0.0 * dep[:1, :1]
+    return value + zero.astype(value.dtype)
 
 
 def wide_dot(a, b):
@@ -71,9 +76,15 @@
         gq = wide_dot(block_slopes, held[k].astype(jnp.float32))
         grad_q = gq if grad_q is None else grad_q + gq
         terms.append(wide_dot(block_slopes.T, query_wide))
-    grad_p = terms[STEPS - 1]
+    half = terms[0].shape[1] // 2
+    lead = terms[STEPS - 1][:, :half]
+    trail = terms[STEPS - 1][:, half:]
     for k in range(STEPS - 2, -1, -1):
-        grad_p = shifted(grad_p, "loop", -1) + terms[k]
+        lead = shifted(lead, "loop", -1)
+        trail = shifted(after(trail, lead), "loop", -1)
+        lead = lead + terms[k][:, :half]
+        trail = trail + terms[k][:, half:]
+    grad_p = jnp.concatenate([lead, trail], 1)
     return (grad_q, grad_p)
 
 

time: 458 us -> 461 us (level)
  waiting for transfers between devices: 277 us -> 257 us
  starting transfers between devices: 16.3 us -> 34.2 us
    ppermute x9 -> x12, waiting for transfers between devices: 110 us -> 90.9 us  [shifted(): return lax.ppermute(block, axis, route)]
    ppermute x9 -> x12, starting transfers between devices: 16.2 us -> 34.1 us  [shifted(): return lax.ppermute(block, axis, route)]
    unnamed x12 -> x16, local copies, waits for them, and re-layouts: 20 us -> 20 us
  transfers between devices with their start and end apart: 11 -> 14, of which waited for: 8 -> 9; matrix products, arithmetic and copies ran while one was open for 16% -> 19% of each run, Pallas kernels for 0% -> 0%
where the time goes in v7:
time: 461 us; the launch traced here: 456 us
  waiting for transfers between devices  257 us (56%)
  blocking collectives  46 us (10%)
  local copies, waits for them, and re-layouts  38.4 us (8%)
  matrix products  38.2 us (8%)
  starting transfers between devices  34.2 us (7%)
  other arithmetic  25.6 us (6%)
  between operations  16.5 us (4%)
    all_gather x1, waiting for transfers between devices, per_device(): slopes = lax.all_gather(slopes_cols, 'width', axis=1, tiled=True)  166 us
    ppermute x12, waiting for transfers between devices, shifted(): return lax.ppermute(block, axis, route)  90.9 us
    ppermute x12, starting transfers between devices, shifted(): return lax.ppermute(block, axis, route)  34.1 us
    dot_general x8, matrix products, wide_dot(): jnp.dot(a, b, precision=lax.Precision.HIGHEST, preferred_element_type=jnp...  29.3 us
    all_to_all x1, blocking collectives, per_device(): p_cols = lax.all_to_all(passages, 'width', 0, 1, tiled=True)  26.1 us
    unnamed x16, local copies, waits for them, and re-layouts  20 us
    psum x1, blocking collectives, per_device(): stats = lax.psum(jnp.stack([pos_part, row_part], 0), 'width')  19.9 us
    unnamed x1, other arithmetic  11.8 us
  transfers between devices with their start and end apart: 14, of which 9 were waited for; matrix products, arithmetic and copies ran while one was open for 19% of the time, Pallas kernels for 0%

profile of v7, /device:TPU:0, one launch (start us, length us, event | category | flops | bytes accessed | tf_op | source)
XLA Modules:
  0.0 456.0 jit_solution(5271595481085254808)
XLA Ops:
  7.2 0.0 all-gather.3.cloned.1.call-start
  7.2 0.7 all-gather.3.cloned.1.call-update
  7.9 0.0 all-gather.5.cloned.1.call-start
  7.9 26.1 %all_to_all.19 = bf16[8,128,512]{2,1,0:T(8,128)(2,1)S(1)} all-to-all(bf16[8,128,512]{2,1,0:T(8,128)(2,1)} %bitcast.58), channel_id=1, replica_groups=mesh['loop'=16,'width'=8] {'width'}, dimensions={0} | all-to-all | bytes 2097152 | tf_op jit(solution)/shard_map/all_to_all | solution.py:35
  34.1 0.7 copy.12
  34.7 0.1 collective-permute-start
  34.8 40.4 %collective-permute-done = bf16[128,4096]{0,1:T(8,128)(2,1)S(1)} collective-permute-done((bf16[128,4096]{0,1:T(8,128)(2,1)S(1)}, bf16[128,4096]{0,1:T(8,128)(2,1)S(1)}, u32[]{:S(2)}, u32[]{:S(2)}) %collective-permute-start) | collective-permute-done | bytes 1048608 | tf_op jit(solution)/shard_map/ppermute | solution.py:15
  75.2 0.0 collective-permute-start.1
  75.2 11.8 %convert_bitcast_fusion = f32[128,8,32,128]{3,1,2,0:T(8,128)} fusion(bf16[1024,4096]{1,0:T(8,128)(2,1)} %param.6), kind=kLoop, calls=%fused_computation | loop fusion | flops 4194304 | bytes 25165824
  87.0 14.1 %copy.18 = f32[128,8,32,128]{3,2,1,0:T(8,128)} copy(f32[128,8,32,128]{3,1,2,0:T(8,128)} %convert_bitcast_fusion) | data formatting | bytes 33554432
  101.2 14.6 %collective-permute-done.1 = bf16[128,4096]{0,1:T(8,128)(2,1)} collective-permute-done((bf16[128,4096]{0,1:T(8,128)(2,1)S(1)}, bf16[128,4096]{0,1:T(8,128)(2,1)}, u32[]{:S(2)}, u32[]{:S(2)}) %collective-permute-start.1) | collective-permute-done | bytes 1048608 | tf_op jit(solution)/shard_map/ppermute | solution.py:15
  115.8 0.2 collective-permute-start.2
  115.9 0.0 copy-start.3
  115.9 9.2 %constant_dynamic-slice_fusion = f32[1024,4,1,128]{3,2,1,0:T(1,128)} fusion(f32[1024,4,8,128]{3,2,1,0:T(8,128)} %bitcast.49, s32[]{:T(128)S(6)} %select_n.37), kind=kLoop, calls=%fused_computation.49 | loop fusion | bytes 4194308 | tf_op jit(solution)/shard_map/dynamic_slice | solution.py:54
  125.2 4.6 %copy.17 = f32[1024,4,1,128]{0,3,1,2:T(8,128)S(1)} copy(f32[1024,4,1,128]{3,2,1,0:T(1,128)} %constant_dynamic-slice_fusion) | data formatting | bytes 4194304
  129.8 6.8 %convert_reduce_fusion = (f32[1024]{0:T(1024)S(1)}, f32[1024]{0:T(1024)S(1)}) fusion(bf16[1024,4096]{1,0:T(8,128)(2,1)} %param.6, s32[1024]{0:T(1024)S(1)} %copy-done.3), kind=kLoop, calls=%fused_computation.1 | loop fusion | flops 20969472 | bytes 8400896 | tf_op jit(solution)/shard_map/reduce_sum | solution.py:49
  136.6 7.4 %collective-permute-done.2 = bf16[128,4096]{0,1:T(8,128)(2,1)} collective-permute-done((bf16[128,4096]{0,1:T(8,128)(2,1)}, bf16[128,4096]{0,1:T(8,128)(2,1)}, u32[]{:S(2)}, u32[]{:S(2)}) %collective-permute-start.2) | collective-permute-done | bytes 1048608 | tf_op jit(solution)/shard_map/ppermute | solution.py:15
  144.0 8.9 %multiply_reduce_fusion = (f32[1024]{0:T(1024)S(1)}, f32[512,1024]{1,0:T(8,128)S(1)}) fusion(bf16[1024,4096]{1,0:T(8,128)(2,1)} %all-gather.3.cloned.1.call-done, bf16[128,4096]{0,1:T(8,128)(2,1)} %collective-permute-done.2, bf16[128,4096]{0,1:T(8,128)(2,1)} %collective-permute-done.1, bf16[128,4096]{0,1:T(8,128)(2,1)} %copy-done.6, ...), kind=kOutput, calls=%fused_computation.23 | convolution fusion | flops 4312792064 | bytes 14684160 | tf_op jit(solution)/shard_map/qd,cd->qc/dot_general | solution.py:43
  152.9 0.0 copy-start.1
  152.9 1.3 copy-done.1
  154.2 0.3 fusion.9
  154.6 19.9 %psum.7 = f32[2,1024]{1,0:T(2,128)S(1)} all-reduce(f32[2,1024]{1,0:T(2,128)S(1)} %pad_maximum_fusion.1), channel_id=1, replica_groups=mesh['loop'=16,'width'=8] {'width'}, use_global_device_ids=true, to_apply=%region_2.3 | all-reduce | flops 2048 | bytes 16384 | tf_op jit(solution)/shard_map/psum | solution.py:60
  174.5 0.0 copy-start.2
  174.5 3.8 fusion.11
  178.3 0.0 all-gather.5.cloned.1.call-update
  178.4 0.3 collective-permute-start.3
  178.6 165.5 %all-gather.5.cloned.1.call-done = f32[1024,4096]{0,1:T(8,128)} async-done(((f32[1024,512]{0,1:T(8,128)}), f32[1024,4096]{0,1:T(8,128)}) %all-gather.5.cloned.1.call-update) | async-done | bytes 16777232 | tf_op jit(solution)/shard_map/all_gather | solution.py:68
  344.2 6.8 %fusion.26 = (f32[1024,8,1,128]{0,3,2,1:T(8,128)S(1)}, f32[1024,8,1,128]{0,3,2,1:T(8,128)S(1)}, f32[1024,8,1,128]{0,3,2,1:T(8,128)S(1)}, f32[1024,8,1,128]{0,3,2,1:T(8,128)S(1)}) fusion(f32[1024,8,4,128]{0,3,2,1:T(8,128)} %bitcast.50), kind=kLoop, calls=%fused_computation.51 | loop fusion | bytes 33554432 | tf_op jit(solution)/shard_map/slice | solution.py:75
  351.0 3.5 fusion.31
  354.5 0.1 slice.74
  354.6 10.1 %collective-permute-start.6 = (f32[1024,256]{1,0:T(8,128)S(1)}, f32[1024,256]{1,0:T(8,128)S(1)}, u32[]{:S(2)}, u32[]{:S(2)}) collective-permute-start(f32[1024,256]{1,0:T(8,128)S(1)} %slice.74), channel_id=1, source_target_pairs={{8,0},{16,8},{24,16},{32,24},{40,32},{48,40},{56,48},{64,56},{72,6... | collective-permute-start | bytes 3145736 | tf_op jit(solution)/shard_map/ppermute | solution.py:15
  364.7 0.0 collective-permute-done.3
  364.7 0.0 collective-permute-start.4
  364.7 3.5 fusion.32
  368.1 8.8 %collective-permute-done.6 = f32[1024,256]{1,0:T(8,128)S(1)} collective-permute-done((f32[1024,256]{1,0:T(8,128)S(1)}, f32[1024,256]{1,0:T(8,128)S(1)}, u32[]{:S(2)}, u32[]{:S(2)}) %collective-permute-start.6) | collective-permute-done | bytes 1048608 | tf_op jit(solution)/shard_map/ppermute | solution.py:15
  377.0 0.2 slice_add_fusion.6
  377.2 5.6 %collective-permute-start.7 = (f32[1024,256]{1,0:T(8,128)S(1)}, f32[1024,256]{1,0:T(8,128)S(1)}, u32[]{:S(2)}, u32[]{:S(2)}) collective-permute-start(f32[1024,256]{1,0:T(8,128)S(1)} %slice_add_fusion.6), channel_id=1, source_target_pairs={{8,0},{16,8},{24,16},{32,24},{40,32},{48,40},{56,48},{64,56},{72,6... | collective-permute-start | bytes 3145736 | tf_op jit(solution)/shard_map/ppermute | solution.py:15
  382.8 0.5 slice.79
  383.9 0.1 slice_add_fusion.3
  384.1 0.1 collective-permute-start.9
  384.2 0.0 collective-permute-done.4
  384.2 0.5 collective-permute-start.5
  384.7 3.5 fusion.33
  388.1 7.0 %collective-permute-done.7 = f32[1024,256]{1,0:T(8,128)S(1)} collective-permute-done((f32[1024,256]{1,0:T(8,128)S(1)}, f32[1024,256]{1,0:T(8,128)S(1)}, u32[]{:S(2)}, u32[]{:S(2)}) %collective-permute-start.7) | collective-permute-done | bytes 1048608 | tf_op jit(solution)/shard_map/ppermute | solution.py:15
  395.1 0.2 slice_add_fusion.5
  395.3 6.0 %collective-permute-start.8 = (f32[1024,256]{1,0:T(8,128)S(1)}, f32[1024,256]{1,0:T(8,128)S(1)}, u32[]{:S(2)}, u32[]{:S(2)}) collective-permute-start(f32[1024,256]{1,0:T(8,128)S(1)} %slice_add_fusion.5), channel_id=1, source_target_pairs={{8,0},{16,8},{24,16},{32,24},{40,32},{48,40},{56,48},{64,56},{72,6... | collective-permute-start | bytes 3145736 | tf_op jit(solution)/shard_map/ppermute | solution.py:15
  401.3 0.5 slice.81
  402.4 3.9 collective-permute-done.9
  406.3 0.2 fusion.14
  406.5 5.6 %collective-permute-start.10 = (f32[1024,256]{1,0:T(8,128)S(1)}, f32[1024,256]{1,0:T(8,128)S(1)}, u32[]{:S(2)}, u32[]{:S(2)}) collective-permute-start(f32[1024,256]{1,0:T(8,128)S(1)} %fusion.14), channel_id=1, source_target_pairs={{8,0},{16,8},{24,16},{32,24},{40,32},{48,40},{56,48},{64,56},{72,6... | collective-permute-start | bytes 3145736 | tf_op jit(solution)/shard_map/ppermute | solution.py:15
  412.1 3.5 fusion.28
  415.7 3.4 fusion.34
  419.1 0.0 copy-start.5
  419.1 3.5 fusion.30
  422.6 0.0 collective-permute-done.8
  422.6 0.5 slice.83
  423.8 5.0 %collective-permute-done.10 = f32[1024,256]{1,0:T(8,128)S(1)} collective-permute-done((f32[1024,256]{1,0:T(8,128)S(1)}, f32[1024,256]{1,0:T(8,128)S(1)}, u32[]{:S(2)}, u32[]{:S(2)}) %collective-permute-start.10) | collective-permute-done | bytes 1048608 | tf_op jit(solution)/shard_map/ppermute | solution.py:15
  428.8 0.2 fusion.13
  429.0 5.8 %collective-permute-start.11 = (f32[1024,256]{1,0:T(8,128)S(1)}, f32[1024,256]{1,0:T(8,128)S(1)}, u32[]{:S(2)}, u32[]{:S(2)}) collective-permute-start(f32[1024,256]{1,0:T(8,128)S(1)} %fusion.13), channel_id=1, source_target_pairs={{8,0},{16,8},{24,16},{32,24},{40,32},{48,40},{56,48},{64,56},{72,6... | collective-permute-start | bytes 3145736 | tf_op jit(solution)/shard_map/ppermute | solution.py:15
  434.8 3.5 fusion.29
  438.3 4.9 %add_add_fusion = f32[1024,512]{1,0:T(8,128)} fusion(f32[1024,512]{1,0:T(8,128)S(1)} %fusion.30, f32[1024,512]{1,0:T(8,128)S(1)} %fusion.28, f32[1024,512]{1,0:T(8,128)S(1)} %fusion.29, f32[1024,1024]{0,1:T(8,128)S(1)} %bitcast.48, bf16[1024,512]{1,0:T(8,128)(2,1)S(1)} %collective-permute-done.5), kind=kOutput, calls=%fused_computation.22 | convolution fusion | flops 6444023808 | bytes 13631488 | tf_op jit(solution)/shard_map/dot_general | solution.py:24
  443.2 3.8 collective-permute-done.11
  447.1 0.3 slice_add_fusion.4
  447.4 1.6 pad_maximum_fusion
  (15 shorter events, 0.1 us)
Async XLA Ops:
  7.2 136.8 %all-gather.3.cloned.1.call-start = ((), (), s32[]{:S(2)}) async-start(), calls=%async_computation.1 | async-start | bytes 9437184 | tf_op jit(solution)/shard_map/all_gather | solution.py:34
  7.9 336.3 %all-gather.5.cloned.1.call-start = ((), (), s32[]{:S(2)}) async-start(), calls=%async_computation.2 | async-start | bytes 18874368 | tf_op jit(solution)/shard_map/all_gather | solution.py:68
  34.7 40.5 %collective-permute-start = (bf16[128,4096]{0,1:T(8,128)(2,1)S(1)}, bf16[128,4096]{0,1:T(8,128)(2,1)S(1)}, u32[]{:S(2)}, u32[]{:S(2)}) collective-permute-start(bf16[128,4096]{0,1:T(8,128)(2,1)S(1)} %bitcast.59), channel_id=1, source_target_pairs={{120,0},{0,8},{8,16},{16,24},{24,32},{32,40},{40,48},{48,56},{56,6... | collective-permute-start | bytes 3145736 | tf_op jit(solution)/shard_map/ppermute | solution.py:15
  75.2 11.8 %copy-start.6 = (bf16[128,4096]{0,1:T(8,128)(2,1)}, bf16[128,4096]{0,1:T(8,128)(2,1)S(1)}, u32[]{:S(2)}) copy-start(bf16[128,4096]{0,1:T(8,128)(2,1)S(1)} %collective-permute-done) | copy-start | bytes 3145732
  75.2 40.5 %collective-permute-start.1 = (bf16[128,4096]{0,1:T(8,128)(2,1)S(1)}, bf16[128,4096]{0,1:T(8,128)(2,1)}, u32[]{:S(2)}, u32[]{:S(2)}) collective-permute-start(bf16[128,4096]{0,1:T(8,128)(2,1)S(1)} %collective-permute-done), channel_id=1, source_target_pairs={{120,0},{0,8},{8,16},{16,24},{24,32},{32,40},{40,48},{48,56},{56,6... | collective-permute-start | bytes 3145736 | tf_op jit(solution)/shard_map/ppermute | solution.py:15
  115.8 28.2 %collective-permute-start.2 = (bf16[128,4096]{0,1:T(8,128)(2,1)}, bf16[128,4096]{0,1:T(8,128)(2,1)}, u32[]{:S(2)}, u32[]{:S(2)}) collective-permute-start(bf16[128,4096]{0,1:T(8,128)(2,1)} %collective-permute-done.1), channel_id=1, source_target_pairs={{120,0},{0,8},{8,16},{16,24},{24,32},{32,40},{40,48},{48,56},{56,6... | collective-permute-start | bytes 3145736 | tf_op jit(solution)/shard_map/ppermute | solution.py:15
  115.9 13.8 %copy-start.3 = (s32[1024]{0:T(1024)S(1)}, s32[1024]{0:T(1024)}, u32[]{:S(2)}) copy-start(s32[1024]{0:T(1024)} %param.7) | copy-start | bytes 12292
  152.9 1.3 copy-start.1
  174.5 3.8 copy-start.2
  178.4 186.3 %collective-permute-start.3 = (bf16[1024,512]{1,0:T(8,128)(2,1)S(1)}, bf16[1024,512]{1,0:T(8,128)(2,1)S(1)}, u32[]{:S(2)}, u32[]{:S(2)}) collective-permute-start(bf16[1024,512]{1,0:T(8,128)(2,1)S(1)} %copy-done.2), channel_id=1, source_target_pairs={{120,0},{0,8},{8,16},{16,24},{24,32},{32,40},{40,48},{48,56},{56,6... | collective-permute-start | bytes 3145736 | tf_op jit(solution)/shard_map/ppermute | solution.py:15
  344.2 6.8 %copy-start = (bf16[1024,512]{1,0:T(8,128)(2,1)S(1)}, bf16[1024,512]{1,0:T(8,128)(2,1)}, u32[]{:S(2)}) copy-start(bf16[1024,512]{1,0:T(8,128)(2,1)} %param.4) | copy-start | bytes 3145732
  354.6 22.4 %collective-permute-start.6 = (f32[1024,256]{1,0:T(8,128)S(1)}, f32[1024,256]{1,0:T(8,128)S(1)}, u32[]{:S(2)}, u32[]{:S(2)}) collective-permute-start(f32[1024,256]{1,0:T(8,128)S(1)} %slice.74), channel_id=1, source_target_pairs={{8,0},{16,8},{24,16},{32,24},{40,32},{48,40},{56,48},{64,56},{72,6... | collective-permute-start | bytes 3145736 | tf_op jit(solution)/shard_map/ppermute | solution.py:15
  364.7 12.5 %copy-start.4 = (bf16[1024,512]{1,0:T(8,128)(2,1)}, bf16[1024,512]{1,0:T(8,128)(2,1)S(1)}, u32[]{:S(2)}) copy-start(bf16[1024,512]{1,0:T(8,128)(2,1)S(1)} %collective-permute-done.3) | copy-start | bytes 3145732
  364.7 19.5 %collective-permute-start.4 = (bf16[1024,512]{1,0:T(8,128)(2,1)S(1)}, bf16[1024,512]{1,0:T(8,128)(2,1)S(1)}, u32[]{:S(2)}, u32[]{:S(2)}) collective-permute-start(bf16[1024,512]{1,0:T(8,128)(2,1)S(1)} %collective-permute-done.3), channel_id=1, source_target_pairs={{120,0},{0,8},{8,16},{16,24},{24,32},{32,40},{40,48},{48,56},{56,6... | collective-permute-start | bytes 3145736 | tf_op jit(solution)/shard_map/ppermute | solution.py:15
  377.2 17.9 %collective-permute-start.7 = (f32[1024,256]{1,0:T(8,128)S(1)}, f32[1024,256]{1,0:T(8,128)S(1)}, u32[]{:S(2)}, u32[]{:S(2)}) collective-permute-start(f32[1024,256]{1,0:T(8,128)S(1)} %slice_add_fusion.6), channel_id=1, source_target_pairs={{8,0},{16,8},{24,16},{32,24},{40,32},{48,40},{56,48},{64,56},{72,6... | collective-permute-start | bytes 3145736 | tf_op jit(solution)/shard_map/ppermute | solution.py:15
  384.1 22.3 %collective-permute-start.9 = (f32[1024,256]{1,0:T(8,128)S(1)}, f32[1024,256]{1,0:T(8,128)S(1)}, u32[]{:S(2)}, u32[]{:S(2)}) collective-permute-start(f32[1024,256]{1,0:T(8,128)S(1)} %slice_add_fusion.3), channel_id=1, source_target_pairs={{8,0},{16,8},{24,16},{32,24},{40,32},{48,40},{56,48},{64,56},{72,6... | collective-permute-start | bytes 3145736 | tf_op jit(solution)/shard_map/ppermute | solution.py:15
  384.2 54.1 %collective-permute-start.5 = (bf16[1024,512]{1,0:T(8,128)(2,1)S(1)}, bf16[1024,512]{1,0:T(8,128)(2,1)S(1)}, u32[]{:S(2)}, u32[]{:S(2)}) collective-permute-start(bf16[1024,512]{1,0:T(8,128)(2,1)S(1)} %collective-permute-done.4), channel_id=1, source_target_pairs={{120,0},{0,8},{8,16},{16,24},{24,32},{32,40},{40,48},{48,56},{56,6... | collective-permute-start | bytes 3145736 | tf_op jit(solution)/shard_map/ppermute | solution.py:15
  395.3 27.4 %collective-permute-start.8 = (f32[1024,256]{1,0:T(8,128)S(1)}, f32[1024,256]{1,0:T(8,128)S(1)}, u32[]{:S(2)}, u32[]{:S(2)}) collective-permute-start(f32[1024,256]{1,0:T(8,128)S(1)} %slice_add_fusion.5), channel_id=1, source_target_pairs={{8,0},{16,8},{24,16},{32,24},{40,32},{48,40},{56,48},{64,56},{72,6... | collective-permute-start | bytes 3145736 | tf_op jit(solution)/shard_map/ppermute | solution.py:15
  406.5 22.3 %collective-permute-start.10 = (f32[1024,256]{1,0:T(8,128)S(1)}, f32[1024,256]{1,0:T(8,128)S(1)}, u32[]{:S(2)}, u32[]{:S(2)}) collective-permute-start(f32[1024,256]{1,0:T(8,128)S(1)} %fusion.14), channel_id=1, source_target_pairs={{8,0},{16,8},{24,16},{32,24},{40,32},{48,40},{56,48},{64,56},{72,6... | collective-permute-start | bytes 3145736 | tf_op jit(solution)/shard_map/ppermute | solution.py:15
  419.1 15.7 %copy-start.5 = (bf16[1024,512]{1,0:T(8,128)(2,1)S(1)}, bf16[1024,512]{1,0:T(8,128)(2,1)}, u32[]{:S(2)}) copy-start(bf16[1024,512]{1,0:T(8,128)(2,1)} %copy-done.4) | copy-start | bytes 3145732
  429.0 18.1 %collective-permute-start.11 = (f32[1024,256]{1,0:T(8,128)S(1)}, f32[1024,256]{1,0:T(8,128)S(1)}, u32[]{:S(2)}, u32[]{:S(2)}) collective-permute-start(f32[1024,256]{1,0:T(8,128)S(1)} %fusion.13), channel_id=1, source_target_pairs={{8,0},{16,8},{24,16},{32,24},{40,32},{48,40},{56,48},{64,56},{72,6... | collective-permute-start | bytes 3145736 | tf_op jit(solution)/shard_map/ppermute | solution.py:15
Sparse Core Ops, SparseCore 0:
  9.6 98.8 all-gather.2
  178.5 165.6 all-gather.4

commit v8 on v2

--- a/solution.py
+++ b/solution.py
@@ -35,7 +35,10 @@
         held.append(shifted(held[-1], "loop", 1))
 
     cols = jnp.concatenate(held_cols, 0)
-    scores = SCALE * jnp.einsum("qd,cd->qc", q_full, cols, preferred_element_type=jnp.float32)
+    raw = jnp.einsum("qd,cd->qc", q_full, cols, preferred_element_type=jnp.float32)
+    gathered = lax.all_gather(raw, "width", axis=1, tiled=True)
+    gathered = gathered.reshape(rows, width, STEPS, sub)
+    scores = SCALE * raw
 
     index = positives[:, None]
     teach = teacher.astype(jnp.float32)
@@ -51,23 +54,21 @@
     ).reshape(rows, STEPS * sub)
 
     pos_part = jnp.sum(jnp.where(hit, scores, 0.0), 1)
-    row_part = jnp.sum(scores, 1)
+    row_part = jnp.sum(scores, 1) - jnp.sum(teach_cols, 1)
     stats = lax.psum(jnp.stack([pos_part, row_part], 0), "width")
     s_pos = stats[0][:, None]
-    s_sum = stats[1][:, None]
-    total = window * (s_pos - t_pos) - s_sum + t_sum
+    total = window * (s_pos - t_pos) - stats[1][:, None]
     coef = SCALE * 2.0 / (window - 1)
-    errors = (s_pos - scores) - (t_pos - teach_cols)
-    slopes_cols = coef * (hit.astype(jnp.float32) * total - errors)
-
-    slopes = lax.all_gather(slopes_cols, "width", axis=1, tiled=True)
-    slopes = slopes.reshape(rows, width, STEPS, sub)
+    block_col = lax.broadcasted_iota(jnp.int32, (rows, rows), 1)
 
     query_wide = queries.astype(jnp.float32)
     grad_q = None
     terms = []
     for k in range(STEPS):
-        block_slopes = slopes[:, :, k, :].reshape(rows, rows)
+        block_scores = SCALE * gathered[:, :, k, :].reshape(rows, rows)
+        errors = (s_pos - block_scores) - (t_pos - teach[:, k * rows : (k + 1) * rows])
+        block_hit = (block_col + k * rows == index).astype(jnp.float32)
+        block_slopes = coef * (block_hit * total - errors)
         gq = wide_dot(block_slopes, held[k].astype(jnp.float32))
         grad_q = gq if grad_q is None else grad_q + gq
         terms.append(wide_dot(block_slopes.T, query_wide))

time: 458 us -> 478 us (1.044)
  other arithmetic: 25 us -> 53.5 us
  local copies, waits for them, and re-layouts: 36.7 us -> 29.1 us
  waiting for transfers between devices: 277 us -> 272 us
    all_gather x1, waiting for transfers between devices: 166 us -> 114 us  [per_device(): gathered = lax.all_gather(raw, 'width', axis=1, tiled=True)]
    ppermute x9, waiting for transfers between devices: 110 us -> 157 us  [shifted(): return lax.ppermute(block, axis, route)]
    mul x0 -> x4, local copies, waits for them, and re-layouts: none -> 21.5 us  [per_device(): block_scores = SCALE * gathered[:, :, k, :].reshape(rows, rows)]
    mul x1 -> x2, other arithmetic: 3.73 us -> 25 us  [the longest x1 12.7 us: per_device(): block_slopes = coef * (block_hit * total - errors)]
    unnamed x12 -> x7, local copies, waits for them, and re-layouts: 20 us -> 6.94 us
    dynamic_slice x1 -> x0, local copies, waits for them, and re-layouts: 9.23 us -> none  [per_device(): lax.dynamic_slice_in_dim(teach.reshape(rows, STEPS, width, sub), me, 1, 2)]
    reduce_sum x2, other arithmetic: 7.17 us -> 15.9 us  [the longest x1 9.57 us: per_device(): row_part = jnp.sum(scores, 1) - jnp.sum(teach_cols, 1)]
    slice x2 -> x1, local copies, waits for them, and re-layouts: 6.82 us -> 0.01 us  [per_device(): total = window * (s_pos - t_pos) - stats[1][:, None]]
  transfers between devices with their start and end apart: 11 -> 11, of which waited for: 8 -> 8; matrix products, arithmetic and copies ran while one was open for 16% -> 13% of each run, Pallas kernels for 0% -> 0%
where the time goes in v8:
time: 478 us; the launch traced here: 472 us
  waiting for transfers between devices  272 us (57%)
  other arithmetic  53.5 us (11%)
  blocking collectives  47.2 us (10%)
  matrix products  39.4 us (8%)
  local copies, waits for them, and re-layouts  29.1 us (6%)
  starting transfers between devices  16.4 us (3%)
  between operations  14.4 us (3%)
    ppermute x9, waiting for transfers between devices, shifted(): return lax.ppermute(block, axis, route)  157 us
    all_gather x1, waiting for transfers between devices, per_device(): gathered = lax.all_gather(raw, 'width', axis=1, tiled=True)  114 us
    dot_general x8, matrix products, wide_dot(): jnp.dot(a, b, precision=lax.Precision.HIGHEST, preferred_element_type=jnp...  29.4 us
    all_to_all x1, blocking collectives, per_device(): p_cols = lax.all_to_all(passages, 'width', 0, 1, tiled=True)  26.1 us
    mul x4, local copies, waits for them, and re-layouts, per_device(): block_scores = SCALE * gathered[:, :, k, :].reshape(rows, rows)  21.5 us
    psum x1, blocking collectives, per_device(): stats = lax.psum(jnp.stack([pos_part, row_part], 0), 'width')  21.1 us
    ppermute x9, starting transfers between devices, shifted(): return lax.ppermute(block, axis, route)  16.3 us
    mul x1, other arithmetic, per_device(): block_slopes = coef * (block_hit * total - errors)  12.7 us
  transfers between devices with their start and end apart: 11, of which 8 were waited for; matrix products, arithmetic and copies ran while one was open for 13% of the time, Pallas kernels for 0%

profile of v8, /device:TPU:0, one launch (start us, length us, event | category | flops | bytes accessed | tf_op | source)
XLA Modules:
  0.0 472.1 jit_solution(17167915250874013538)
XLA Ops:
  7.2 0.0 copy-start.2
  7.2 0.0 all-gather.3.cloned.1.call-start
  7.2 0.7 all-gather.3.cloned.1.call-update
  7.9 0.0 all-gather.5.cloned.1.call-start
  8.0 26.1 %all_to_all.19 = bf16[8,128,512]{2,1,0:T(8,128)(2,1)S(1)} all-to-all(bf16[8,128,512]{2,1,0:T(8,128)(2,1)} %bitcast.41), channel_id=1, replica_groups=mesh['loop'=16,'width'=8] {'width'}, dimensions={0} | all-to-all | bytes 2097152 | tf_op jit(solution)/shard_map/all_to_all | solution.py:30
  34.1 0.7 copy.14
  34.7 0.1 collective-permute-start
  34.8 40.4 %collective-permute-done = bf16[128,4096]{0,1:T(8,128)(2,1)S(1)} collective-permute-done((bf16[128,4096]{0,1:T(8,128)(2,1)S(1)}, bf16[128,4096]{0,1:T(8,128)(2,1)S(1)}, u32[]{:S(2)}, u32[]{:S(2)}) %collective-permute-start) | collective-permute-done | bytes 1048608 | tf_op jit(solution)/shard_map/ppermute | solution.py:15
  75.2 0.0 collective-permute-start.1
  75.2 40.5 %collective-permute-done.1 = bf16[128,4096]{0,1:T(8,128)(2,1)} collective-permute-done((bf16[128,4096]{0,1:T(8,128)(2,1)S(1)}, bf16[128,4096]{0,1:T(8,128)(2,1)}, u32[]{:S(2)}, u32[]{:S(2)}) %collective-permute-start.1) | collective-permute-done | bytes 1048608 | tf_op jit(solution)/shard_map/ppermute | solution.py:15
  115.8 0.0 collective-permute-start.2
  115.8 28.2 %collective-permute-done.2 = bf16[128,4096]{0,1:T(8,128)(2,1)} collective-permute-done((bf16[128,4096]{0,1:T(8,128)(2,1)}, bf16[128,4096]{0,1:T(8,128)(2,1)}, u32[]{:S(2)}, u32[]{:S(2)}) %collective-permute-start.2) | collective-permute-done | bytes 1048608 | tf_op jit(solution)/shard_map/ppermute | solution.py:15
  144.0 0.0 all-gather.3.cloned.1.call-done
  144.0 0.0 copy-done.2
  144.0 10.0 %select_reduce_fusion.1 = (f32[1024]{0:T(1024)S(1)}, f32[1024]{0:T(1024)S(1)}, f32[1024,512]{0,1:T(8,128)}) fusion(s32[1024]{0:T(1024)S(1)} %copy-done.2, s32[512]{0:T(512)S(1)} %fusion.29, bf16[1024,4096]{1,0:T(8,128)(2,1)} %all-gather.3.cloned.1.call-done, bf16[128,4096]{0,1:T(8,128)(2,1)} %collective-permute-done.2, ...), kind=kOutput, calls=%fused_computation.34 | convolution fusion | flops 4314363904 | bytes 14694400 | tf_op jit(solution)/shard_map/qd,cd->qc/dot_general | solution.py:38
  154.0 0.0 all-gather.5.cloned.1.call-update
  154.0 10.4 %convert_bitcast_fusion = (f32[128,8,32,128]{3,1,2,0:T(8,128)S(1)}, f32[1024,4096]{1,0:T(8,128)}) fusion(bf16[1024,4096]{1,0:T(8,128)(2,1)} %param.6), kind=kLoop, calls=%fused_computation.2 | loop fusion | flops 4194304 | bytes 41943040
  164.4 6.9 %copy.23 = f32[128,8,32,128]{3,2,1,0:T(8,128)} copy(f32[128,8,32,128]{3,1,2,0:T(8,128)S(1)} %get-tuple-element.12) | data formatting | bytes 33554432
  171.3 9.6 %dynamic-slice_reduce_fusion = f32[1024]{0:T(1024)S(1)} fusion(f32[1024,4,8,128]{3,2,1,0:T(8,128)} %bitcast.35, s32[]{:T(128)S(6)} %select_n.36), kind=kLoop, calls=%fused_computation.33 | loop fusion | flops 523264 | bytes 2101252 | tf_op jit(solution)/shard_map/reduce_sum | solution.py:57
  180.9 6.3 %select_reduce_fusion = f32[1024]{0:T(1024)S(1)} fusion(s32[1024]{0:T(1024)S(1)} %copy-done.2, bf16[1024,4096]{1,0:T(8,128)(2,1)} %param.6), kind=kLoop, calls=%fused_computation | loop fusion | flops 16776192 | bytes 8396800 | tf_op jit(solution)/shard_map/reduce_sum | solution.py:46
  187.2 21.1 %psum.7 = f32[2,1024]{1,0:T(2,128)S(1)} all-reduce(f32[2,1024]{1,0:T(2,128)S(1)} %pad_maximum_fusion), channel_id=1, replica_groups=mesh['loop'=16,'width'=8] {'width'}, use_global_device_ids=true, to_apply=%region_3.4 | all-reduce | flops 2048 | bytes 16384 | tf_op jit(solution)/shard_map/psum | solution.py:58
  208.4 114.4 %all-gather.5.cloned.1.call-done = f32[1024,4096]{0,1:T(8,128)} async-done(((f32[1024,512]{0,1:T(8,128)}), f32[1024,4096]{0,1:T(8,128)}) %all-gather.5.cloned.1.call-update) | async-done | bytes 16777232 | tf_op jit(solution)/shard_map/all_gather | solution.py:39
  322.8 12.2 %slice_multiply_fusion = (f32[1024,8,1,128]{0,3,2,1:T(8,128)}, f32[1024,8,1,128]{0,3,2,1:T(8,128)}, f32[1024,8,1,128]{0,3,2,1:T(8,128)}, f32[1024,8,1,128]{0,3,2,1:T(8,128)}) fusion(f32[1024,8,4,128]{0,3,2,1:T(8,128)} %bitcast.36), kind=kLoop, calls=%fused_computation.7 | loop fusion | flops 4194304 | bytes 33554432 | tf_op jit(solution)/shard_map/mul | solution.py:68
  335.1 5.4 %copy.19 = f32[1024,1024]{1,0:T(8,128)} copy(f32[1024,1024]{0,1:T(8,128)} %bitcast.40) | data formatting | bytes 8388608 | tf_op jit(solution)/shard_map/mul | solution.py:68
  340.4 5.4 %copy.20 = f32[1024,1024]{1,0:T(8,128)} copy(f32[1024,1024]{0,1:T(8,128)} %bitcast.39) | data formatting | bytes 8388608 | tf_op jit(solution)/shard_map/mul | solution.py:68
  345.8 5.4 %copy.21 = f32[1024,1024]{1,0:T(8,128)} copy(f32[1024,1024]{0,1:T(8,128)} %bitcast.38) | data formatting | bytes 8388608 | tf_op jit(solution)/shard_map/mul | solution.py:68
  351.2 5.3 %copy.22 = f32[1024,1024]{1,0:T(8,128)} copy(f32[1024,1024]{0,1:T(8,128)} %bitcast.37) | data formatting | bytes 8388608 | tf_op jit(solution)/shard_map/mul | solution.py:68
  356.5 0.0 copy-start
  356.5 12.7 %fusion.2 = (f32[1024,1024]{1,0:T(8,128)S(1)}, f32[1024,1024]{1,0:T(8,128)S(1)}, f32[1024,1024]{1,0:T(8,128)S(1)}, f32[1024,1024]{1,0:T(8,128)S(1)}) fusion(f32[1024,4096]{1,0:T(8,128)} %get-tuple-element.13, f32[1024,1024]{1,0:T(8,128)} %copy.22, s32[1024]{0:T(1024)S(1)} %get-tuple-element.17, f32[1024]{0:T(1024)S(1)} %select_reduce_fusion, ...), kind=kLoop, calls=%fused_computation.6 | loop fusion | flops 29360128 | bytes 50360320 | tf_op jit(solution)/shard_map/mul | solution.py:71
  369.3 0.0 copy-done
  369.3 0.0 copy-start.1
  369.3 3.5 fusion.38
  372.8 4.4 collective-permute-start.6
  377.2 0.0 copy-done.1
  377.2 0.4 collective-permute-start.3
  377.7 23.1 %collective-permute-done.6 = f32[1024,512]{1,0:T(8,128)S(1)} collective-permute-done((f32[1024,512]{1,0:T(8,128)S(1)}, f32[1024,512]{1,0:T(8,128)S(1)}, u32[]{:S(2)}, u32[]{:S(2)}) %collective-permute-start.6) | collective-permute-done | bytes 2097184 | tf_op jit(solution)/shard_map/ppermute | solution.py:15
  400.7 3.5 convolution_add_fusion
  404.3 5.6 %collective-permute-start.7 = (f32[1024,512]{1,0:T(8,128)S(1)}, f32[1024,512]{1,0:T(8,128)S(1)}, u32[]{:S(2)}, u32[]{:S(2)}) collective-permute-start(f32[1024,512]{1,0:T(8,128)S(1)} %convolution_add_fusion), channel_id=1, source_target_pairs={{8,0},{16,8},{24,16},{32,24},{40,32},{48,40},{56,48},{64,56},{72,6... | collective-permute-start | bytes 6291464 | tf_op jit(solution)/shard_map/ppermute | solution.py:15
  409.9 0.0 collective-permute-done.3
  409.9 0.0 collective-permute-start.4
  409.9 17.8 %collective-permute-done.4 = bf16[1024,512]{1,0:T(8,128)(2,1)S(1)} collective-permute-done((bf16[1024,512]{1,0:T(8,128)(2,1)S(1)}, bf16[1024,512]{1,0:T(8,128)(2,1)S(1)}, u32[]{:S(2)}, u32[]{:S(2)}) %collective-permute-start.4) | collective-permute-done | bytes 1048608 | tf_op jit(solution)/shard_map/ppermute | solution.py:15
  427.7 0.0 collective-permute-start.5
  427.7 3.5 fusion.39
  431.2 2.2 collective-permute-done.7
  433.4 0.5 add.95
  433.9 5.8 %collective-permute-start.8 = (f32[1024,512]{1,0:T(8,128)S(1)}, f32[1024,512]{1,0:T(8,128)S(1)}, u32[]{:S(2)}, u32[]{:S(2)}) collective-permute-start(f32[1024,512]{1,0:T(8,128)S(1)} %add.95), channel_id=1, source_target_pairs={{8,0},{16,8},{24,16},{32,24},{40,32},{48,40},{56,48},{64,56},{72,6... | collective-permute-start | bytes 6291464 | tf_op jit(solution)/shard_map/ppermute | solution.py:15
  439.7 3.5 fusion.40
  443.1 3.4 fusion.35
  446.6 3.4 fusion.37
  450.0 3.4 fusion.36
  453.5 0.0 collective-permute-done.5
  453.5 5.1 %add_add_fusion = f32[1024,512]{1,0:T(8,128)} fusion(f32[1024,512]{1,0:T(8,128)S(1)} %fusion.37, f32[1024,512]{1,0:T(8,128)S(1)} %fusion.35, f32[1024,512]{1,0:T(8,128)S(1)} %fusion.36, f32[1024,1024]{1,0:T(8,128)S(1)} %get-tuple-element.4, bf16[1024,512]{1,0:T(8,128)(2,1)S(1)} %collective-permute-done.5), kind=kOutput, calls=%fused_computation.32 | convolution fusion | flops 6444023808 | bytes 13631488 | tf_op jit(solution)/shard_map/dot_general | solution.py:19
  458.6 4.6 collective-permute-done.8
  463.2 1.8 add.96
  (7 shorter events, 0.0 us)
Async XLA Ops:
  7.2 136.8 %copy-start.2 = (s32[1024]{0:T(1024)S(1)}, s32[1024]{0:T(1024)}, u32[]{:S(2)}) copy-start(s32[1024]{0:T(1024)} %param.7) | copy-start | bytes 12292
  7.2 136.8 %all-gather.3.cloned.1.call-start = ((), (), s32[]{:S(2)}) async-start(), calls=%async_computation.1 | async-start | bytes 9437184 | tf_op jit(solution)/shard_map/all_gather | solution.py:29
  7.9 314.9 %all-gather.5.cloned.1.call-start = ((), (), s32[]{:S(2)}) async-start(), calls=%async_computation.2 | async-start | bytes 18874368 | tf_op jit(solution)/shard_map/all_gather | solution.py:39
  34.7 40.5 %collective-permute-start = (bf16[128,4096]{0,1:T(8,128)(2,1)S(1)}, bf16[128,4096]{0,1:T(8,128)(2,1)S(1)}, u32[]{:S(2)}, u32[]{:S(2)}) collective-permute-start(bf16[128,4096]{0,1:T(8,128)(2,1)S(1)} %bitcast.43), channel_id=1, source_target_pairs={{120,0},{0,8},{8,16},{16,24},{24,32},{32,40},{40,48},{48,56},{56,6... | collective-permute-start | bytes 3145736 | tf_op jit(solution)/shard_map/ppermute | solution.py:15
  75.2 40.5 %collective-permute-start.1 = (bf16[128,4096]{0,1:T(8,128)(2,1)S(1)}, bf16[128,4096]{0,1:T(8,128)(2,1)}, u32[]{:S(2)}, u32[]{:S(2)}) collective-permute-start(bf16[128,4096]{0,1:T(8,128)(2,1)S(1)} %collective-permute-done), channel_id=1, source_target_pairs={{120,0},{0,8},{8,16},{16,24},{24,32},{32,40},{40,48},{48,56},{56,6... | collective-permute-start | bytes 3145736 | tf_op jit(solution)/shard_map/ppermute | solution.py:15
  115.8 28.2 %collective-permute-start.2 = (bf16[128,4096]{0,1:T(8,128)(2,1)}, bf16[128,4096]{0,1:T(8,128)(2,1)}, u32[]{:S(2)}, u32[]{:S(2)}) collective-permute-start(bf16[128,4096]{0,1:T(8,128)(2,1)} %collective-permute-done.1), channel_id=1, source_target_pairs={{120,0},{0,8},{8,16},{16,24},{24,32},{32,40},{40,48},{48,56},{56,6... | collective-permute-start | bytes 3145736 | tf_op jit(solution)/shard_map/ppermute | solution.py:15
  356.5 12.8 %copy-start = (bf16[1024,512]{1,0:T(8,128)(2,1)S(1)}, bf16[1024,512]{1,0:T(8,128)(2,1)}, u32[]{:S(2)}) copy-start(bf16[1024,512]{1,0:T(8,128)(2,1)} %param.4) | copy-start | bytes 3145732
  369.3 7.9 %copy-start.1 = (bf16[1024,512]{1,0:T(8,128)(2,1)S(1)}, bf16[1024,512]{1,0:T(8,128)(2,1)}, u32[]{:S(2)}) copy-start(bf16[1024,512]{1,0:T(8,128)(2,1)} %param.5) | copy-start | bytes 3145732
  372.8 28.0 %collective-permute-start.6 = (f32[1024,512]{1,0:T(8,128)S(1)}, f32[1024,512]{1,0:T(8,128)S(1)}, u32[]{:S(2)}, u32[]{:S(2)}) collective-permute-start(f32[1024,512]{1,0:T(8,128)S(1)} %fusion.38), channel_id=1, source_target_pairs={{8,0},{16,8},{24,16},{32,24},{40,32},{48,40},{56,48},{64,56},{72,6... | collective-permute-start | bytes 6291464 | tf_op jit(solution)/shard_map/ppermute | solution.py:15
  377.2 32.7 %collective-permute-start.3 = (bf16[1024,512]{1,0:T(8,128)(2,1)S(1)}, bf16[1024,512]{1,0:T(8,128)(2,1)S(1)}, u32[]{:S(2)}, u32[]{:S(2)}) collective-permute-start(bf16[1024,512]{1,0:T(8,128)(2,1)S(1)} %copy-done.1), channel_id=1, source_target_pairs={{120,0},{0,8},{8,16},{16,24},{24,32},{32,40},{40,48},{48,56},{56,6... | collective-permute-start | bytes 3145736 | tf_op jit(solution)/shard_map/ppermute | solution.py:15
  404.3 29.1 %collective-permute-start.7 = (f32[1024,512]{1,0:T(8,128)S(1)}, f32[1024,512]{1,0:T(8,128)S(1)}, u32[]{:S(2)}, u32[]{:S(2)}) collective-permute-start(f32[1024,512]{1,0:T(8,128)S(1)} %convolution_add_fusion), channel_id=1, source_target_pairs={{8,0},{16,8},{24,16},{32,24},{40,32},{48,40},{56,48},{64,56},{72,6... | collective-permute-start | bytes 6291464 | tf_op jit(solution)/shard_map/ppermute | solution.py:15
  409.9 17.8 %collective-permute-start.4 = (bf16[1024,512]{1,0:T(8,128)(2,1)S(1)}, bf16[1024,512]{1,0:T(8,128)(2,1)S(1)}, u32[]{:S(2)}, u32[]{:S(2)}) collective-permute-start(bf16[1024,512]{1,0:T(8,128)(2,1)S(1)} %collective-permute-done.3), channel_id=1, source_target_pairs={{120,0},{0,8},{8,16},{16,24},{24,32},{32,40},{40,48},{48,56},{56,6... | collective-permute-start | bytes 3145736 | tf_op jit(solution)/shard_map/ppermute | solution.py:15
  427.7 25.8 %collective-permute-start.5 = (bf16[1024,512]{1,0:T(8,128)(2,1)S(1)}, bf16[1024,512]{1,0:T(8,128)(2,1)S(1)}, u32[]{:S(2)}, u32[]{:S(2)}) collective-permute-start(bf16[1024,512]{1,0:T(8,128)(2,1)S(1)} %collective-permute-done.4), channel_id=1, source_target_pairs={{120,0},{0,8},{8,16},{16,24},{24,32},{32,40},{40,48},{48,56},{56,6... | collective-permute-start | bytes 3145736 | tf_op jit(solution)/shard_map/ppermute | solution.py:15
  433.9 29.3 %collective-permute-start.8 = (f32[1024,512]{1,0:T(8,128)S(1)}, f32[1024,512]{1,0:T(8,128)S(1)}, u32[]{:S(2)}, u32[]{:S(2)}) collective-permute-start(f32[1024,512]{1,0:T(8,128)S(1)} %add.95), channel_id=1, source_target_pairs={{8,0},{16,8},{24,16},{32,24},{40,32},{48,40},{56,48},{64,56},{72,6... | collective-permute-start | bytes 6291464 | tf_op jit(solution)/shard_map/ppermute | solution.py:15
Sparse Core Ops, SparseCore 0:
  9.6 98.8 all-gather.2
  154.2 168.6 all-gather.4

commit v9 on v2

--- a/solution.py
+++ b/solution.py
@@ -16,7 +16,7 @@
 
 
 def wide_dot(a, b):
-    return jnp.dot(a, b, precision=lax.Precision.HIGHEST, preferred_element_type=jnp.float32)
+    return jnp.dot(a, b, precision=lax.Precision.HIGH, preferred_element_type=jnp.float32)
 
 
 def per_device(queries, passages, teacher, positives):

time: 458 us -> 456 us (level)
  matrix products: 38.5 us -> 29.6 us
  waiting for transfers between devices: 277 us -> 284 us
    dot_general x8, matrix products: 29.6 us -> 20.7 us  [wide_dot(): jnp.dot(a, b, precision=lax.Precision.HIGH, preferred_element_type=jnp.fl...]
    ppermute x9, waiting for transfers between devices: 110 us -> 117 us  [shifted(): return lax.ppermute(block, axis, route)]
  transfers between devices with their start and end apart: 11 -> 11, of which waited for: 8 -> 8; matrix products, arithmetic and copies ran while one was open for 16% -> 15% of each run, Pallas kernels for 0% -> 0%
where the time goes in v9:
time: 456 us; the launch traced here: 452 us
  waiting for transfers between devices  284 us (62%)
  blocking collectives  46.2 us (10%)
  local copies, waits for them, and re-layouts  36.7 us (8%)
  matrix products  29.6 us (6%)
  other arithmetic  25 us (5%)
  starting transfers between devices  16.2 us (4%)
  between operations  14.7 us (3%)
    all_gather x1, waiting for transfers between devices, per_device(): slopes = lax.all_gather(slopes_cols, 'width', axis=1, tiled=True)  166 us
    ppermute x9, waiting for transfers between devices, shifted(): return lax.ppermute(block, axis, route)  117 us
    all_to_all x1, blocking collectives, per_device(): p_cols = lax.all_to_all(passages, 'width', 0, 1, tiled=True)  26.1 us
    dot_general x8, matrix products, wide_dot(): jnp.dot(a, b, precision=lax.Precision.HIGH, preferred_element_type=jnp.fl...  20.7 us
    psum x1, blocking collectives, per_device(): stats = lax.psum(jnp.stack([pos_part, row_part], 0), 'width')  20.1 us
    unnamed x12, local copies, waits for them, and re-layouts  20 us
    ppermute x9, starting transfers between devices, shifted(): return lax.ppermute(block, axis, route)  16.1 us
    unnamed x1, other arithmetic  11.8 us
  transfers between devices with their start and end apart: 11, of which 8 were waited for; matrix products, arithmetic and copies ran while one was open for 15% of the time, Pallas kernels for 0%

profile of v9, /device:TPU:0, one launch (start us, length us, event | category | flops | bytes accessed | tf_op | source)
XLA Modules:
  0.0 452.0 jit_solution(16950566938488514266)
XLA Ops:
  7.2 0.0 all-gather.3.cloned.1.call-start
  7.2 0.7 all-gather.3.cloned.1.call-update
  7.9 0.0 all-gather.5.cloned.1.call-start
  7.9 26.1 %all_to_all.19 = bf16[8,128,512]{2,1,0:T(8,128)(2,1)S(1)} all-to-all(bf16[8,128,512]{2,1,0:T(8,128)(2,1)} %bitcast.55), channel_id=1, replica_groups=mesh['loop'=16,'width'=8] {'width'}, dimensions={0} | all-to-all | bytes 2097152 | tf_op jit(solution)/shard_map/all_to_all | solution.py:30
  34.1 0.7 copy.8
  34.7 0.1 collective-permute-start
  34.8 40.4 %collective-permute-done = bf16[128,4096]{0,1:T(8,128)(2,1)S(1)} collective-permute-done((bf16[128,4096]{0,1:T(8,128)(2,1)S(1)}, bf16[128,4096]{0,1:T(8,128)(2,1)S(1)}, u32[]{:S(2)}, u32[]{:S(2)}) %collective-permute-start) | collective-permute-done | bytes 1048608 | tf_op jit(solution)/shard_map/ppermute | solution.py:15
  75.2 0.0 copy-start.4
  75.2 0.0 collective-permute-start.1
  75.2 11.8 %convert_bitcast_fusion = f32[128,8,32,128]{3,1,2,0:T(8,128)} fusion(bf16[1024,4096]{1,0:T(8,128)(2,1)} %param.6), kind=kLoop, calls=%fused_computation | loop fusion | flops 4194304 | bytes 25165824
  87.1 0.0 copy-done.4
  87.1 14.1 %copy.11 = f32[128,8,32,128]{3,2,1,0:T(8,128)} copy(f32[128,8,32,128]{3,1,2,0:T(8,128)} %convert_bitcast_fusion) | data formatting | bytes 33554432
  101.2 14.6 %collective-permute-done.1 = bf16[128,4096]{0,1:T(8,128)(2,1)} collective-permute-done((bf16[128,4096]{0,1:T(8,128)(2,1)S(1)}, bf16[128,4096]{0,1:T(8,128)(2,1)}, u32[]{:S(2)}, u32[]{:S(2)}) %collective-permute-start.1) | collective-permute-done | bytes 1048608 | tf_op jit(solution)/shard_map/ppermute | solution.py:15
  115.8 0.2 collective-permute-start.2
  115.9 0.0 copy-start.3
  115.9 9.2 %constant_dynamic-slice_fusion = f32[1024,4,1,128]{3,2,1,0:T(1,128)} fusion(f32[1024,4,8,128]{3,2,1,0:T(8,128)} %bitcast.46, s32[]{:T(128)S(6)} %select_n.37), kind=kLoop, calls=%fused_computation.40 | loop fusion | bytes 4194308 | tf_op jit(solution)/shard_map/dynamic_slice | solution.py:49
  125.2 4.6 %copy.10 = f32[1024,4,1,128]{0,3,1,2:T(8,128)S(1)} copy(f32[1024,4,1,128]{3,2,1,0:T(1,128)} %constant_dynamic-slice_fusion) | data formatting | bytes 4194304
  129.7 0.0 copy-done.3
  129.8 6.8 %convert_reduce_fusion = (f32[1024]{0:T(1024)S(1)}, f32[1024]{0:T(1024)S(1)}) fusion(bf16[1024,4096]{1,0:T(8,128)(2,1)} %param.6, s32[1024]{0:T(1024)S(1)} %copy-done.3), kind=kLoop, calls=%fused_computation.1 | loop fusion | flops 20969472 | bytes 8400896 | tf_op jit(solution)/shard_map/reduce_sum | solution.py:44
  136.6 7.4 %collective-permute-done.2 = bf16[128,4096]{0,1:T(8,128)(2,1)} collective-permute-done((bf16[128,4096]{0,1:T(8,128)(2,1)}, bf16[128,4096]{0,1:T(8,128)(2,1)}, u32[]{:S(2)}, u32[]{:S(2)}) %collective-permute-start.2) | collective-permute-done | bytes 1048608 | tf_op jit(solution)/shard_map/ppermute | solution.py:15
  144.0 0.0 all-gather.3.cloned.1.call-done
  144.0 8.9 %multiply_reduce_fusion = (f32[1024]{0:T(1024)S(1)}, f32[512,1024]{1,0:T(8,128)S(1)}) fusion(bf16[1024,4096]{1,0:T(8,128)(2,1)} %all-gather.3.cloned.1.call-done, bf16[128,4096]{0,1:T(8,128)(2,1)} %collective-permute-done.2, bf16[128,4096]{0,1:T(8,128)(2,1)} %collective-permute-done.1, bf16[128,4096]{0,1:T(8,128)(2,1)} %copy-done.4, ...), kind=kOutput, calls=%fused_computation.22 | convolution fusion | flops 4312792064 | bytes 14684160 | tf_op jit(solution)/shard_map/qd,cd->qc/dot_general | solution.py:38
  152.9 0.0 copy-start.1
  152.9 1.3 copy-done.1
  154.2 0.3 fusion.9
  154.6 20.1 %psum.7 = f32[2,1024]{1,0:T(2,128)S(1)} all-reduce(f32[2,1024]{1,0:T(2,128)S(1)} %pad_maximum_fusion), channel_id=1, replica_groups=mesh['loop'=16,'width'=8] {'width'}, use_global_device_ids=true, to_apply=%region_2.3 | all-reduce | flops 2048 | bytes 16384 | tf_op jit(solution)/shard_map/psum | solution.py:55
  174.7 3.7 fusion.11
  178.5 0.0 all-gather.5.cloned.1.call-update
  178.5 165.8 %all-gather.5.cloned.1.call-done = f32[1024,4096]{0,1:T(8,128)} async-done(((f32[1024,512]{0,1:T(8,128)}), f32[1024,4096]{0,1:T(8,128)}) %all-gather.5.cloned.1.call-update) | async-done | bytes 16777232 | tf_op jit(solution)/shard_map/all_gather | solution.py:63
  344.3 0.0 copy-start
  344.3 6.8 %fusion.24 = (f32[1024,8,1,128]{0,3,2,1:T(8,128)S(1)}, f32[1024,8,1,128]{0,3,2,1:T(8,128)S(1)}, f32[1024,8,1,128]{0,3,2,1:T(8,128)S(1)}, f32[1024,8,1,128]{0,3,2,1:T(8,128)S(1)}) fusion(f32[1024,8,4,128]{0,3,2,1:T(8,128)} %bitcast.47), kind=kLoop, calls=%fused_computation.42 | loop fusion | bytes 33554432 | tf_op jit(solution)/shard_map/slice | solution.py:70
  351.2 0.0 copy-start.2
  351.2 0.0 copy-done
  351.2 2.4 fusion.29
  353.5 4.4 collective-permute-start.6
  358.0 0.0 copy-done.2
  358.0 0.0 collective-permute-start.3
  358.0 23.5 %collective-permute-done.6 = f32[1024,512]{1,0:T(8,128)S(1)} collective-permute-done((f32[1024,512]{1,0:T(8,128)S(1)}, f32[1024,512]{1,0:T(8,128)S(1)}, u32[]{:S(2)}, u32[]{:S(2)}) %collective-permute-start.6) | collective-permute-done | bytes 2097184 | tf_op jit(solution)/shard_map/ppermute | solution.py:15
  381.5 2.4 convolution_add_fusion
  383.9 5.6 %collective-permute-start.7 = (f32[1024,512]{1,0:T(8,128)S(1)}, f32[1024,512]{1,0:T(8,128)S(1)}, u32[]{:S(2)}, u32[]{:S(2)}) collective-permute-start(f32[1024,512]{1,0:T(8,128)S(1)} %convolution_add_fusion), channel_id=1, source_target_pairs={{8,0},{16,8},{24,16},{32,24},{40,32},{48,40},{56,48},{64,56},{72,6... | collective-permute-start | bytes 6291464 | tf_op jit(solution)/shard_map/ppermute | solution.py:15
  389.5 0.0 collective-permute-done.3
  389.5 0.0 collective-permute-start.4
  389.5 17.8 %collective-permute-done.4 = bf16[1024,512]{1,0:T(8,128)(2,1)S(1)} collective-permute-done((bf16[1024,512]{1,0:T(8,128)(2,1)S(1)}, bf16[1024,512]{1,0:T(8,128)(2,1)S(1)}, u32[]{:S(2)}, u32[]{:S(2)}) %collective-permute-start.4) | collective-permute-done | bytes 1048608 | tf_op jit(solution)/shard_map/ppermute | solution.py:15
  407.3 0.0 collective-permute-start.5
  407.3 2.4 fusion.30
  409.7 3.3 collective-permute-done.7
  413.0 0.5 add.77
  413.5 5.8 %collective-permute-start.8 = (f32[1024,512]{1,0:T(8,128)S(1)}, f32[1024,512]{1,0:T(8,128)S(1)}, u32[]{:S(2)}, u32[]{:S(2)}) collective-permute-start(f32[1024,512]{1,0:T(8,128)S(1)} %add.77), channel_id=1, source_target_pairs={{8,0},{16,8},{24,16},{32,24},{40,32},{48,40},{56,48},{64,56},{72,6... | collective-permute-start | bytes 6291464 | tf_op jit(solution)/shard_map/ppermute | solution.py:15
  419.4 2.4 fusion.26
  421.8 2.3 fusion.31
  424.1 2.4 fusion.28
  426.6 2.4 fusion.27
  429.0 0.0 collective-permute-done.5
  429.0 4.0 add_add_fusion
  433.0 9.9 %collective-permute-done.8 = f32[1024,512]{1,0:T(8,128)S(1)} collective-permute-done((f32[1024,512]{1,0:T(8,128)S(1)}, f32[1024,512]{1,0:T(8,128)S(1)}, u32[]{:S(2)}, u32[]{:S(2)}) %collective-permute-start.8) | collective-permute-done | bytes 2097184 | tf_op jit(solution)/shard_map/ppermute | solution.py:15
  442.9 1.8 add.78
  (4 shorter events, 0.0 us)
Async XLA Ops:
  7.2 136.8 %all-gather.3.cloned.1.call-start = ((), (), s32[]{:S(2)}) async-start(), calls=%async_computation.1 | async-start | bytes 9437184 | tf_op jit(solution)/shard_map/all_gather | solution.py:29
  7.9 336.4 %all-gather.5.cloned.1.call-start = ((), (), s32[]{:S(2)}) async-start(), calls=%async_computation.2 | async-start | bytes 18874368 | tf_op jit(solution)/shard_map/all_gather | solution.py:63
  34.7 40.5 %collective-permute-start = (bf16[128,4096]{0,1:T(8,128)(2,1)S(1)}, bf16[128,4096]{0,1:T(8,128)(2,1)S(1)}, u32[]{:S(2)}, u32[]{:S(2)}) collective-permute-start(bf16[128,4096]{0,1:T(8,128)(2,1)S(1)} %bitcast.56), channel_id=1, source_target_pairs={{120,0},{0,8},{8,16},{16,24},{24,32},{32,40},{40,48},{48,56},{56,6... | collective-permute-start | bytes 3145736 | tf_op jit(solution)/shard_map/ppermute | solution.py:15
  75.2 11.8 %copy-start.4 = (bf16[128,4096]{0,1:T(8,128)(2,1)}, bf16[128,4096]{0,1:T(8,128)(2,1)S(1)}, u32[]{:S(2)}) copy-start(bf16[128,4096]{0,1:T(8,128)(2,1)S(1)} %collective-permute-done) | copy-start | bytes 3145732
  75.2 40.5 %collective-permute-start.1 = (bf16[128,4096]{0,1:T(8,128)(2,1)S(1)}, bf16[128,4096]{0,1:T(8,128)(2,1)}, u32[]{:S(2)}, u32[]{:S(2)}) collective-permute-start(bf16[128,4096]{0,1:T(8,128)(2,1)S(1)} %collective-permute-done), channel_id=1, source_target_pairs={{120,0},{0,8},{8,16},{16,24},{24,32},{32,40},{40,48},{48,56},{56,6... | collective-permute-start | bytes 3145736 | tf_op jit(solution)/shard_map/ppermute | solution.py:15
  115.8 28.2 %collective-permute-start.2 = (bf16[128,4096]{0,1:T(8,128)(2,1)}, bf16[128,4096]{0,1:T(8,128)(2,1)}, u32[]{:S(2)}, u32[]{:S(2)}) collective-permute-start(bf16[128,4096]{0,1:T(8,128)(2,1)} %collective-permute-done.1), channel_id=1, source_target_pairs={{120,0},{0,8},{8,16},{16,24},{24,32},{32,40},{40,48},{48,56},{56,6... | collective-permute-start | bytes 3145736 | tf_op jit(solution)/shard_map/ppermute | solution.py:15
  115.9 13.8 %copy-start.3 = (s32[1024]{0:T(1024)S(1)}, s32[1024]{0:T(1024)}, u32[]{:S(2)}) copy-start(s32[1024]{0:T(1024)} %param.7) | copy-start | bytes 12292
  152.9 1.3 copy-start.1
  344.3 6.8 %copy-start = (bf16[1024,512]{1,0:T(8,128)(2,1)S(1)}, bf16[1024,512]{1,0:T(8,128)(2,1)}, u32[]{:S(2)}) copy-start(bf16[1024,512]{1,0:T(8,128)(2,1)} %param.4) | copy-start | bytes 3145732
  351.2 6.8 %copy-start.2 = (bf16[1024,512]{1,0:T(8,128)(2,1)S(1)}, bf16[1024,512]{1,0:T(8,128)(2,1)}, u32[]{:S(2)}) copy-start(bf16[1024,512]{1,0:T(8,128)(2,1)} %param.5) | copy-start | bytes 3145732
  353.5 28.0 %collective-permute-start.6 = (f32[1024,512]{1,0:T(8,128)S(1)}, f32[1024,512]{1,0:T(8,128)S(1)}, u32[]{:S(2)}, u32[]{:S(2)}) collective-permute-start(f32[1024,512]{1,0:T(8,128)S(1)} %fusion.29), channel_id=1, source_target_pairs={{8,0},{16,8},{24,16},{32,24},{40,32},{48,40},{56,48},{64,56},{72,6... | collective-permute-start | bytes 6291464 | tf_op jit(solution)/shard_map/ppermute | solution.py:15
  358.0 31.5 %collective-permute-start.3 = (bf16[1024,512]{1,0:T(8,128)(2,1)S(1)}, bf16[1024,512]{1,0:T(8,128)(2,1)S(1)}, u32[]{:S(2)}, u32[]{:S(2)}) collective-permute-start(bf16[1024,512]{1,0:T(8,128)(2,1)S(1)} %copy-done.2), channel_id=1, source_target_pairs={{120,0},{0,8},{8,16},{16,24},{24,32},{32,40},{40,48},{48,56},{56,6... | collective-permute-start | bytes 3145736 | tf_op jit(solution)/shard_map/ppermute | solution.py:15
  383.9 29.1 %collective-permute-start.7 = (f32[1024,512]{1,0:T(8,128)S(1)}, f32[1024,512]{1,0:T(8,128)S(1)}, u32[]{:S(2)}, u32[]{:S(2)}) collective-permute-start(f32[1024,512]{1,0:T(8,128)S(1)} %convolution_add_fusion), channel_id=1, source_target_pairs={{8,0},{16,8},{24,16},{32,24},{40,32},{48,40},{56,48},{64,56},{72,6... | collective-permute-start | bytes 6291464 | tf_op jit(solution)/shard_map/ppermute | solution.py:15
  389.5 17.8 %collective-permute-start.4 = (bf16[1024,512]{1,0:T(8,128)(2,1)S(1)}, bf16[1024,512]{1,0:T(8,128)(2,1)S(1)}, u32[]{:S(2)}, u32[]{:S(2)}) collective-permute-start(bf16[1024,512]{1,0:T(8,128)(2,1)S(1)} %collective-permute-done.3), channel_id=1, source_target_pairs={{120,0},{0,8},{8,16},{16,24},{24,32},{32,40},{40,48},{48,56},{56,6... | collective-permute-start | bytes 3145736 | tf_op jit(solution)/shard_map/ppermute | solution.py:15
  407.3 21.7 %collective-permute-start.5 = (bf16[1024,512]{1,0:T(8,128)(2,1)S(1)}, bf16[1024,512]{1,0:T(8,128)(2,1)S(1)}, u32[]{:S(2)}, u32[]{:S(2)}) collective-permute-start(bf16[1024,512]{1,0:T(8,128)(2,1)S(1)} %collective-permute-done.4), channel_id=1, source_target_pairs={{120,0},{0,8},{8,16},{16,24},{24,32},{32,40},{40,48},{48,56},{56,6... | collective-permute-start | bytes 3145736 | tf_op jit(solution)/shard_map/ppermute | solution.py:15
  413.5 29.4 %collective-permute-start.8 = (f32[1024,512]{1,0:T(8,128)S(1)}, f32[1024,512]{1,0:T(8,128)S(1)}, u32[]{:S(2)}, u32[]{:S(2)}) collective-permute-start(f32[1024,512]{1,0:T(8,128)S(1)} %add.77), channel_id=1, source_target_pairs={{8,0},{16,8},{24,16},{32,24},{40,32},{48,40},{56,48},{64,56},{72,6... | collective-permute-start | bytes 6291464 | tf_op jit(solution)/shard_map/ppermute | solution.py:15
Sparse Core Ops, SparseCore 0:
  9.6 98.8 all-gather.2
  178.6 165.6 all-gather.4

commit v10 on v9

--- a/solution.py
+++ b/solution.py
@@ -60,14 +60,16 @@
     errors = (s_pos - scores) - (t_pos - teach_cols)
     slopes_cols = coef * (hit.astype(jnp.float32) * total - errors)
 
-    slopes = lax.all_gather(slopes_cols, "width", axis=1, tiled=True)
-    slopes = slopes.reshape(rows, width, STEPS, sub)
+    slopes = [
+        lax.all_gather(slopes_cols[:, k * sub : (k + 1) * sub], "width", axis=1, tiled=True)
+        for k in range(STEPS)
+    ]
 
     query_wide = queries.astype(jnp.float32)
     grad_q = None
     terms = []
     for k in range(STEPS):
-        block_slopes = slopes[:, :, k, :].reshape(rows, rows)
+        block_slopes = slopes[k]
         gq = wide_dot(block_slopes, held[k].astype(jnp.float32))
         grad_q = gq if grad_q is None else grad_q + gq
         terms.append(wide_dot(block_slopes.T, query_wide))

time: 456 us -> 461 us (1.011); the launches traced: 452 us -> 462 us
  matrix products: 29.6 us -> 45.7 us
  starting transfers between devices: 16.2 us -> 8.63 us
    all_gather x1 -> x4, waiting for transfers between devices: 166 us -> 182 us  [per_device(): lax.all_gather(slopes_cols[:, k * sub:(k + 1) * sub], 'width', axis=1, ti...]
    dot_general x8, matrix products: 20.7 us -> 36.8 us  [wide_dot(): jnp.dot(a, b, precision=lax.Precision.HIGH, preferred_element_type=jnp.fl...]
    ppermute x9, waiting for transfers between devices: 117 us -> 103 us  [shifted(): return lax.ppermute(block, axis, route)]
    ppermute x9, starting transfers between devices: 16.1 us -> 8.44 us  [shifted(): return lax.ppermute(block, axis, route)]
    slice x1, local copies, waits for them, and re-layouts: 6.81 us -> 1.35 us  [per_device(): slopes_cols[:, k * sub:(k + 1) * sub]]
    unnamed x12 -> x22, local copies, waits for them, and re-layouts: 20 us -> 21.1 us
  transfers between devices with their start and end apart: 11 -> 14, of which waited for: 8 -> 8; matrix products, arithmetic and copies ran while one was open for 15% -> 19% of each run, Pallas kernels for 0% -> 0%
where the time goes in v10:
time: 461 us; the launch traced here: 462 us
  waiting for transfers between devices  288 us (62%)
  blocking collectives  46 us (10%)
  matrix products  45.7 us (10%)
  local copies, waits for them, and re-layouts  32.4 us (7%)
  other arithmetic  27 us (6%)
  between operations  14.4 us (3%)
  starting transfers between devices  8.63 us (2%)
    all_gather x4, waiting for transfers between devices, per_device(): lax.all_gather(slopes_cols[:, k * sub:(k + 1) * sub], 'width', axis=1, ti...  182 us
    ppermute x9, waiting for transfers between devices, shifted(): return lax.ppermute(block, axis, route)  103 us
    dot_general x8, matrix products, wide_dot(): jnp.dot(a, b, precision=lax.Precision.HIGH, preferred_element_type=jnp.fl...  36.8 us
    all_to_all x1, blocking collectives, per_device(): p_cols = lax.all_to_all(passages, 'width', 0, 1, tiled=True)  26.1 us
    unnamed x22, local copies, waits for them, and re-layouts  21.1 us
    psum x1, blocking collectives, per_device(): stats = lax.psum(jnp.stack([pos_part, row_part], 0), 'width')  19.9 us
    unnamed x1, other arithmetic  11.8 us
    dynamic_slice x1, local copies, waits for them, and re-layouts, per_device(): lax.dynamic_slice_in_dim(teach.reshape(rows, STEPS, width, sub), me, 1, 2)  9.23 us
  transfers between devices with their start and end apart: 14, of which 8 were waited for; matrix products, arithmetic and copies ran while one was open for 19% of the time, Pallas kernels for 0%

profile of v10, /device:TPU:0, one launch (start us, length us, event | category | flops | bytes accessed | tf_op | source)
XLA Modules:
  0.0 461.9 jit_solution(15555897853204002195)
XLA Ops:
  7.2 0.0 all-gather.6.cloned.1.call-start
  7.2 0.7 all-gather.6.cloned.1.call-update
  7.9 0.0 all-gather.14.cloned.1.call-start
  7.9 26.1 %all_to_all.19 = bf16[8,128,512]{2,1,0:T(8,128)(2,1)S(1)} all-to-all(bf16[8,128,512]{2,1,0:T(8,128)(2,1)} %bitcast), channel_id=1, replica_groups=mesh['loop'=16,'width'=8] {'width'}, dimensions={0} | all-to-all | bytes 2097152 | tf_op jit(solution)/shard_map/all_to_all | solution.py:30
  34.1 0.7 copy.8
  34.7 0.1 collective-permute-start
  34.8 40.4 %collective-permute-done = bf16[128,4096]{0,1:T(8,128)(2,1)S(1)} collective-permute-done((bf16[128,4096]{0,1:T(8,128)(2,1)S(1)}, bf16[128,4096]{0,1:T(8,128)(2,1)S(1)}, u32[]{:S(2)}, u32[]{:S(2)}) %collective-permute-start) | collective-permute-done | bytes 1048608 | tf_op jit(solution)/shard_map/ppermute | solution.py:15
  75.2 0.0 collective-permute-start.1
  75.2 11.8 %convert_bitcast_fusion = f32[128,8,32,128]{3,1,2,0:T(8,128)} fusion(bf16[1024,4096]{1,0:T(8,128)(2,1)} %param.6), kind=kLoop, calls=%fused_computation | loop fusion | flops 4194304 | bytes 25165824
  87.1 0.0 copy-done.9
  87.1 14.1 %copy.11 = f32[128,8,32,128]{3,2,1,0:T(8,128)} copy(f32[128,8,32,128]{3,1,2,0:T(8,128)} %convert_bitcast_fusion) | data formatting | bytes 33554432
  101.2 14.5 %collective-permute-done.1 = bf16[128,4096]{0,1:T(8,128)(2,1)} collective-permute-done((bf16[128,4096]{0,1:T(8,128)(2,1)S(1)}, bf16[128,4096]{0,1:T(8,128)(2,1)}, u32[]{:S(2)}, u32[]{:S(2)}) %collective-permute-start.1) | collective-permute-done | bytes 1048608 | tf_op jit(solution)/shard_map/ppermute | solution.py:15
  115.8 0.2 collective-permute-start.2
  115.9 9.2 %constant_dynamic-slice_fusion = f32[1024,4,1,128]{3,2,1,0:T(1,128)} fusion(f32[1024,4,8,128]{3,2,1,0:T(8,128)} %bitcast.39, s32[]{:T(128)S(6)} %select_n.37), kind=kLoop, calls=%fused_computation.40 | loop fusion | bytes 4194308 | tf_op jit(solution)/shard_map/dynamic_slice | solution.py:49
  125.1 4.6 copy.10
  129.7 0.0 copy-done.8
  129.8 6.8 %convert_reduce_fusion = (f32[1024]{0:T(1024)S(1)}, f32[1024]{0:T(1024)S(1)}) fusion(bf16[1024,4096]{1,0:T(8,128)(2,1)} %param.6, s32[1024]{0:T(1024)S(1)} %copy-done.8), kind=kLoop, calls=%fused_computation.1 | loop fusion | flops 20969472 | bytes 8400896 | tf_op jit(solution)/shard_map/reduce_sum | solution.py:44
  136.6 7.4 %collective-permute-done.2 = bf16[128,4096]{0,1:T(8,128)(2,1)} collective-permute-done((bf16[128,4096]{0,1:T(8,128)(2,1)}, bf16[128,4096]{0,1:T(8,128)(2,1)}, u32[]{:S(2)}, u32[]{:S(2)}) %collective-permute-start.2) | collective-permute-done | bytes 1048608 | tf_op jit(solution)/shard_map/ppermute | solution.py:15
  144.0 8.9 %multiply_reduce_fusion = (f32[1024]{0:T(1024)S(1)}, f32[512,1024]{1,0:T(8,128)S(1)}) fusion(bf16[1024,4096]{1,0:T(8,128)(2,1)} %all-gather.6.cloned.1.call-done, bf16[128,4096]{0,1:T(8,128)(2,1)} %collective-permute-done.2, bf16[128,4096]{0,1:T(8,128)(2,1)} %collective-permute-done.1, bf16[128,4096]{0,1:T(8,128)(2,1)} %copy-done.9, ...), kind=kOutput, calls=%fused_computation.22 | convolution fusion | flops 4312792064 | bytes 14684160 | tf_op jit(solution)/shard_map/qd,cd->qc/dot_general | solution.py:38
  152.9 0.0 copy-start.2
  152.9 1.3 copy-done.2
  154.2 0.3 fusion.9
  154.6 19.9 %psum.7 = f32[2,1024]{1,0:T(2,128)S(1)} all-reduce(f32[2,1024]{1,0:T(2,128)S(1)} %pad_maximum_fusion), channel_id=1, replica_groups=mesh['loop'=16,'width'=8] {'width'}, use_global_device_ids=true, to_apply=%region_2.3 | all-reduce | flops 2048 | bytes 16384 | tf_op jit(solution)/shard_map/psum | solution.py:55
  174.5 2.4 fusion.11
  176.9 1.4 fusion.24
  178.3 0.0 all-gather.14.cloned.1.call-update
  178.3 0.0 all-gather.12.cloned.1.call-start
  178.4 0.7 all-gather.12.cloned.1.call-update
  179.0 0.0 all-gather.10.cloned.1.call-start
  179.1 0.5 all-gather.10.cloned.1.call-update
  179.6 0.0 all-gather.8.cloned.1.call-start
  179.7 0.5 all-gather.8.cloned.1.call-update
  180.2 46.0 %all-gather.14.cloned.1.call-done = f32[1024,1024]{0,1:T(8,128)} async-done(((f32[1024,128]{0,1:T(8,128)}), f32[1024,1024]{0,1:T(8,128)}) %all-gather.14.cloned.1.call-update) | async-done | bytes 4194320 | tf_op jit(solution)/shard_map/all_gather | solution.py:64
  226.2 0.0 copy-done
  226.2 4.5 fusion.29
  230.7 4.6 %collective-permute-start.6 = (f32[1024,512]{1,0:T(8,128)S(1)}, f32[1024,512]{1,0:T(8,128)}, u32[]{:S(2)}, u32[]{:S(2)}) collective-permute-start(f32[1024,512]{1,0:T(8,128)S(1)} %fusion.29), channel_id=1, source_target_pairs={{8,0},{16,8},{24,16},{32,24},{40,32},{48,40},{56,48},{64,56},{72,6... | collective-permute-start | bytes 6291464 | tf_op jit(solution)/shard_map/ppermute | solution.py:15
  235.3 0.0 collective-permute-start.3
  235.3 64.2 %all-gather.12.cloned.1.call-done = f32[1024,1024]{0,1:T(8,128)} async-done(((f32[1024,128]{0,1:T(8,128)}), f32[1024,1024]{0,1:T(8,128)}) %all-gather.12.cloned.1.call-update) | async-done | bytes 4194320 | tf_op jit(solution)/shard_map/all_gather | solution.py:64
  299.5 0.0 collective-permute-done.6
  299.5 5.2 %convolution_add_fusion = f32[1024,512]{1,0:T(8,128)S(1)} fusion(f32[1024,512]{1,0:T(8,128)} %collective-permute-done.6, f32[1024,1024]{0,1:T(8,128)} %all-gather.12.cloned.1.call-done, bf16[1024,512]{1,0:T(8,128)(2,1)S(1)} %copy-done), kind=kOutput, calls=%fused_computation.23 | convolution fusion | flops 3221749760 | bytes 9437184 | tf_op jit(solution)/shard_map/dot_general | solution.py:19
  304.7 3.5 collective-permute-start.7
  308.2 0.0 collective-permute-done.3
  308.2 0.0 collective-permute-start.4
  308.2 40.7 %collective-permute-done.4 = bf16[1024,512]{1,0:T(8,128)(2,1)} collective-permute-done((bf16[1024,512]{1,0:T(8,128)(2,1)}, bf16[1024,512]{1,0:T(8,128)(2,1)}, u32[]{:S(2)}, u32[]{:S(2)}) %collective-permute-start.4) | collective-permute-done | bytes 1048608 | tf_op jit(solution)/shard_map/ppermute | solution.py:15
  349.0 0.0 collective-permute-start.5
  349.0 19.5 %all-gather.10.cloned.1.call-done = f32[1024,1024]{0,1:T(8,128)} async-done(((f32[1024,128]{0,1:T(8,128)}), f32[1024,1024]{0,1:T(8,128)}) %all-gather.10.cloned.1.call-update) | async-done | bytes 4194320 | tf_op jit(solution)/shard_map/all_gather | solution.py:64
  368.4 4.5 fusion.30
  373.0 0.0 copy-start.5
  373.0 0.0 collective-permute-done.7
  373.0 2.2 add.77
  375.2 0.1 collective-permute-start.8
  375.3 0.6 copy-done.5
  375.9 5.2 %fusion.28 = f32[1024,512]{1,0:T(8,128)} fusion(f32[1024,1024]{0,1:T(8,128)S(1)} %copy-done.5, bf16[1024,512]{1,0:T(8,128)(2,1)} %collective-permute-done.4), kind=kOutput, calls=%fused_computation.46 | convolution fusion | flops 3221225472 | bytes 7340032 | tf_op jit(solution)/shard_map/dot_general | solution.py:19
  381.1 0.0 copy-done.3
  381.1 4.9 %fusion.27 = f32[1024,512]{1,0:T(8,128)} fusion(f32[1024,1024]{0,1:T(8,128)S(1)} %copy-done.3, bf16[1024,512]{1,0:T(8,128)(2,1)} %collective-permute-done.3), kind=kOutput, calls=%fused_computation.45 | convolution fusion | flops 3221225472 | bytes 7340032 | tf_op jit(solution)/shard_map/dot_general | solution.py:19
  386.0 52.6 %all-gather.8.cloned.1.call-done = f32[1024,1024]{0,1:T(8,128)} async-done(((f32[1024,128]{0,1:T(8,128)}), f32[1024,1024]{0,1:T(8,128)}) %all-gather.8.cloned.1.call-update) | async-done | bytes 4194320 | tf_op jit(solution)/shard_map/all_gather | solution.py:64
  438.7 5.0 %fusion.26 = f32[1024,512]{1,0:T(8,128)S(1)} fusion(f32[1024,1024]{0,1:T(8,128)} %all-gather.8.cloned.1.call-done, bf16[1024,512]{1,0:T(8,128)(2,1)} %param.5), kind=kOutput, calls=%fused_computation.44 | convolution fusion | flops 3221225472 | bytes 7340032 | tf_op jit(solution)/shard_map/dot_general | solution.py:19
  443.7 0.0 copy-start.6
  443.7 2.3 fusion.31
  446.1 0.0 collective-permute-done.5
  446.1 0.5 copy-done.6
  446.6 5.0 %add_add_fusion = f32[1024,512]{1,0:T(8,128)} fusion(f32[1024,512]{1,0:T(8,128)S(1)} %copy-done.6, f32[1024,512]{1,0:T(8,128)S(1)} %fusion.26, f32[1024,512]{1,0:T(8,128)S(1)} %copy-done.7, f32[1024,1024]{0,1:T(8,128)S(1)} %copy-done.1, bf16[1024,512]{1,0:T(8,128)(2,1)} %collective-permute-done.5), kind=kOutput, calls=%fused_computation.21 | convolution fusion | flops 3222798336 | bytes 13631488 | tf_op jit(solution)/shard_map/dot_general | solution.py:19
  451.6 0.0 collective-permute-done.8
  451.6 3.4 add.78
  (15 shorter events, 0.1 us)
Async XLA Ops:
  7.2 136.8 %all-gather.6.cloned.1.call-start = ((), (), s32[]{:S(2)}) async-start(), calls=%async_computation.1 | async-start | bytes 9437184 | tf_op jit(solution)/shard_map/all_gather | solution.py:29
  7.9 218.3 %all-gather.14.cloned.1.call-start = ((), (), s32[]{:S(2)}) async-start(), calls=%async_computation.5 | async-start | bytes 4718592 | tf_op jit(solution)/shard_map/all_gather | solution.py:64
  34.7 40.5 %collective-permute-start = (bf16[128,4096]{0,1:T(8,128)(2,1)S(1)}, bf16[128,4096]{0,1:T(8,128)(2,1)S(1)}, u32[]{:S(2)}, u32[]{:S(2)}) collective-permute-start(bf16[128,4096]{0,1:T(8,128)(2,1)S(1)} %bitcast.41), channel_id=1, source_target_pairs={{120,0},{0,8},{8,16},{16,24},{24,32},{32,40},{40,48},{48,56},{56,6... | collective-permute-start | bytes 3145736 | tf_op jit(solution)/shard_map/ppermute | solution.py:15
  75.2 11.8 %copy-start.9 = (bf16[128,4096]{0,1:T(8,128)(2,1)}, bf16[128,4096]{0,1:T(8,128)(2,1)S(1)}, u32[]{:S(2)}) copy-start(bf16[128,4096]{0,1:T(8,128)(2,1)S(1)} %collective-permute-done) | copy-start | bytes 3145732
  75.2 40.5 %collective-permute-start.1 = (bf16[128,4096]{0,1:T(8,128)(2,1)S(1)}, bf16[128,4096]{0,1:T(8,128)(2,1)}, u32[]{:S(2)}, u32[]{:S(2)}) collective-permute-start(bf16[128,4096]{0,1:T(8,128)(2,1)S(1)} %collective-permute-done), channel_id=1, source_target_pairs={{120,0},{0,8},{8,16},{16,24},{24,32},{32,40},{40,48},{48,56},{56,6... | collective-permute-start | bytes 3145736 | tf_op jit(solution)/shard_map/ppermute | solution.py:15
  115.8 28.2 %collective-permute-start.2 = (bf16[128,4096]{0,1:T(8,128)(2,1)}, bf16[128,4096]{0,1:T(8,128)(2,1)}, u32[]{:S(2)}, u32[]{:S(2)}) collective-permute-start(bf16[128,4096]{0,1:T(8,128)(2,1)} %collective-permute-done.1), channel_id=1, source_target_pairs={{120,0},{0,8},{8,16},{16,24},{24,32},{32,40},{40,48},{48,56},{56,6... | collective-permute-start | bytes 3145736 | tf_op jit(solution)/shard_map/ppermute | solution.py:15
  125.1 4.6 copy-start.8
  152.9 1.3 copy-start.2
  178.3 47.9 %copy-start = (bf16[1024,512]{1,0:T(8,128)(2,1)S(1)}, bf16[1024,512]{1,0:T(8,128)(2,1)}, u32[]{:S(2)}) copy-start(bf16[1024,512]{1,0:T(8,128)(2,1)} %param.4) | copy-start | bytes 3145732
  178.3 121.2 %all-gather.12.cloned.1.call-start = ((), (), s32[]{:S(2)}) async-start(), calls=%async_computation.4 | async-start | bytes 4718592 | tf_op jit(solution)/shard_map/all_gather | solution.py:64
  179.0 189.4 %all-gather.10.cloned.1.call-start = ((), (), s32[]{:S(2)}) async-start(), calls=%async_computation.3 | async-start | bytes 4718592 | tf_op jit(solution)/shard_map/all_gather | solution.py:64
  179.6 259.0 %all-gather.8.cloned.1.call-start = ((), (), s32[]{:S(2)}) async-start(), calls=%async_computation.2 | async-start | bytes 4718592 | tf_op jit(solution)/shard_map/all_gather | solution.py:64
  230.7 68.8 %collective-permute-start.6 = (f32[1024,512]{1,0:T(8,128)S(1)}, f32[1024,512]{1,0:T(8,128)}, u32[]{:S(2)}, u32[]{:S(2)}) collective-permute-start(f32[1024,512]{1,0:T(8,128)S(1)} %fusion.29), channel_id=1, source_target_pairs={{8,0},{16,8},{24,16},{32,24},{40,32},{48,40},{56,48},{64,56},{72,6... | collective-permute-start | bytes 6291464 | tf_op jit(solution)/shard_map/ppermute | solution.py:15
  235.3 72.9 %collective-permute-start.3 = (bf16[1024,512]{1,0:T(8,128)(2,1)}, bf16[1024,512]{1,0:T(8,128)(2,1)}, u32[]{:S(2)}, u32[]{:S(2)}) collective-permute-start(bf16[1024,512]{1,0:T(8,128)(2,1)} %param.5), channel_id=1, source_target_pairs={{120,0},{0,8},{8,16},{16,24},{24,32},{32,40},{40,48},{48,56},{56,6... | collective-permute-start | bytes 3145736 | tf_op jit(solution)/shard_map/ppermute | solution.py:15
  304.7 68.2 %collective-permute-start.7 = (f32[1024,512]{1,0:T(8,128)S(1)}, f32[1024,512]{1,0:T(8,128)}, u32[]{:S(2)}, u32[]{:S(2)}) collective-permute-start(f32[1024,512]{1,0:T(8,128)S(1)} %convolution_add_fusion), channel_id=1, source_target_pairs={{8,0},{16,8},{24,16},{32,24},{40,32},{48,40},{56,48},{64,56},{72,6... | collective-permute-start | bytes 6291464 | tf_op jit(solution)/shard_map/ppermute | solution.py:15
  308.2 40.7 %collective-permute-start.4 = (bf16[1024,512]{1,0:T(8,128)(2,1)}, bf16[1024,512]{1,0:T(8,128)(2,1)}, u32[]{:S(2)}, u32[]{:S(2)}) collective-permute-start(bf16[1024,512]{1,0:T(8,128)(2,1)} %collective-permute-done.3), channel_id=1, source_target_pairs={{120,0},{0,8},{8,16},{16,24},{24,32},{32,40},{40,48},{48,56},{56,6... | collective-permute-start | bytes 3145736 | tf_op jit(solution)/shard_map/ppermute | solution.py:15
  349.0 97.1 %collective-permute-start.5 = (bf16[1024,512]{1,0:T(8,128)(2,1)}, bf16[1024,512]{1,0:T(8,128)(2,1)}, u32[]{:S(2)}, u32[]{:S(2)}) collective-permute-start(bf16[1024,512]{1,0:T(8,128)(2,1)} %collective-permute-done.4), channel_id=1, source_target_pairs={{120,0},{0,8},{8,16},{16,24},{24,32},{32,40},{40,48},{48,56},{56,6... | collective-permute-start | bytes 3145736 | tf_op jit(solution)/shard_map/ppermute | solution.py:15
  373.0 2.9 copy-start.5
  375.2 5.9 %copy-start.3 = (f32[1024,1024]{0,1:T(8,128)S(1)}, f32[1024,1024]{0,1:T(8,128)}, u32[]{:S(2)}) copy-start(f32[1024,1024]{0,1:T(8,128)} %all-gather.10.cloned.1.call-done) | copy-start | bytes 12582916
  375.2 76.4 %collective-permute-start.8 = (f32[1024,512]{1,0:T(8,128)S(1)}, f32[1024,512]{1,0:T(8,128)}, u32[]{:S(2)}, u32[]{:S(2)}) collective-permute-start(f32[1024,512]{1,0:T(8,128)S(1)} %add.77), channel_id=1, source_target_pairs={{8,0},{16,8},{24,16},{32,24},{40,32},{48,40},{56,48},{64,56},{72,6... | collective-permute-start | bytes 6291464 | tf_op jit(solution)/shard_map/ppermute | solution.py:15
  438.7 5.0 %copy-start.4 = (f32[1024,1024]{0,1:T(8,128)S(1)}, f32[1024,1024]{0,1:T(8,128)}, u32[]{:S(2)}) copy-start(f32[1024,1024]{0,1:T(8,128)} %all-gather.8.cloned.1.call-done) | copy-start | bytes 12582916
  438.7 7.4 %copy-start.7 = (f32[1024,512]{1,0:T(8,128)S(1)}, f32[1024,512]{1,0:T(8,128)}, u32[]{:S(2)}) copy-start(f32[1024,512]{1,0:T(8,128)} %fusion.27) | copy-start | bytes 6291460
  443.7 2.4 copy-start.1
  443.7 2.9 copy-start.6
Sparse Core Ops, SparseCore 0:
  9.6 98.8 all-gather.5
  178.4 47.7 all-gather.13
  228.4 71.0 all-gather.11
  301.0 67.3 all-gather.9
  369.9 68.6 all-gather.7

commit v11 on v8

--- a/solution.py
+++ b/solution.py
@@ -16,7 +16,7 @@
 
 
 def wide_dot(a, b):
-    return jnp.dot(a, b, precision=lax.Precision.HIGHEST, preferred_element_type=jnp.float32)
+    return jnp.dot(a, b, precision=lax.Precision.HIGH, preferred_element_type=jnp.float32)
 
 
 def per_device(queries, passages, teacher, positives):
@@ -36,15 +36,16 @@
 
     cols = jnp.concatenate(held_cols, 0)
     raw = jnp.einsum("qd,cd->qc", q_full, cols, preferred_element_type=jnp.float32)
-    gathered = lax.all_gather(raw, "width", axis=1, tiled=True)
-    gathered = gathered.reshape(rows, width, STEPS, sub)
+    gathered = [
+        lax.all_gather(raw[:, k * sub : (k + 1) * sub], "width", axis=1, tiled=True)
+        for k in range(STEPS)
+    ]
     scores = SCALE * raw
 
     index = positives[:, None]
     teach = teacher.astype(jnp.float32)
     column = lax.broadcasted_iota(jnp.int32, teach.shape, 1)
     t_pos = jnp.sum(jnp.where(column == index, teach, 0.0), 1, keepdims=True)
-    t_sum = jnp.sum(teach, 1, keepdims=True)
 
     local = lax.broadcasted_iota(jnp.int32, (1, STEPS * sub), 1)
     wcol = (local // sub) * rows + me * sub + local % sub
@@ -65,7 +66,7 @@
     grad_q = None
     terms = []
     for k in range(STEPS):
-        block_scores = SCALE * gathered[:, :, k, :].reshape(rows, rows)
+        block_scores = SCALE * gathered[k]
         errors = (s_pos - block_scores) - (t_pos - teach[:, k * rows : (k + 1) * rows])
         block_hit = (block_col + k * rows == index).astype(jnp.float32)
         block_slopes = coef * (block_hit * total - errors)

time: 478 us -> 452 us (0.946)
  other arithmetic: 53.5 us -> 21.8 us
  matrix products: 39.4 us -> 61.6 us
  local copies, waits for them, and re-layouts: 29.1 us -> 14.1 us
    mul x2 -> x0, other arithmetic: 25 us -> none  [the longest x1 12.7 us: per_device(): block_slopes = coef * (block_hit * total - errors)]
    dot_general x8, matrix products: 29.4 us -> 53.1 us  [wide_dot(): jnp.dot(a, b, precision=lax.Precision.HIGH, preferred_element_type=jnp.fl...]
    mul x4 -> x0, local copies, waits for them, and re-layouts: 21.5 us -> none  [per_device(): block_scores = SCALE * gathered[:, :, k, :].reshape(rows, rows)]
    convert_element_type x0 -> x1, other arithmetic: none -> 11.3 us  [per_device(): teach = teacher.astype(jnp.float32)]
    unnamed x1, other arithmetic: 10.4 us -> 0.01 us
    reduce_sum x1, other arithmetic: 9.57 us -> 1.77 us  [per_device(): row_part = jnp.sum(scores, 1) - jnp.sum(teach_cols, 1)]
    unnamed x7 -> x25, local copies, waits for them, and re-layouts: 6.94 us -> 12.1 us
    all_gather x1 -> x4, waiting for transfers between devices: 114 us -> 112 us  [per_device(): lax.all_gather(raw[:, k * sub:(k + 1) * sub], 'width', axis=1, tiled=True)]
  transfers between devices with their start and end apart: 11 -> 14, of which waited for: 8 -> 8; matrix products, arithmetic and copies ran while one was open for 13% -> 19% of each run, Pallas kernels for 0% -> 0%
where the time goes in v11:
time: 452 us; the launch traced here: 446 us
  waiting for transfers between devices  269 us (60%)
  matrix products  61.6 us (14%)
  blocking collectives  46.4 us (10%)
  other arithmetic  21.8 us (5%)
  starting transfers between devices  19.1 us (4%)
  between operations  14.5 us (3%)
  local copies, waits for them, and re-layouts  14.1 us (3%)
    ppermute x9, waiting for transfers between devices, shifted(): return lax.ppermute(block, axis, route)  155 us
    all_gather x4, waiting for transfers between devices, per_device(): lax.all_gather(raw[:, k * sub:(k + 1) * sub], 'width', axis=1, tiled=True)  112 us
    dot_general x8, matrix products, wide_dot(): jnp.dot(a, b, precision=lax.Precision.HIGH, preferred_element_type=jnp.fl...  53.1 us
    all_to_all x1, blocking collectives, per_device(): p_cols = lax.all_to_all(passages, 'width', 0, 1, tiled=True)  26.1 us
    psum x1, blocking collectives, per_device(): stats = lax.psum(jnp.stack([pos_part, row_part], 0), 'width')  20.3 us
    ppermute x9, starting transfers between devices, shifted(): return lax.ppermute(block, axis, route)  18.9 us
    unnamed x25, local copies, waits for them, and re-layouts  12.1 us
    convert_element_type x1, other arithmetic, per_device(): teach = teacher.astype(jnp.float32)  11.3 us
  transfers between devices with their start and end apart: 14, of which 8 were waited for; matrix products, arithmetic and copies ran while one was open for 19% of the time, Pallas kernels for 0%

profile of v11, /device:TPU:0, one launch (start us, length us, event | category | flops | bytes accessed | tf_op | source)
XLA Modules:
  0.0 446.3 jit_solution(10487407789075406779)
XLA Ops:
  7.2 0.0 copy-start.3
  7.2 0.0 all-gather.6.cloned.1.call-start
  7.2 0.7 all-gather.6.cloned.1.call-update
  7.9 0.0 all-gather.14.cloned.1.call-start
  8.0 26.1 %all_to_all.19 = bf16[8,128,512]{2,1,0:T(8,128)(2,1)S(1)} all-to-all(bf16[8,128,512]{2,1,0:T(8,128)(2,1)} %bitcast.23), channel_id=1, replica_groups=mesh['loop'=16,'width'=8] {'width'}, dimensions={0} | all-to-all | bytes 2097152 | tf_op jit(solution)/shard_map/all_to_all | solution.py:30
  34.1 0.7 copy.8
  34.7 0.1 collective-permute-start
  34.8 40.4 %collective-permute-done = bf16[128,4096]{0,1:T(8,128)(2,1)S(1)} collective-permute-done((bf16[128,4096]{0,1:T(8,128)(2,1)S(1)}, bf16[128,4096]{0,1:T(8,128)(2,1)S(1)}, u32[]{:S(2)}, u32[]{:S(2)}) %collective-permute-start) | collective-permute-done | bytes 1048608 | tf_op jit(solution)/shard_map/ppermute | solution.py:15
  75.2 0.0 collective-permute-start.1
  75.2 40.4 %collective-permute-done.1 = bf16[128,4096]{0,1:T(8,128)(2,1)S(1)} collective-permute-done((bf16[128,4096]{0,1:T(8,128)(2,1)S(1)}, bf16[128,4096]{0,1:T(8,128)(2,1)S(1)}, u32[]{:S(2)}, u32[]{:S(2)}) %collective-permute-start.1) | collective-permute-done | bytes 1048608 | tf_op jit(solution)/shard_map/ppermute | solution.py:15
  115.7 0.0 collective-permute-start.2
  115.7 28.3 %collective-permute-done.2 = bf16[128,4096]{0,1:T(8,128)(2,1)} collective-permute-done((bf16[128,4096]{0,1:T(8,128)(2,1)S(1)}, bf16[128,4096]{0,1:T(8,128)(2,1)}, u32[]{:S(2)}, u32[]{:S(2)}) %collective-permute-start.2) | collective-permute-done | bytes 1048608 | tf_op jit(solution)/shard_map/ppermute | solution.py:15
  144.0 0.0 copy-done.3
  144.0 8.5 %select_reduce_fusion.1 = (f32[1024]{0:T(1024)S(1)}, f32[1024]{0:T(1024)S(1)}, f32[1024,512]{0,1:T(8,128)S(1)}) fusion(s32[1024]{0:T(1024)S(1)} %copy-done.3, s32[512]{0:T(512)S(1)} %fusion.29, bf16[1024,4096]{1,0:T(8,128)(2,1)} %all-gather.6.cloned.1.call-done, bf16[128,4096]{0,1:T(8,128)(2,1)} %collective-permute-done.2, ...), kind=kOutput, calls=%fused_computation.29 | convolution fusion | flops 4314363904 | bytes 14694400 | tf_op jit(solution)/shard_map/qd,cd->qc/dot_general | solution.py:38
  152.5 0.0 copy-start
  152.5 1.4 fusion.48
  153.8 0.0 all-gather.14.cloned.1.call-update
  153.9 0.0 all-gather.12.cloned.1.call-start
  153.9 0.7 all-gather.12.cloned.1.call-update
  154.6 0.0 all-gather.8.cloned.1.call-start
  154.6 0.5 all-gather.8.cloned.1.call-update
  155.2 0.0 all-gather.10.cloned.1.call-start
  155.2 0.5 all-gather.10.cloned.1.call-update
  155.8 0.0 copy-done
  155.8 0.2 collective-permute-start.3
  156.0 12.1 %copy.9 = bf16[1024,4096]{0,1:T(8,128)(2,1)} copy(bf16[1024,4096]{1,0:T(8,128)(2,1)} %param.6) | data formatting | bytes 16777216 | tf_op args[2]
  168.1 11.3 %convert_element_type.2 = f32[1024,4096]{0,1:T(8,128)} convert(bf16[1024,4096]{0,1:T(8,128)(2,1)} %copy.9) | non-fusion elementwise | flops 4194304 | bytes 25165824 | tf_op jit(solution)/shard_map/convert_element_type | solution.py:46
  179.4 1.8 dynamic-slice_reduce_fusion
  181.2 0.0 copy-start.1
  181.2 6.4 %select_reduce_fusion = f32[1024]{0:T(1024)S(1)} fusion(s32[1024]{0:T(1024)S(1)} %copy-done.3, bf16[1024,4096]{0,1:T(8,128)(2,1)} %copy.9), kind=kLoop, calls=%fused_computation | loop fusion | flops 16776192 | bytes 8396800 | tf_op jit(solution)/shard_map/reduce_sum | solution.py:48
  187.6 20.3 %psum.7 = f32[2,1024]{1,0:T(2,128)S(1)} all-reduce(f32[2,1024]{1,0:T(2,128)S(1)} %pad_maximum_fusion), channel_id=1, replica_groups=mesh['loop'=16,'width'=8] {'width'}, use_global_device_ids=true, to_apply=%region_3.4 | all-reduce | flops 2048 | bytes 16384 | tf_op jit(solution)/shard_map/psum | solution.py:59
  208.0 0.0 all-gather.14.cloned.1.call-done
  208.0 0.0 copy-done.1
  208.0 7.4 %fusion.41 = f32[1024,512]{1,0:T(8,128)} fusion(bf16[1024,512]{1,0:T(8,128)(2,1)S(1)} %copy-done.1, f32[1024,4096]{0,1:T(8,128)} %convert_element_type.2, f32[1024,1024]{0,1:T(8,128)} %all-gather.14.cloned.1.call-done, f32[1024]{0:T(1024)S(1)} %select_reduce_fusion, f32[1024]{0:T(1024)S(1)} %bitcast.28, f32[1024]{0:T(1024)S(1)} %multiply_subtract_fusion, ...), kind=kOutput, calls=%fused_computation.56 | convolution fusion | flops 3229614080 | bytes 11554816 | tf_op jit(solution)/shard_map/dot_general | solution.py:19
  215.4 10.3 %collective-permute-start.6 = (f32[1024,512]{1,0:T(8,128)}, f32[1024,512]{1,0:T(8,128)}, u32[]{:S(2)}, u32[]{:S(2)}) collective-permute-start(f32[1024,512]{1,0:T(8,128)} %fusion.41), channel_id=1, source_target_pairs={{8,0},{16,8},{24,16},{32,24},{40,32},{48,40},{56,48},{64,56},{72,6... | collective-permute-start | bytes 6291464 | tf_op jit(solution)/shard_map/ppermute | solution.py:15
  225.7 0.0 collective-permute-done.3
  225.7 0.0 collective-permute-start.4
  225.7 40.2 %collective-permute-done.4 = bf16[1024,512]{1,0:T(8,128)(2,1)} collective-permute-done((bf16[1024,512]{1,0:T(8,128)(2,1)}, bf16[1024,512]{1,0:T(8,128)(2,1)}, u32[]{:S(2)}, u32[]{:S(2)}) %collective-permute-start.4) | collective-permute-done | bytes 1048608 | tf_op jit(solution)/shard_map/ppermute | solution.py:15
  265.9 0.0 collective-permute-start.5
  265.9 20.7 %all-gather.12.cloned.1.call-done = f32[1024,1024]{0,1:T(8,128)} async-done(((f32[1024,128]{0,1:T(8,128)}), f32[1024,1024]{0,1:T(8,128)}) %all-gather.12.cloned.1.call-update) | async-done | bytes 4194320 | tf_op jit(solution)/shard_map/all_gather | solution.py:40
  286.6 0.0 collective-permute-done.6
  286.6 8.0 %convolution_add_fusion = f32[1024,512]{1,0:T(8,128)} fusion(f32[1024,512]{1,0:T(8,128)} %collective-permute-done.6, bf16[1024,512]{1,0:T(8,128)(2,1)S(1)} %copy-done.1, f32[1024,4096]{0,1:T(8,128)} %convert_element_type.2, f32[1024,1024]{0,1:T(8,128)} %all-gather.12.cloned.1.call-done, f32[1024]{0:T(1024)S(1)} %select_reduce_fusion, ...), kind=kOutput, calls=%fused_computation.32 | convolution fusion | flops 3230138368 | bytes 13651968 | tf_op jit(solution)/shard_map/dot_general | solution.py:19
  294.6 3.6 collective-permute-start.7
  298.3 54.5 %all-gather.8.cloned.1.call-done = f32[1024,1024]{0,1:T(8,128)} async-done(((f32[1024,128]{0,1:T(8,128)}), f32[1024,1024]{0,1:T(8,128)}) %all-gather.8.cloned.1.call-update) | async-done | bytes 4194320 | tf_op jit(solution)/shard_map/all_gather | solution.py:40
  352.8 7.7 %fusion.36 = f32[1024,512]{1,0:T(8,128)} fusion(bf16[1024,512]{1,0:T(8,128)(2,1)S(1)} %copy-done, f32[1024,4096]{0,1:T(8,128)} %convert_element_type.2, f32[1024,1024]{0,1:T(8,128)} %all-gather.8.cloned.1.call-done, f32[1024]{0:T(1024)S(1)} %select_reduce_fusion, f32[1024]{0:T(1024)S(1)} %bitcast.30, f32[1024]{0:T(1024)S(1)} %multiply_subtract_fusion, ...), kind=kOutput, calls=%fused_computation.54 | convolution fusion | flops 3229614080 | bytes 11550720 | tf_op jit(solution)/shard_map/dot_general | solution.py:19
  360.5 0.0 copy-done.6
  360.5 6.7 %fusion.39 = f32[1024,512]{1,0:T(8,128)} fusion(bf16[1024,512]{1,0:T(8,128)(2,1)} %collective-permute-done.4, f32[1024,4096]{0,1:T(8,128)} %convert_element_type.2, f32[1024,1024]{0,1:T(8,128)S(1)} %copy-done.6, f32[1024]{0:T(1024)S(1)} %select_reduce_fusion, f32[1024]{0:T(1024)S(1)} %bitcast.31, f32[1024]{0:T(1024)S(1)} %multiply_subtract_fusion, ...), kind=kOutput, calls=%fused_computation.55 | convolution fusion | flops 3229614080 | bytes 11554816 | tf_op jit(solution)/shard_map/dot_general | solution.py:19
  367.2 36.3 %all-gather.10.cloned.1.call-done = f32[1024,1024]{0,1:T(8,128)} async-done(((f32[1024,128]{0,1:T(8,128)}), f32[1024,1024]{0,1:T(8,128)}) %all-gather.10.cloned.1.call-update) | async-done | bytes 4194320 | tf_op jit(solution)/shard_map/all_gather | solution.py:40
  403.5 0.0 copy-done.2
  403.5 5.4 %fusion.44 = f32[1024,512]{1,0:T(8,128)S(1)} fusion(bf16[1024,512]{1,0:T(8,128)(2,1)S(1)} %copy-done.2, f32[1024,4096]{0,1:T(8,128)} %convert_element_type.2, f32[1024,1024]{0,1:T(8,128)} %all-gather.10.cloned.1.call-done, f32[1024]{0:T(1024)S(1)} %select_reduce_fusion, f32[1024]{0:T(1024)S(1)} %bitcast.32, f32[1024]{0:T(1024)S(1)} %multiply_subtract_fusion, ...), kind=kOutput, calls=%fused_computation.57 | convolution fusion | flops 3229614080 | bytes 11554816 | tf_op jit(solution)/shard_map/dot_general | solution.py:19
  408.8 0.0 slice-start.2
  408.8 0.0 collective-permute-done.7
  408.9 0.5 add.95
  409.3 0.0 slice-start.3
  409.4 0.0 copy-start.7
  409.4 4.7 %collective-permute-start.8 = (f32[1024,512]{1,0:T(8,128)S(1)}, f32[1024,512]{1,0:T(8,128)S(1)}, u32[]{:S(2)}, u32[]{:S(2)}) collective-permute-start(f32[1024,512]{1,0:T(8,128)S(1)} %add.95), channel_id=1, source_target_pairs={{8,0},{16,8},{24,16},{32,24},{40,32},{48,40},{56,48},{64,56},{72,6... | collective-permute-start | bytes 6291464 | tf_op jit(solution)/shard_map/ppermute | solution.py:15
  414.0 0.0 copy-done.5
  414.0 4.9 %fusion.34 = f32[1024,512]{1,0:T(8,128)S(1)} fusion(bf16[1024,512]{1,0:T(8,128)(2,1)S(1)} %copy-done.2, f32[1024,4096]{0,1:T(8,128)} %convert_element_type.2, f32[1024,1024]{0,1:T(8,128)S(1)} %copy-done.5, f32[1024]{0:T(1024)S(1)} %select_reduce_fusion, f32[1024]{0:T(1024)S(1)} %bitcast.33, f32[1024]{0:T(1024)S(1)} %multiply_subtract_fusion, ...), kind=kOutput, calls=%fused_computation.53 | convolution fusion | flops 3229614080 | bytes 11550720 | tf_op jit(solution)/shard_map/dot_general | solution.py:19
  419.0 0.0 slice-done
  419.0 5.5 %fusion.46 = f32[1024,512]{1,0:T(8,128)} fusion(bf16[1024,512]{1,0:T(8,128)(2,1)} %collective-permute-done.3, f32[1024,4096]{0,1:T(8,128)S(1)} %bitcast.21, f32[1024,1024]{0,1:T(8,128)S(1)} %copy-done.7, f32[1024]{0:T(1024)S(1)} %select_reduce_fusion, f32[1024]{0:T(1024)S(1)} %bitcast.34, f32[1024]{0:T(1024)S(1)} %multiply_subtract_fusion, ...), kind=kOutput, calls=%fused_computation.58 | convolution fusion | flops 3229614080 | bytes 11554816 | tf_op jit(solution)/shard_map/dot_general | solution.py:19
  424.6 0.0 collective-permute-done.5
  424.6 7.4 %add_add_fusion = f32[1024,512]{1,0:T(8,128)} fusion(f32[1024,512]{1,0:T(8,128)} %fusion.39, f32[1024,512]{1,0:T(8,128)} %fusion.36, f32[1024,512]{1,0:T(8,128)} %fusion.46, bf16[1024,512]{1,0:T(8,128)(2,1)} %collective-permute-done.5, f32[1024,4096]{0,1:T(8,128)S(1)} %bitcast.21, f32[1024,1024]{0,1:T(8,128)S(1)} %copy-done.4, ...), kind=kOutput, calls=%fused_computation.27 | convolution fusion | flops 3231186944 | bytes 17846272 | tf_op jit(solution)/shard_map/dot_general | solution.py:19
  432.0 5.6 %collective-permute-done.8 = f32[1024,512]{1,0:T(8,128)S(1)} collective-permute-done((f32[1024,512]{1,0:T(8,128)S(1)}, f32[1024,512]{1,0:T(8,128)S(1)}, u32[]{:S(2)}, u32[]{:S(2)}) %collective-permute-start.8) | collective-permute-done | bytes 2097184 | tf_op jit(solution)/shard_map/ppermute | solution.py:15
  437.6 1.8 add.96
  (21 shorter events, 0.1 us)
Async XLA Ops:
  7.2 136.8 %copy-start.3 = (s32[1024]{0:T(1024)S(1)}, s32[1024]{0:T(1024)}, u32[]{:S(2)}) copy-start(s32[1024]{0:T(1024)} %param.7) | copy-start | bytes 12292
  7.2 136.8 %all-gather.6.cloned.1.call-start = ((), (), s32[]{:S(2)}) async-start(), calls=%async_computation.1 | async-start | bytes 9437184 | tf_op jit(solution)/shard_map/all_gather | solution.py:29
  7.9 200.1 %all-gather.14.cloned.1.call-start = ((), (), s32[]{:S(2)}) async-start(), calls=%async_computation.5 | async-start | bytes 4718592 | tf_op jit(solution)/shard_map/all_gather | solution.py:40
  34.7 40.5 %collective-permute-start = (bf16[128,4096]{0,1:T(8,128)(2,1)S(1)}, bf16[128,4096]{0,1:T(8,128)(2,1)S(1)}, u32[]{:S(2)}, u32[]{:S(2)}) collective-permute-start(bf16[128,4096]{0,1:T(8,128)(2,1)S(1)} %bitcast.24), channel_id=1, source_target_pairs={{120,0},{0,8},{8,16},{16,24},{24,32},{32,40},{40,48},{48,56},{56,6... | collective-permute-start | bytes 3145736 | tf_op jit(solution)/shard_map/ppermute | solution.py:15
  75.2 40.4 %collective-permute-start.1 = (bf16[128,4096]{0,1:T(8,128)(2,1)S(1)}, bf16[128,4096]{0,1:T(8,128)(2,1)S(1)}, u32[]{:S(2)}, u32[]{:S(2)}) collective-permute-start(bf16[128,4096]{0,1:T(8,128)(2,1)S(1)} %collective-permute-done), channel_id=1, source_target_pairs={{120,0},{0,8},{8,16},{16,24},{24,32},{32,40},{40,48},{48,56},{56,6... | collective-permute-start | bytes 3145736 | tf_op jit(solution)/shard_map/ppermute | solution.py:15
  115.7 28.3 %collective-permute-start.2 = (bf16[128,4096]{0,1:T(8,128)(2,1)S(1)}, bf16[128,4096]{0,1:T(8,128)(2,1)}, u32[]{:S(2)}, u32[]{:S(2)}) collective-permute-start(bf16[128,4096]{0,1:T(8,128)(2,1)S(1)} %collective-permute-done.1), channel_id=1, source_target_pairs={{120,0},{0,8},{8,16},{16,24},{24,32},{32,40},{40,48},{48,56},{56,6... | collective-permute-start | bytes 3145736 | tf_op jit(solution)/shard_map/ppermute | solution.py:15
  152.5 3.3 copy-start
  153.9 132.7 %all-gather.12.cloned.1.call-start = ((), (), s32[]{:S(2)}) async-start(), calls=%async_computation.4 | async-start | bytes 4718592 | tf_op jit(solution)/shard_map/all_gather | solution.py:40
  154.6 198.2 %all-gather.8.cloned.1.call-start = ((), (), s32[]{:S(2)}) async-start(), calls=%async_computation.2 | async-start | bytes 4718592 | tf_op jit(solution)/shard_map/all_gather | solution.py:40
  155.2 248.3 %all-gather.10.cloned.1.call-start = ((), (), s32[]{:S(2)}) async-start(), calls=%async_computation.3 | async-start | bytes 4718592 | tf_op jit(solution)/shard_map/all_gather | solution.py:40
  155.8 69.9 %collective-permute-start.3 = (bf16[1024,512]{1,0:T(8,128)(2,1)S(1)}, bf16[1024,512]{1,0:T(8,128)(2,1)}, u32[]{:S(2)}, u32[]{:S(2)}) collective-permute-start(bf16[1024,512]{1,0:T(8,128)(2,1)S(1)} %copy-done), channel_id=1, source_target_pairs={{120,0},{0,8},{8,16},{16,24},{24,32},{32,40},{40,48},{48,56},{56,6... | collective-permute-start | bytes 3145736 | tf_op jit(solution)/shard_map/ppermute | solution.py:15
  181.2 26.8 %copy-start.1 = (bf16[1024,512]{1,0:T(8,128)(2,1)S(1)}, bf16[1024,512]{1,0:T(8,128)(2,1)}, u32[]{:S(2)}) copy-start(bf16[1024,512]{1,0:T(8,128)(2,1)} %param.4) | copy-start | bytes 3145732
  215.4 71.2 %collective-permute-start.6 = (f32[1024,512]{1,0:T(8,128)}, f32[1024,512]{1,0:T(8,128)}, u32[]{:S(2)}, u32[]{:S(2)}) collective-permute-start(f32[1024,512]{1,0:T(8,128)} %fusion.41), channel_id=1, source_target_pairs={{8,0},{16,8},{24,16},{32,24},{40,32},{48,40},{56,48},{64,56},{72,6... | collective-permute-start | bytes 6291464 | tf_op jit(solution)/shard_map/ppermute | solution.py:15
  225.7 40.2 %collective-permute-start.4 = (bf16[1024,512]{1,0:T(8,128)(2,1)}, bf16[1024,512]{1,0:T(8,128)(2,1)}, u32[]{:S(2)}, u32[]{:S(2)}) collective-permute-start(bf16[1024,512]{1,0:T(8,128)(2,1)} %collective-permute-done.3), channel_id=1, source_target_pairs={{120,0},{0,8},{8,16},{16,24},{24,32},{32,40},{40,48},{48,56},{56,6... | collective-permute-start | bytes 3145736 | tf_op jit(solution)/shard_map/ppermute | solution.py:15
  265.9 158.6 %collective-permute-start.5 = (bf16[1024,512]{1,0:T(8,128)(2,1)}, bf16[1024,512]{1,0:T(8,128)(2,1)}, u32[]{:S(2)}, u32[]{:S(2)}) collective-permute-start(bf16[1024,512]{1,0:T(8,128)(2,1)} %collective-permute-done.4), channel_id=1, source_target_pairs={{120,0},{0,8},{8,16},{16,24},{24,32},{32,40},{40,48},{48,56},{56,6... | collective-permute-start | bytes 3145736 | tf_op jit(solution)/shard_map/ppermute | solution.py:15
  294.6 114.2 %collective-permute-start.7 = (f32[1024,512]{1,0:T(8,128)}, f32[1024,512]{1,0:T(8,128)S(1)}, u32[]{:S(2)}, u32[]{:S(2)}) collective-permute-start(f32[1024,512]{1,0:T(8,128)} %convolution_add_fusion), channel_id=1, source_target_pairs={{8,0},{16,8},{24,16},{32,24},{40,32},{48,40},{56,48},{64,56},{72,6... | collective-permute-start | bytes 6291464 | tf_op jit(solution)/shard_map/ppermute | solution.py:15
  352.8 7.7 %copy-start.6 = (f32[1024,1024]{0,1:T(8,128)S(1)}, f32[1024,1024]{0,1:T(8,128)}, u32[]{:S(2)}) copy-start(f32[1024,1024]{0,1:T(8,128)} %all-gather.12.cloned.1.call-done) | copy-start | bytes 12582916
  360.5 43.0 %copy-start.2 = (bf16[1024,512]{1,0:T(8,128)(2,1)S(1)}, bf16[1024,512]{1,0:T(8,128)(2,1)}, u32[]{:S(2)}) copy-start(bf16[1024,512]{1,0:T(8,128)(2,1)} %param.4) | copy-start | bytes 3145732
  403.5 10.6 %copy-start.5 = (f32[1024,1024]{0,1:T(8,128)S(1)}, f32[1024,1024]{0,1:T(8,128)}, u32[]{:S(2)}) copy-start(f32[1024,1024]{0,1:T(8,128)} %all-gather.8.cloned.1.call-done) | copy-start | bytes 12582916
  403.5 15.5 %slice-start = ((s8[16777216]{0:T(1024)(128)(4,1)}), s8[4194304]{0:T(1024)(128)(4,1)S(1)}, s32[]{:S(2)}) async-start(s8[16777216]{0:T(1024)(128)(4,1)} %bitcast.20), calls=%async_computation.6 | async-start | bytes 8388608
  403.5 15.5 %slice-start.1 = ((s8[16777216]{0:T(1024)(128)(4,1)}), s8[4194304]{0:T(1024)(128)(4,1)S(1)}, s32[]{:S(2)}) async-start(s8[16777216]{0:T(1024)(128)(4,1)} %bitcast.20), calls=%async_computation.7 | async-start | bytes 8388608
  408.8 10.1 %slice-start.2 = ((s8[16777216]{0:T(1024)(128)(4,1)}), s8[4194304]{0:T(1024)(128)(4,1)S(1)}, s32[]{:S(2)}) async-start(s8[16777216]{0:T(1024)(128)(4,1)} %bitcast.20), calls=%async_computation.8 | async-start | bytes 8388608
  409.3 9.6 %slice-start.3 = ((s8[16777216]{0:T(1024)(128)(4,1)}), s8[4194304]{0:T(1024)(128)(4,1)S(1)}, s32[]{:S(2)}) async-start(s8[16777216]{0:T(1024)(128)(4,1)} %bitcast.20), calls=%async_computation.9 | async-start | bytes 8388608
  409.4 9.6 %copy-start.7 = (f32[1024,1024]{0,1:T(8,128)S(1)}, f32[1024,1024]{0,1:T(8,128)}, u32[]{:S(2)}) copy-start(f32[1024,1024]{0,1:T(8,128)} %all-gather.10.cloned.1.call-done) | copy-start | bytes 12582916
  409.4 28.2 %collective-permute-start.8 = (f32[1024,512]{1,0:T(8,128)S(1)}, f32[1024,512]{1,0:T(8,128)S(1)}, u32[]{:S(2)}, u32[]{:S(2)}) collective-permute-start(f32[1024,512]{1,0:T(8,128)S(1)} %add.95), channel_id=1, source_target_pairs={{8,0},{16,8},{24,16},{32,24},{40,32},{48,40},{56,48},{64,56},{72,6... | collective-permute-start | bytes 6291464 | tf_op jit(solution)/shard_map/ppermute | solution.py:15
  419.0 5.6 %copy-start.4 = (f32[1024,1024]{0,1:T(8,128)S(1)}, f32[1024,1024]{0,1:T(8,128)}, u32[]{:S(2)}) copy-start(f32[1024,1024]{0,1:T(8,128)} %all-gather.14.cloned.1.call-done) | copy-start | bytes 12582916
Sparse Core Ops, SparseCore 0:
  9.6 98.8 all-gather.5
  154.0 50.5 all-gather.13
  206.8 79.7 all-gather.11
  288.1 64.6 all-gather.7
  354.3 49.1 all-gather.9

commit v12 on v11

--- a/solution.py
+++ b/solution.py
@@ -13,6 +13,11 @@
     devices = range(lax.axis_size(axis))
     route = [((i - distance) % len(devices), i) for i in devices]
     return lax.ppermute(block, axis, route)
+
+
+def after(value, dep):
+    zero = 0.0 * dep[:1, :1]
+    return value + zero.astype(value.dtype)
 
 
 def wide_dot(a, b):
@@ -36,10 +41,12 @@
 
     cols = jnp.concatenate(held_cols, 0)
     raw = jnp.einsum("qd,cd->qc", q_full, cols, preferred_element_type=jnp.float32)
-    gathered = [
-        lax.all_gather(raw[:, k * sub : (k + 1) * sub], "width", axis=1, tiled=True)
-        for k in range(STEPS)
-    ]
+    gathered = [None] * STEPS
+    for k in range(STEPS - 1, -1, -1):
+        piece = raw[:, k * sub : (k + 1) * sub]
+        if k < STEPS - 1:
+            piece = after(piece, gathered[k + 1])
+        gathered[k] = lax.all_gather(piece, "width", axis=1, tiled=True)
     scores = SCALE * raw
 
     index = positives[:, None]

time: 452 us -> 474 us (1.049)
  waiting for transfers between devices: 269 us -> 299 us
  matrix products: 61.6 us -> 50.2 us
  local copies, waits for them, and re-layouts: 14.1 us -> 19.1 us
    ppermute x9, waiting for transfers between devices: 155 us -> 195 us  [shifted(): return lax.ppermute(block, axis, route)]
    dot_general x8, matrix products: 53.1 us -> 41 us  [wide_dot(): jnp.dot(a, b, precision=lax.Precision.HIGH, preferred_element_type=jnp.fl...]
    all_gather x4, waiting for transfers between devices: 112 us -> 103 us  [per_device(): gathered[k] = lax.all_gather(piece, 'width', axis=1, tiled=True)]
    unnamed x25 -> x35, local copies, waits for them, and re-layouts: 12.1 us -> 14.1 us
  transfers between devices with their start and end apart: 14 -> 14, of which waited for: 8 -> 10; matrix products, arithmetic and copies ran while one was open for 19% -> 15% of each run, Pallas kernels for 0% -> 0%
where the time goes in v12:
time: 474 us; the launch traced here: 471 us
  waiting for transfers between devices  299 us (63%)
  matrix products  50.2 us (11%)
  blocking collectives  44.8 us (9%)
  other arithmetic  25.9 us (5%)
  local copies, waits for them, and re-layouts  19.1 us (4%)
  starting transfers between devices  16.3 us (3%)
  between operations  16 us (3%)
    ppermute x9, waiting for transfers between devices, shifted(): return lax.ppermute(block, axis, route)  195 us
    all_gather x4, waiting for transfers between devices, per_device(): gathered[k] = lax.all_gather(piece, 'width', axis=1, tiled=True)  103 us
    dot_general x8, matrix products, wide_dot(): jnp.dot(a, b, precision=lax.Precision.HIGH, preferred_element_type=jnp.fl...  41 us
    all_to_all x1, blocking collectives, per_device(): p_cols = lax.all_to_all(passages, 'width', 0, 1, tiled=True)  26.1 us
    psum x1, blocking collectives, per_device(): stats = lax.psum(jnp.stack([pos_part, row_part], 0), 'width')  18.7 us
    ppermute x9, starting transfers between devices, shifted(): return lax.ppermute(block, axis, route)  15.9 us
    unnamed x35, local copies, waits for them, and re-layouts  14.1 us
    convert_element_type x1, other arithmetic, per_device(): teach = teacher.astype(jnp.float32)  11.3 us
  transfers between devices with their start and end apart: 14, of which 10 were waited for; matrix products, arithmetic and copies ran while one was open for 15% of the time, Pallas kernels for 0%

profile of v12, /device:TPU:0, one launch (start us, length us, event | category | flops | bytes accessed | tf_op | source)
XLA Modules:
  0.0 471.4 jit_solution(8519880825523694834)
XLA Ops:
  7.2 0.0 all-gather.6.cloned.1.call-start
  7.2 0.7 all-gather.6.cloned.1.call-update
  7.9 0.0 all-gather.8.cloned.1.call-start
  8.0 26.1 %all_to_all.19 = bf16[8,128,512]{2,1,0:T(8,128)(2,1)S(1)} all-to-all(bf16[8,128,512]{2,1,0:T(8,128)(2,1)} %bitcast.26), channel_id=1, replica_groups=mesh['loop'=16,'width'=8] {'width'}, dimensions={0} | all-to-all | bytes 2097152 | tf_op jit(solution)/shard_map/all_to_all | solution.py:35
  34.1 0.7 copy.8
  34.7 0.1 collective-permute-start
  34.8 40.4 %collective-permute-done = bf16[128,4096]{0,1:T(8,128)(2,1)S(1)} collective-permute-done((bf16[128,4096]{0,1:T(8,128)(2,1)S(1)}, bf16[128,4096]{0,1:T(8,128)(2,1)S(1)}, u32[]{:S(2)}, u32[]{:S(2)}) %collective-permute-start) | collective-permute-done | bytes 1048608 | tf_op jit(solution)/shard_map/ppermute | solution.py:15
  75.2 1.0 copy-done.8
  76.3 0.0 collective-permute-start.1
  76.3 40.4 %collective-permute-done.1 = bf16[128,4096]{0,1:T(8,128)(2,1)S(1)} collective-permute-done((bf16[128,4096]{0,1:T(8,128)(2,1)S(1)}, bf16[128,4096]{0,1:T(8,128)(2,1)S(1)}, u32[]{:S(2)}, u32[]{:S(2)}) %collective-permute-start.1) | collective-permute-done | bytes 1048608 | tf_op jit(solution)/shard_map/ppermute | solution.py:15
  116.7 0.0 collective-permute-start.2
  116.7 27.2 %collective-permute-done.2 = bf16[128,4096]{0,1:T(8,128)(2,1)S(1)} collective-permute-done((bf16[128,4096]{0,1:T(8,128)(2,1)S(1)}, bf16[128,4096]{0,1:T(8,128)(2,1)S(1)}, u32[]{:S(2)}, u32[]{:S(2)}) %collective-permute-start.2) | collective-permute-done | bytes 1048608 | tf_op jit(solution)/shard_map/ppermute | solution.py:15
  143.9 1.0 copy-done.10
  144.9 9.1 %select_reduce_fusion.1 = (f32[1024]{0:T(1024)S(1)}, f32[1024]{0:T(1024)S(1)}, f32[1024,512]{0,1:T(8,128)S(1)}) fusion(s32[1024]{0:T(1024)S(1)} %copy-done.3, s32[512]{0:T(512)S(1)} %fusion.29, bf16[1024,4096]{1,0:T(8,128)(2,1)} %all-gather.6.cloned.1.call-done, bf16[128,4096]{0,1:T(8,128)(2,1)} %copy-done.10, bf16[128,4096]{0,1:T(8,128)(2,1)} %copy-done.9, ...), kind=kOutput, calls=%fused_computation.29 | convolution fusion | flops 4314363904 | bytes 14694400 | tf_op jit(solution)/shard_map/qd,cd->qc/dot_general | solution.py:43
  154.0 0.8 slice.57
  154.8 0.0 all-gather.8.cloned.1.call-update
  154.9 0.0 all-gather.10.cloned.1.call-start
  154.9 50.1 %all-gather.8.cloned.1.call-done = f32[1024,1024]{0,1:T(8,128)} async-done(((f32[1024,128]{0,1:T(8,128)}), f32[1024,1024]{0,1:T(8,128)}) %all-gather.8.cloned.1.call-update) | async-done | bytes 4194320 | tf_op jit(solution)/shard_map/all_gather | solution.py:49
  205.0 1.2 slice.58
  206.8 0.8 slice_add_fusion
  207.6 0.0 all-gather.10.cloned.1.call-update
  207.7 0.0 all-gather.12.cloned.1.call-start
  207.7 51.4 %all-gather.10.cloned.1.call-done = f32[1024,1024]{0,1:T(8,128)} async-done(((f32[1024,128]{0,1:T(8,128)}), f32[1024,1024]{0,1:T(8,128)}) %all-gather.10.cloned.1.call-update) | async-done | bytes 4194320 | tf_op jit(solution)/shard_map/all_gather | solution.py:49
  259.1 1.2 slice.59
  261.0 0.8 slice_add_fusion.1
  261.8 0.0 all-gather.12.cloned.1.call-update
  261.8 0.2 all-gather.14.cloned.1.call-start
  262.1 12.0 %copy.9 = bf16[1024,4096]{0,1:T(8,128)(2,1)} copy(bf16[1024,4096]{1,0:T(8,128)(2,1)} %param.6) | data formatting | bytes 16777216 | tf_op args[2]
  274.1 11.3 %convert_element_type.2 = f32[1024,4096]{0,1:T(8,128)} convert(bf16[1024,4096]{0,1:T(8,128)(2,1)} %copy.9) | non-fusion elementwise | flops 4194304 | bytes 25165824 | tf_op jit(solution)/shard_map/convert_element_type | solution.py:53
  285.4 1.8 dynamic-slice_reduce_fusion
  287.2 0.0 copy-start
  287.2 6.4 %select_reduce_fusion = f32[1024]{0:T(1024)S(1)} fusion(s32[1024]{0:T(1024)S(1)} %copy-done.3, bf16[1024,4096]{0,1:T(8,128)(2,1)} %copy.9), kind=kLoop, calls=%fused_computation | loop fusion | flops 16776192 | bytes 8396800 | tf_op jit(solution)/shard_map/reduce_sum | solution.py:55
  293.6 18.7 %psum.7 = f32[2,1024]{1,0:T(2,128)S(1)} all-reduce(f32[2,1024]{1,0:T(2,128)S(1)} %pad_maximum_fusion), channel_id=1, replica_groups=mesh['loop'=16,'width'=8] {'width'}, use_global_device_ids=true, to_apply=%region_3.4 | all-reduce | flops 2048 | bytes 16384 | tf_op jit(solution)/shard_map/psum | solution.py:66
  312.3 1.7 all-gather.12.cloned.1.call-done
  314.0 1.2 slice.60
  315.8 0.8 slice_add_fusion.2
  316.7 0.0 all-gather.14.cloned.1.call-update
  316.7 0.0 copy-start.1
  316.7 0.0 slice-start
  316.7 0.0 slice-start.1
  316.7 5.5 %fusion.41 = f32[1024,512]{1,0:T(8,128)S(1)} fusion(bf16[1024,512]{1,0:T(8,128)(2,1)S(1)} %copy-done, f32[1024,4096]{0,1:T(8,128)} %convert_element_type.2, f32[1024,1024]{0,1:T(8,128)} %all-gather.8.cloned.1.call-done, f32[1024]{0:T(1024)S(1)} %select_reduce_fusion, f32[1024]{0:T(1024)S(1)} %bitcast.31, f32[1024]{0:T(1024)S(1)} %multiply_subtract_fusion, ...), kind=kOutput, calls=%fused_computation.59 | convolution fusion | flops 3229614080 | bytes 11554816 | tf_op jit(solution)/shard_map/dot_general | solution.py:24
  322.2 4.4 collective-permute-start.6
  326.6 0.0 collective-permute-start.3
  326.6 0.0 slice-start.2
  326.6 0.0 slice-start.3
  326.7 58.9 %collective-permute-done.6 = f32[1024,512]{1,0:T(8,128)S(1)} collective-permute-done((f32[1024,512]{1,0:T(8,128)S(1)}, f32[1024,512]{1,0:T(8,128)S(1)}, u32[]{:S(2)}, u32[]{:S(2)}) %collective-permute-start.6) | collective-permute-done | bytes 2097184 | tf_op jit(solution)/shard_map/ppermute | solution.py:15
  385.5 4.8 %convolution_add_fusion = f32[1024,512]{1,0:T(8,128)S(1)} fusion(f32[1024,512]{1,0:T(8,128)S(1)} %collective-permute-done.6, bf16[1024,512]{1,0:T(8,128)(2,1)S(1)} %copy-done, f32[1024,4096]{0,1:T(8,128)} %convert_element_type.2, f32[1024,1024]{0,1:T(8,128)S(1)} %copy-done.5, f32[1024]{0:T(1024)S(1)} %select_reduce_fusion, f32[1024]{0:T(1024)S(1)} %bitcast.32, ...), kind=kOutput, calls=%fused_computation.32 | convolution fusion | flops 3230138368 | bytes 13651968 | tf_op jit(solution)/shard_map/dot_general | solution.py:24
  390.3 5.6 %collective-permute-start.7 = (f32[1024,512]{1,0:T(8,128)S(1)}, f32[1024,512]{1,0:T(8,128)S(1)}, u32[]{:S(2)}, u32[]{:S(2)}) collective-permute-start(f32[1024,512]{1,0:T(8,128)S(1)} %convolution_add_fusion), channel_id=1, source_target_pairs={{8,0},{16,8},{24,16},{32,24},{40,32},{48,40},{56,48},{64,56},{72,6... | collective-permute-start | bytes 6291464 | tf_op jit(solution)/shard_map/ppermute | solution.py:15
  395.9 0.0 collective-permute-done.3
  395.9 0.0 collective-permute-start.4
  395.9 17.9 %collective-permute-done.4 = bf16[1024,512]{1,0:T(8,128)(2,1)} collective-permute-done((bf16[1024,512]{1,0:T(8,128)(2,1)S(1)}, bf16[1024,512]{1,0:T(8,128)(2,1)}, u32[]{:S(2)}, u32[]{:S(2)}) %collective-permute-start.4) | collective-permute-done | bytes 1048608 | tf_op jit(solution)/shard_map/ppermute | solution.py:15
  413.9 2.8 fusion.44
  416.7 2.8 collective-permute-done.7
  419.5 0.5 add.134
  419.9 5.8 %collective-permute-start.8 = (f32[1024,512]{1,0:T(8,128)S(1)}, f32[1024,512]{1,0:T(8,128)}, u32[]{:S(2)}, u32[]{:S(2)}) collective-permute-start(f32[1024,512]{1,0:T(8,128)S(1)} %add.134), channel_id=1, source_target_pairs={{8,0},{16,8},{24,16},{32,24},{40,32},{48,40},{56,48},{64,56},{72,6... | collective-permute-start | bytes 6291464 | tf_op jit(solution)/shard_map/ppermute | solution.py:15
  425.8 5.4 %fusion.39 = f32[1024,512]{1,0:T(8,128)} fusion(bf16[1024,512]{1,0:T(8,128)(2,1)} %collective-permute-done.4, f32[1024,4096]{0,1:T(8,128)S(1)} %bitcast.24, f32[1024,1024]{0,1:T(8,128)S(1)} %copy-done.5, f32[1024]{0:T(1024)S(1)} %select_reduce_fusion, f32[1024]{0:T(1024)S(1)} %bitcast.34, f32[1024]{0:T(1024)S(1)} %multiply_subtract_fusion, ...), kind=kOutput, calls=%fused_computation.58 | convolution fusion | flops 3229614080 | bytes 11554816 | tf_op jit(solution)/shard_map/dot_general | solution.py:24
  431.2 4.3 fusion.46
  435.4 6.3 %fusion.34 = f32[1024,512]{1,0:T(8,128)S(1)} fusion(bf16[1024,512]{1,0:T(8,128)(2,1)S(1)} %copy-done, f32[1024,4096]{0,1:T(8,128)} %convert_element_type.2, f32[1024,1024]{0,1:T(8,128)} %all-gather.14.cloned.1.call-done, f32[1024]{0:T(1024)S(1)} %select_reduce_fusion, f32[1024]{0:T(1024)S(1)} %bitcast.36, f32[1024]{0:T(1024)S(1)} %multiply_subtract_fusion, ...), kind=kOutput, calls=%fused_computation.56 | convolution fusion | flops 3229614080 | bytes 11550720 | tf_op jit(solution)/shard_map/dot_general | solution.py:24
  441.7 0.0 copy-start.2
  441.7 7.6 %collective-permute-done.8 = f32[1024,512]{1,0:T(8,128)} collective-permute-done((f32[1024,512]{1,0:T(8,128)S(1)}, f32[1024,512]{1,0:T(8,128)}, u32[]{:S(2)}, u32[]{:S(2)}) %collective-permute-start.8) | collective-permute-done | bytes 2097184 | tf_op jit(solution)/shard_map/ppermute | solution.py:15
  449.3 3.4 add.135
  452.7 5.1 %fusion.36 = f32[1024,512]{1,0:T(8,128)S(1)} fusion(bf16[1024,512]{1,0:T(8,128)(2,1)S(1)} %copy-done.2, f32[1024,4096]{0,1:T(8,128)} %convert_element_type.2, f32[1024,1024]{0,1:T(8,128)S(1)} %copy-done.7, f32[1024]{0:T(1024)S(1)} %select_reduce_fusion, f32[1024]{0:T(1024)S(1)} %bitcast.37, f32[1024]{0:T(1024)S(1)} %multiply_subtract_fusion, ...), kind=kOutput, calls=%fused_computation.57 | convolution fusion | flops 3229614080 | bytes 11550720 | tf_op jit(solution)/shard_map/dot_general | solution.py:24
  457.9 0.0 collective-permute-done.5
  457.9 7.0 %add_add_fusion = f32[1024,512]{1,0:T(8,128)} fusion(f32[1024,512]{1,0:T(8,128)S(1)} %copy-done.11, f32[1024,512]{1,0:T(8,128)S(1)} %fusion.36, f32[1024,512]{1,0:T(8,128)S(1)} %copy-done.12, bf16[1024,512]{1,0:T(8,128)(2,1)} %collective-permute-done.5, f32[1024,4096]{0,1:T(8,128)} %convert_element_type.2, f32[1024,1024]{0,1:T(8,128)S(1)} %copy-done.4, ...), kind=kOutput, calls=%fused_computation.27 | convolution fusion | flops 3231186944 | bytes 17846272 | tf_op jit(solution)/shard_map/dot_general | solution.py:24
  (37 shorter events, 0.1 us)
Async XLA Ops:
  7.2 137.7 %copy-start.3 = (s32[1024]{0:T(1024)S(1)}, s32[1024]{0:T(1024)}, u32[]{:S(2)}) copy-start(s32[1024]{0:T(1024)} %param.7) | copy-start | bytes 12292
  7.2 137.7 %all-gather.6.cloned.1.call-start = ((), (), s32[]{:S(2)}) async-start(), calls=%async_computation.1 | async-start | bytes 9437184 | tf_op jit(solution)/shard_map/all_gather | solution.py:34
  7.9 197.1 %all-gather.8.cloned.1.call-start = ((), (), s32[]{:S(2)}) async-start(), calls=%async_computation.2 | async-start | bytes 4718592 | tf_op jit(solution)/shard_map/all_gather | solution.py:49
  34.7 40.5 %collective-permute-start = (bf16[128,4096]{0,1:T(8,128)(2,1)S(1)}, bf16[128,4096]{0,1:T(8,128)(2,1)S(1)}, u32[]{:S(2)}, u32[]{:S(2)}) collective-permute-start(bf16[128,4096]{0,1:T(8,128)(2,1)S(1)} %bitcast.27), channel_id=1, source_target_pairs={{120,0},{0,8},{8,16},{16,24},{24,32},{32,40},{40,48},{48,56},{56,6... | collective-permute-start | bytes 3145736 | tf_op jit(solution)/shard_map/ppermute | solution.py:15
  75.2 1.0 copy-start.8
  76.3 40.4 %collective-permute-start.1 = (bf16[128,4096]{0,1:T(8,128)(2,1)S(1)}, bf16[128,4096]{0,1:T(8,128)(2,1)S(1)}, u32[]{:S(2)}, u32[]{:S(2)}) collective-permute-start(bf16[128,4096]{0,1:T(8,128)(2,1)S(1)} %collective-permute-done), channel_id=1, source_target_pairs={{120,0},{0,8},{8,16},{16,24},{24,32},{32,40},{40,48},{48,56},{56,6... | collective-permute-start | bytes 3145736 | tf_op jit(solution)/shard_map/ppermute | solution.py:15
  116.7 27.2 %copy-start.9 = (bf16[128,4096]{0,1:T(8,128)(2,1)}, bf16[128,4096]{0,1:T(8,128)(2,1)S(1)}, u32[]{:S(2)}) copy-start(bf16[128,4096]{0,1:T(8,128)(2,1)S(1)} %collective-permute-done.1) | copy-start | bytes 3145732
  116.7 27.2 %collective-permute-start.2 = (bf16[128,4096]{0,1:T(8,128)(2,1)S(1)}, bf16[128,4096]{0,1:T(8,128)(2,1)S(1)}, u32[]{:S(2)}, u32[]{:S(2)}) collective-permute-start(bf16[128,4096]{0,1:T(8,128)(2,1)S(1)} %collective-permute-done.1), channel_id=1, source_target_pairs={{120,0},{0,8},{8,16},{16,24},{24,32},{32,40},{40,48},{48,56},{56,6... | collective-permute-start | bytes 3145736 | tf_op jit(solution)/shard_map/ppermute | solution.py:15
  143.9 1.0 copy-start.10
  154.9 104.3 %all-gather.10.cloned.1.call-start = ((), (), s32[]{:S(2)}) async-start(), calls=%async_computation.3 | async-start | bytes 4718592 | tf_op jit(solution)/shard_map/all_gather | solution.py:49
  207.7 106.3 %all-gather.12.cloned.1.call-start = ((), (), s32[]{:S(2)}) async-start(), calls=%async_computation.4 | async-start | bytes 4718592 | tf_op jit(solution)/shard_map/all_gather | solution.py:49
  261.8 173.6 %all-gather.14.cloned.1.call-start = ((), (), s32[]{:S(2)}) async-start(), calls=%async_computation.5 | async-start | bytes 4718592 | tf_op jit(solution)/shard_map/all_gather | solution.py:49
  287.2 29.5 %copy-start = (bf16[1024,512]{1,0:T(8,128)(2,1)S(1)}, bf16[1024,512]{1,0:T(8,128)(2,1)}, u32[]{:S(2)}) copy-start(bf16[1024,512]{1,0:T(8,128)(2,1)} %param.4) | copy-start | bytes 3145732
  316.7 9.9 %copy-start.1 = (bf16[1024,512]{1,0:T(8,128)(2,1)S(1)}, bf16[1024,512]{1,0:T(8,128)(2,1)}, u32[]{:S(2)}) copy-start(bf16[1024,512]{1,0:T(8,128)(2,1)} %param.5) | copy-start | bytes 3145732
  316.7 68.8 %copy-start.5 = (f32[1024,1024]{0,1:T(8,128)S(1)}, f32[1024,1024]{0,1:T(8,128)}, u32[]{:S(2)}) copy-start(f32[1024,1024]{0,1:T(8,128)} %all-gather.10.cloned.1.call-done) | copy-start | bytes 12582916
  316.7 97.1 %slice-start = ((s8[16777216]{0:T(1024)(128)(4,1)}), s8[4194304]{0:T(1024)(128)(4,1)S(1)}, s32[]{:S(2)}) async-start(s8[16777216]{0:T(1024)(128)(4,1)} %bitcast.23), calls=%async_computation.6 | async-start | bytes 8388608
  316.7 97.1 %slice-start.1 = ((s8[16777216]{0:T(1024)(128)(4,1)}), s8[4194304]{0:T(1024)(128)(4,1)S(1)}, s32[]{:S(2)}) async-start(s8[16777216]{0:T(1024)(128)(4,1)} %bitcast.23), calls=%async_computation.7 | async-start | bytes 8388608
  322.2 63.3 %collective-permute-start.6 = (f32[1024,512]{1,0:T(8,128)S(1)}, f32[1024,512]{1,0:T(8,128)S(1)}, u32[]{:S(2)}, u32[]{:S(2)}) collective-permute-start(f32[1024,512]{1,0:T(8,128)S(1)} %fusion.41), channel_id=1, source_target_pairs={{8,0},{16,8},{24,16},{32,24},{40,32},{48,40},{56,48},{64,56},{72,6... | collective-permute-start | bytes 6291464 | tf_op jit(solution)/shard_map/ppermute | solution.py:15
  326.6 69.3 %collective-permute-start.3 = (bf16[1024,512]{1,0:T(8,128)(2,1)S(1)}, bf16[1024,512]{1,0:T(8,128)(2,1)S(1)}, u32[]{:S(2)}, u32[]{:S(2)}) collective-permute-start(bf16[1024,512]{1,0:T(8,128)(2,1)S(1)} %copy-done.1), channel_id=1, source_target_pairs={{120,0},{0,8},{8,16},{16,24},{24,32},{32,40},{40,48},{48,56},{56,6... | collective-permute-start | bytes 3145736 | tf_op jit(solution)/shard_map/ppermute | solution.py:15
  326.6 87.2 %slice-start.2 = ((s8[16777216]{0:T(1024)(128)(4,1)}), s8[4194304]{0:T(1024)(128)(4,1)S(1)}, s32[]{:S(2)}) async-start(s8[16777216]{0:T(1024)(128)(4,1)} %bitcast.23), calls=%async_computation.8 | async-start | bytes 8388608
  326.6 87.2 %slice-start.3 = ((s8[16777216]{0:T(1024)(128)(4,1)}), s8[4194304]{0:T(1024)(128)(4,1)S(1)}, s32[]{:S(2)}) async-start(s8[16777216]{0:T(1024)(128)(4,1)} %bitcast.23), calls=%async_computation.9 | async-start | bytes 8388608
  326.7 87.2 %copy-start.6 = (f32[1024,1024]{0,1:T(8,128)S(1)}, f32[1024,1024]{0,1:T(8,128)}, u32[]{:S(2)}) copy-start(f32[1024,1024]{0,1:T(8,128)} %all-gather.12.cloned.1.call-done) | copy-start | bytes 12582916
  390.3 29.1 %collective-permute-start.7 = (f32[1024,512]{1,0:T(8,128)S(1)}, f32[1024,512]{1,0:T(8,128)S(1)}, u32[]{:S(2)}, u32[]{:S(2)}) collective-permute-start(f32[1024,512]{1,0:T(8,128)S(1)} %convolution_add_fusion), channel_id=1, source_target_pairs={{8,0},{16,8},{24,16},{32,24},{40,32},{48,40},{56,48},{64,56},{72,6... | collective-permute-start | bytes 6291464 | tf_op jit(solution)/shard_map/ppermute | solution.py:15
  395.9 17.9 %collective-permute-start.4 = (bf16[1024,512]{1,0:T(8,128)(2,1)S(1)}, bf16[1024,512]{1,0:T(8,128)(2,1)}, u32[]{:S(2)}, u32[]{:S(2)}) collective-permute-start(bf16[1024,512]{1,0:T(8,128)(2,1)S(1)} %collective-permute-done.3), channel_id=1, source_target_pairs={{120,0},{0,8},{8,16},{16,24},{24,32},{32,40},{40,48},{48,56},{56,6... | collective-permute-start | bytes 3145736 | tf_op jit(solution)/shard_map/ppermute | solution.py:15
  413.9 44.0 %collective-permute-start.5 = (bf16[1024,512]{1,0:T(8,128)(2,1)}, bf16[1024,512]{1,0:T(8,128)(2,1)}, u32[]{:S(2)}, u32[]{:S(2)}) collective-permute-start(bf16[1024,512]{1,0:T(8,128)(2,1)} %collective-permute-done.4), channel_id=1, source_target_pairs={{120,0},{0,8},{8,16},{16,24},{24,32},{32,40},{40,48},{48,56},{56,6... | collective-permute-start | bytes 3145736 | tf_op jit(solution)/shard_map/ppermute | solution.py:15
  419.9 29.4 %collective-permute-start.8 = (f32[1024,512]{1,0:T(8,128)S(1)}, f32[1024,512]{1,0:T(8,128)}, u32[]{:S(2)}, u32[]{:S(2)}) collective-permute-start(f32[1024,512]{1,0:T(8,128)S(1)} %add.134), channel_id=1, source_target_pairs={{8,0},{16,8},{24,16},{32,24},{40,32},{48,40},{56,48},{64,56},{72,6... | collective-permute-start | bytes 6291464 | tf_op jit(solution)/shard_map/ppermute | solution.py:15
  441.7 11.0 %copy-start.2 = (bf16[1024,512]{1,0:T(8,128)(2,1)S(1)}, bf16[1024,512]{1,0:T(8,128)(2,1)}, u32[]{:S(2)}) copy-start(bf16[1024,512]{1,0:T(8,128)(2,1)} %param.5) | copy-start | bytes 3145732
  441.7 11.0 %copy-start.7 = (f32[1024,1024]{0,1:T(8,128)S(1)}, f32[1024,1024]{0,1:T(8,128)}, u32[]{:S(2)}) copy-start(f32[1024,1024]{0,1:T(8,128)} %all-gather.14.cloned.1.call-done) | copy-start | bytes 12582916
  452.7 5.2 %copy-start.4 = (f32[1024,1024]{0,1:T(8,128)S(1)}, f32[1024,1024]{0,1:T(8,128)}, u32[]{:S(2)}) copy-start(f32[1024,1024]{0,1:T(8,128)} %all-gather.8.cloned.1.call-done) | copy-start | bytes 12582916
  452.7 5.2 %copy-start.11 = (f32[1024,512]{1,0:T(8,128)S(1)}, f32[1024,512]{1,0:T(8,128)}, u32[]{:S(2)}) copy-start(f32[1024,512]{1,0:T(8,128)} %fusion.39) | copy-start | bytes 6291460
  452.7 5.2 %copy-start.12 = (f32[1024,512]{1,0:T(8,128)S(1)}, f32[1024,512]{1,0:T(8,128)}, u32[]{:S(2)}) copy-start(f32[1024,512]{1,0:T(8,128)} %fusion.46) | copy-start | bytes 6291460
Sparse Core Ops, SparseCore 0:
  9.6 98.8 all-gather.5
  155.0 49.9 all-gather.7
  207.8 51.2 all-gather.9
  261.9 51.9 all-gather.11
  316.8 70.7 all-gather.13

commit v13 on v11

--- a/solution.py
+++ b/solution.py
@@ -13,6 +13,11 @@
     devices = range(lax.axis_size(axis))
     route = [((i - distance) % len(devices), i) for i in devices]
     return lax.ppermute(block, axis, route)
+
+
+def after(value, dep):
+    zero = 0.0 * dep[:1, :1]
+    return value + zero.astype(value.dtype)
 
 
 def wide_dot(a, b):
@@ -34,7 +39,7 @@
         held_cols.append(shifted(held_cols[-1], "loop", 1))
         held.append(shifted(held[-1], "loop", 1))
 
-    cols = jnp.concatenate(held_cols, 0)
+    cols = after(jnp.concatenate(held_cols, 0), held[-1])
     raw = jnp.einsum("qd,cd->qc", q_full, cols, preferred_element_type=jnp.float32)
     gathered = [
         lax.all_gather(raw[:, k * sub : (k + 1) * sub], "width", axis=1, tiled=True)

time: 452 us -> 478 us (1.058)
  waiting for transfers between devices: 269 us -> 323 us
  blocking collectives: 46.4 us -> 19.9 us
    all_gather x4, waiting for transfers between devices: 112 us -> 152 us  [per_device(): lax.all_gather(raw[:, k * sub:(k + 1) * sub], 'width', axis=1, tiled=True)]
    all_to_all x1 -> x0, blocking collectives: 26.1 us -> none  [per_device(): p_cols = lax.all_to_all(passages, 'width', 0, 1, tiled=True)]
    all_to_all x0 -> x1, waiting for transfers between devices: none -> 19.4 us  [per_device(): p_cols = lax.all_to_all(passages, 'width', 0, 1, tiled=True)]
    ppermute x9, starting transfers between devices: 18.9 us -> 9.97 us  [shifted(): return lax.ppermute(block, axis, route)]
    ppermute x9, waiting for transfers between devices: 155 us -> 149 us  [shifted(): return lax.ppermute(block, axis, route)]
    all_to_all x0 -> x1, starting transfers between devices: none -> 5.52 us  [per_device(): p_cols = lax.all_to_all(passages, 'width', 0, 1, tiled=True)]
    unnamed x25 -> x31, local copies, waits for them, and re-layouts: 12.1 us -> 12.1 us
  transfers between devices with their start and end apart: 14 -> 15, of which waited for: 8 -> 11; matrix products, arithmetic and copies ran while one was open for 19% -> 18% of each run, Pallas kernels for 0% -> 0%
where the time goes in v13:
time: 478 us; the launch traced here: 472 us
  waiting for transfers between devices  323 us (68%)
  matrix products  60.9 us (13%)
  other arithmetic  21.8 us (5%)
  blocking collectives  19.9 us (4%)
  starting transfers between devices  15.9 us (3%)
  local copies, waits for them, and re-layouts  15.3 us (3%)
  between operations  15.1 us (3%)
    all_gather x4, waiting for transfers between devices, per_device(): lax.all_gather(raw[:, k * sub:(k + 1) * sub], 'width', axis=1, tiled=True)  152 us
    ppermute x9, waiting for transfers between devices, shifted(): return lax.ppermute(block, axis, route)  149 us
    dot_general x8, matrix products, wide_dot(): jnp.dot(a, b, precision=lax.Precision.HIGH, preferred_element_type=jnp.fl...  51.7 us
    psum x1, blocking collectives, per_device(): stats = lax.psum(jnp.stack([pos_part, row_part], 0), 'width')  19.9 us
    all_to_all x1, waiting for transfers between devices, per_device(): p_cols = lax.all_to_all(passages, 'width', 0, 1, tiled=True)  19.4 us
    unnamed x31, local copies, waits for them, and re-layouts  12.1 us
    convert_element_type x1, other arithmetic, per_device(): teach = teacher.astype(jnp.float32)  11.3 us
    ppermute x9, starting transfers between devices, shifted(): return lax.ppermute(block, axis, route)  9.97 us
  transfers between devices with their start and end apart: 15, of which 11 were waited for; matrix products, arithmetic and copies ran while one was open for 18% of the time, Pallas kernels for 0%

profile of v13, /device:TPU:0, one launch (start us, length us, event | category | flops | bytes accessed | tf_op | source)
XLA Modules:
  0.0 471.6 jit_solution(14247802635397884580)
XLA Ops:
  7.2 0.0 copy-start.3
  7.2 0.0 all-gather.6.cloned.1.call-start
  7.2 0.7 all-gather.6.cloned.1.call-update
  7.9 5.5 %all-to-all-start = ((bf16[8,128,512]{2,1,0:T(8,128)(2,1)}), bf16[8,128,512]{2,1,0:T(8,128)(2,1)S(1)}, u32[]{:S(2)}, u32[]{:S(2)}) async-start(bf16[8,128,512]{2,1,0:T(8,128)(2,1)} %bitcast.24), calls=%async_computation | async-start | bytes 2097152 | tf_op jit(solution)/shard_map/all_to_all | solution.py:35
  13.4 0.0 all-gather.14.cloned.1.call-start
  13.5 0.1 collective-permute-start.3
  13.6 19.4 %all-to-all-done = bf16[8,128,512]{2,1,0:T(8,128)(2,1)S(1)} async-done(((bf16[8,128,512]{2,1,0:T(8,128)(2,1)}), bf16[8,128,512]{2,1,0:T(8,128)(2,1)S(1)}, u32[]{:S(2)}, u32[]{:S(2)}) %all-to-all-start) | async-done | bytes 1048608 | tf_op jit(solution)/shard_map/all_to_all | solution.py:35
  32.9 0.7 copy.8
  33.6 0.1 collective-permute-start
  33.7 35.4 %collective-permute-done.3 = bf16[1024,512]{1,0:T(8,128)(2,1)S(1)} collective-permute-done((bf16[1024,512]{1,0:T(8,128)(2,1)}, bf16[1024,512]{1,0:T(8,128)(2,1)S(1)}, u32[]{:S(2)}, u32[]{:S(2)}) %collective-permute-start.3) | collective-permute-done | bytes 1048608 | tf_op jit(solution)/shard_map/ppermute | solution.py:15
  69.1 0.0 collective-permute-start.4
  69.1 33.7 %collective-permute-done = bf16[128,4096]{0,1:T(8,128)(2,1)S(1)} collective-permute-done((bf16[128,4096]{0,1:T(8,128)(2,1)S(1)}, bf16[128,4096]{0,1:T(8,128)(2,1)S(1)}, u32[]{:S(2)}, u32[]{:S(2)}) %collective-permute-start) | collective-permute-done | bytes 1048608 | tf_op jit(solution)/shard_map/ppermute | solution.py:15
  102.8 0.0 collective-permute-start.1
  102.8 33.8 %collective-permute-done.4 = bf16[1024,512]{1,0:T(8,128)(2,1)} collective-permute-done((bf16[1024,512]{1,0:T(8,128)(2,1)S(1)}, bf16[1024,512]{1,0:T(8,128)(2,1)}, u32[]{:S(2)}, u32[]{:S(2)}) %collective-permute-start.4) | collective-permute-done | bytes 1048608 | tf_op jit(solution)/shard_map/ppermute | solution.py:15
  136.6 0.0 copy-done.10
  136.6 0.0 collective-permute-start.5
  136.6 18.6 %collective-permute-done.1 = bf16[128,4096]{0,1:T(8,128)(2,1)} collective-permute-done((bf16[128,4096]{0,1:T(8,128)(2,1)S(1)}, bf16[128,4096]{0,1:T(8,128)(2,1)}, u32[]{:S(2)}, u32[]{:S(2)}) %collective-permute-start.1) | collective-permute-done | bytes 1048608 | tf_op jit(solution)/shard_map/ppermute | solution.py:15
  155.2 0.0 collective-permute-start.2
  155.2 11.2 %collective-permute-done.5 = bf16[1024,512]{1,0:T(8,128)(2,1)} collective-permute-done((bf16[1024,512]{1,0:T(8,128)(2,1)}, bf16[1024,512]{1,0:T(8,128)(2,1)}, u32[]{:S(2)}, u32[]{:S(2)}) %collective-permute-start.5) | collective-permute-done | bytes 1048608 | tf_op jit(solution)/shard_map/ppermute | solution.py:15
  166.5 1.2 slice.44
  168.3 9.4 %collective-permute-done.2 = bf16[128,4096]{0,1:T(8,128)(2,1)} collective-permute-done((bf16[128,4096]{0,1:T(8,128)(2,1)}, bf16[128,4096]{0,1:T(8,128)(2,1)}, u32[]{:S(2)}, u32[]{:S(2)}) %collective-permute-start.2) | collective-permute-done | bytes 1048608 | tf_op jit(solution)/shard_map/ppermute | solution.py:15
  177.7 0.0 copy-done.8
  177.7 0.0 copy-done.3
  177.7 9.1 %select_reduce_fusion.1 = (f32[1024]{0:T(1024)S(1)}, f32[1024]{0:T(1024)S(1)}, f32[1024,512]{0,1:T(8,128)S(1)}) fusion(s32[1024]{0:T(1024)S(1)} %copy-done.3, s32[512]{0:T(512)S(1)} %fusion.27, bf16[1024,4096]{1,0:T(8,128)(2,1)} %all-gather.6.cloned.1.call-done, bf16[128,4096]{0,1:T(8,128)(2,1)} %collective-permute-done.2, ...), kind=kOutput, calls=%fused_computation.29 | convolution fusion | flops 4318558208 | bytes 14694402 | tf_op jit(solution)/shard_map/qd,cd->qc/dot_general | solution.py:43
  186.8 1.4 fusion.46
  188.2 0.0 all-gather.14.cloned.1.call-update
  188.2 0.0 all-gather.12.cloned.1.call-start
  188.3 0.7 all-gather.12.cloned.1.call-update
  188.9 0.0 all-gather.8.cloned.1.call-start
  189.0 0.5 all-gather.8.cloned.1.call-update
  189.5 0.2 all-gather.10.cloned.1.call-start
  189.7 0.4 all-gather.10.cloned.1.call-update
  190.1 12.1 %copy.9 = bf16[1024,4096]{0,1:T(8,128)(2,1)} copy(bf16[1024,4096]{1,0:T(8,128)(2,1)} %param.6) | data formatting | bytes 16777216 | tf_op args[2]
  202.2 11.3 %convert_element_type.2 = f32[1024,4096]{0,1:T(8,128)} convert(bf16[1024,4096]{0,1:T(8,128)(2,1)} %copy.9) | non-fusion elementwise | flops 4194304 | bytes 25165824 | tf_op jit(solution)/shard_map/convert_element_type | solution.py:51
  213.5 1.8 dynamic-slice_reduce_fusion
  215.3 0.0 copy-start.1
  215.3 6.4 %select_reduce_fusion = f32[1024]{0:T(1024)S(1)} fusion(s32[1024]{0:T(1024)S(1)} %copy-done.3, bf16[1024,4096]{0,1:T(8,128)(2,1)} %copy.9), kind=kLoop, calls=%fused_computation | loop fusion | flops 16776192 | bytes 8396800 | tf_op jit(solution)/shard_map/reduce_sum | solution.py:53
  221.7 19.9 %psum.7 = f32[2,1024]{1,0:T(2,128)S(1)} all-reduce(f32[2,1024]{1,0:T(2,128)S(1)} %pad_maximum_fusion), channel_id=1, replica_groups=mesh['loop'=16,'width'=8] {'width'}, use_global_device_ids=true, to_apply=%region_3.4 | all-reduce | flops 2048 | bytes 16384 | tf_op jit(solution)/shard_map/psum | solution.py:64
  241.7 0.0 all-gather.14.cloned.1.call-done
  241.7 0.0 copy-done.1
  241.7 7.4 %fusion.39 = f32[1024,512]{1,0:T(8,128)} fusion(bf16[1024,512]{1,0:T(8,128)(2,1)S(1)} %copy-done.1, f32[1024,4096]{0,1:T(8,128)} %convert_element_type.2, f32[1024,1024]{0,1:T(8,128)} %all-gather.14.cloned.1.call-done, f32[1024]{0:T(1024)S(1)} %select_reduce_fusion, f32[1024]{0:T(1024)S(1)} %bitcast.29, f32[1024]{0:T(1024)S(1)} %multiply_subtract_fusion, ...), kind=kOutput, calls=%fused_computation.57 | convolution fusion | flops 3229614080 | bytes 11554816 | tf_op jit(solution)/shard_map/dot_general | solution.py:24
  249.2 1.4 collective-permute-start.6
  250.6 61.1 %all-gather.12.cloned.1.call-done = f32[1024,1024]{0,1:T(8,128)} async-done(((f32[1024,128]{0,1:T(8,128)}), f32[1024,1024]{0,1:T(8,128)}) %all-gather.12.cloned.1.call-update) | async-done | bytes 4194320 | tf_op jit(solution)/shard_map/all_gather | solution.py:45
  311.7 0.0 collective-permute-done.6
  311.7 8.1 %convolution_add_fusion = f32[1024,512]{1,0:T(8,128)} fusion(f32[1024,512]{1,0:T(8,128)} %collective-permute-done.6, bf16[1024,512]{1,0:T(8,128)(2,1)S(1)} %copy-done.1, f32[1024,4096]{0,1:T(8,128)} %convert_element_type.2, f32[1024,1024]{0,1:T(8,128)} %all-gather.12.cloned.1.call-done, f32[1024]{0:T(1024)S(1)} %select_reduce_fusion, ...), kind=kOutput, calls=%fused_computation.33 | convolution fusion | flops 3230138368 | bytes 13651968 | tf_op jit(solution)/shard_map/dot_general | solution.py:24
  319.8 3.7 collective-permute-start.7
  323.5 54.5 %all-gather.8.cloned.1.call-done = f32[1024,1024]{0,1:T(8,128)} async-done(((f32[1024,128]{0,1:T(8,128)}), f32[1024,1024]{0,1:T(8,128)}) %all-gather.8.cloned.1.call-update) | async-done | bytes 4194320 | tf_op jit(solution)/shard_map/all_gather | solution.py:45
  378.0 0.0 copy-done
  378.0 7.7 %fusion.34 = f32[1024,512]{1,0:T(8,128)} fusion(bf16[1024,512]{1,0:T(8,128)(2,1)S(1)} %copy-done, f32[1024,4096]{0,1:T(8,128)} %convert_element_type.2, f32[1024,1024]{0,1:T(8,128)} %all-gather.8.cloned.1.call-done, f32[1024]{0:T(1024)S(1)} %select_reduce_fusion, f32[1024]{0:T(1024)S(1)} %bitcast.31, f32[1024]{0:T(1024)S(1)} %multiply_subtract_fusion, ...), kind=kOutput, calls=%fused_computation.55 | convolution fusion | flops 3229614080 | bytes 11550720 | tf_op jit(solution)/shard_map/dot_general | solution.py:24
  385.7 0.0 copy-done.7
  385.7 6.7 %fusion.37 = f32[1024,512]{1,0:T(8,128)} fusion(bf16[1024,512]{1,0:T(8,128)(2,1)} %collective-permute-done.4, f32[1024,4096]{0,1:T(8,128)} %convert_element_type.2, f32[1024,1024]{0,1:T(8,128)S(1)} %copy-done.7, f32[1024]{0:T(1024)S(1)} %select_reduce_fusion, f32[1024]{0:T(1024)S(1)} %bitcast.32, f32[1024]{0:T(1024)S(1)} %multiply_subtract_fusion, ...), kind=kOutput, calls=%fused_computation.56 | convolution fusion | flops 3229614080 | bytes 11554816 | tf_op jit(solution)/shard_map/dot_general | solution.py:24
  392.4 36.3 %all-gather.10.cloned.1.call-done = f32[1024,1024]{0,1:T(8,128)} async-done(((f32[1024,128]{0,1:T(8,128)}), f32[1024,1024]{0,1:T(8,128)}) %all-gather.10.cloned.1.call-update) | async-done | bytes 4194320 | tf_op jit(solution)/shard_map/all_gather | solution.py:45
  428.7 0.0 copy-done.2
  428.7 5.4 %fusion.42 = f32[1024,512]{1,0:T(8,128)S(1)} fusion(bf16[1024,512]{1,0:T(8,128)(2,1)S(1)} %copy-done.2, f32[1024,4096]{0,1:T(8,128)} %convert_element_type.2, f32[1024,1024]{0,1:T(8,128)} %all-gather.10.cloned.1.call-done, f32[1024]{0:T(1024)S(1)} %select_reduce_fusion, f32[1024]{0:T(1024)S(1)} %bitcast.33, f32[1024]{0:T(1024)S(1)} %multiply_subtract_fusion, ...), kind=kOutput, calls=%fused_computation.58 | convolution fusion | flops 3229614080 | bytes 11554816 | tf_op jit(solution)/shard_map/dot_general | solution.py:24
  434.1 0.0 slice-start.2
  434.1 0.0 collective-permute-done.7
  434.1 0.5 add.108
  434.6 0.0 slice-start.3
  434.6 4.7 collective-permute-start.8
  439.3 4.9 %fusion.32 = f32[1024,512]{1,0:T(8,128)S(1)} fusion(bf16[1024,512]{1,0:T(8,128)(2,1)S(1)} %copy-done.2, f32[1024,4096]{0,1:T(8,128)} %convert_element_type.2, f32[1024,1024]{0,1:T(8,128)S(1)} %copy-done.5, f32[1024]{0:T(1024)S(1)} %select_reduce_fusion, f32[1024]{0:T(1024)S(1)} %bitcast.34, f32[1024]{0:T(1024)S(1)} %multiply_subtract_fusion, ...), kind=kOutput, calls=%fused_computation.54 | convolution fusion | flops 3229614080 | bytes 11550720 | tf_op jit(solution)/shard_map/dot_general | solution.py:24
  444.3 4.2 fusion.44
  448.5 7.4 %add_add_fusion = f32[1024,512]{1,0:T(8,128)} fusion(f32[1024,512]{1,0:T(8,128)} %fusion.37, f32[1024,512]{1,0:T(8,128)} %fusion.34, f32[1024,512]{1,0:T(8,128)} %fusion.44, bf16[1024,512]{1,0:T(8,128)(2,1)} %collective-permute-done.5, f32[1024,4096]{0,1:T(8,128)S(1)} %bitcast.22, f32[1024,1024]{0,1:T(8,128)S(1)} %copy-done.4, ...), kind=kOutput, calls=%fused_computation.27 | convolution fusion | flops 3231186944 | bytes 17846272 | tf_op jit(solution)/shard_map/dot_general | solution.py:24
  455.9 6.9 %collective-permute-done.8 = f32[1024,512]{1,0:T(8,128)S(1)} collective-permute-done((f32[1024,512]{1,0:T(8,128)S(1)}, f32[1024,512]{1,0:T(8,128)S(1)}, u32[]{:S(2)}, u32[]{:S(2)}) %collective-permute-start.8) | collective-permute-done | bytes 2097184 | tf_op jit(solution)/shard_map/ppermute | solution.py:15
  462.8 1.8 add.109
  (29 shorter events, 0.1 us)
Async XLA Ops:
  7.2 170.5 %copy-start.3 = (s32[1024]{0:T(1024)S(1)}, s32[1024]{0:T(1024)}, u32[]{:S(2)}) copy-start(s32[1024]{0:T(1024)} %param.7) | copy-start | bytes 12292
  7.2 170.5 %all-gather.6.cloned.1.call-start = ((), (), s32[]{:S(2)}) async-start(), calls=%async_computation.1 | async-start | bytes 9437184 | tf_op jit(solution)/shard_map/all_gather | solution.py:34
  7.9 25.0 %all-to-all-start = ((bf16[8,128,512]{2,1,0:T(8,128)(2,1)}), bf16[8,128,512]{2,1,0:T(8,128)(2,1)S(1)}, u32[]{:S(2)}, u32[]{:S(2)}) async-start(bf16[8,128,512]{2,1,0:T(8,128)(2,1)} %bitcast.24), calls=%async_computation | async-start | bytes 2097152 | tf_op jit(solution)/shard_map/all_to_all | solution.py:35
  13.4 228.3 %all-gather.14.cloned.1.call-start = ((), (), s32[]{:S(2)}) async-start(), calls=%async_computation.5 | async-start | bytes 4718592 | tf_op jit(solution)/shard_map/all_gather | solution.py:45
  13.5 55.6 %collective-permute-start.3 = (bf16[1024,512]{1,0:T(8,128)(2,1)}, bf16[1024,512]{1,0:T(8,128)(2,1)S(1)}, u32[]{:S(2)}, u32[]{:S(2)}) collective-permute-start(bf16[1024,512]{1,0:T(8,128)(2,1)} %param.5), channel_id=1, source_target_pairs={{120,0},{0,8},{8,16},{16,24},{24,32},{32,40},{40,48},{48,56},{56,6... | collective-permute-start | bytes 3145736 | tf_op jit(solution)/shard_map/ppermute | solution.py:15
  33.6 69.2 %collective-permute-start = (bf16[128,4096]{0,1:T(8,128)(2,1)S(1)}, bf16[128,4096]{0,1:T(8,128)(2,1)S(1)}, u32[]{:S(2)}, u32[]{:S(2)}) collective-permute-start(bf16[128,4096]{0,1:T(8,128)(2,1)S(1)} %bitcast.25), channel_id=1, source_target_pairs={{120,0},{0,8},{8,16},{16,24},{24,32},{32,40},{40,48},{48,56},{56,6... | collective-permute-start | bytes 3145736 | tf_op jit(solution)/shard_map/ppermute | solution.py:15
  69.1 108.6 %copy-start.8 = (bf16[1024,512]{1,0:T(8,128)(2,1)}, bf16[1024,512]{1,0:T(8,128)(2,1)S(1)}, u32[]{:S(2)}) copy-start(bf16[1024,512]{1,0:T(8,128)(2,1)S(1)} %collective-permute-done.3) | copy-start | bytes 3145732
  69.1 67.5 %collective-permute-start.4 = (bf16[1024,512]{1,0:T(8,128)(2,1)S(1)}, bf16[1024,512]{1,0:T(8,128)(2,1)}, u32[]{:S(2)}, u32[]{:S(2)}) collective-permute-start(bf16[1024,512]{1,0:T(8,128)(2,1)S(1)} %collective-permute-done.3), channel_id=1, source_target_pairs={{120,0},{0,8},{8,16},{16,24},{24,32},{32,40},{40,48},{48,56},{56,6... | collective-permute-start | bytes 3145736 | tf_op jit(solution)/shard_map/ppermute | solution.py:15
  102.8 33.8 %copy-start.10 = (bf16[128,4096]{0,1:T(8,128)(2,1)}, bf16[128,4096]{0,1:T(8,128)(2,1)S(1)}, u32[]{:S(2)}) copy-start(bf16[128,4096]{0,1:T(8,128)(2,1)S(1)} %collective-permute-done) | copy-start | bytes 3145732
  102.8 52.4 %collective-permute-start.1 = (bf16[128,4096]{0,1:T(8,128)(2,1)S(1)}, bf16[128,4096]{0,1:T(8,128)(2,1)}, u32[]{:S(2)}, u32[]{:S(2)}) collective-permute-start(bf16[128,4096]{0,1:T(8,128)(2,1)S(1)} %collective-permute-done), channel_id=1, source_target_pairs={{120,0},{0,8},{8,16},{16,24},{24,32},{32,40},{40,48},{48,56},{56,6... | collective-permute-start | bytes 3145736 | tf_op jit(solution)/shard_map/ppermute | solution.py:15
  136.6 29.9 %collective-permute-start.5 = (bf16[1024,512]{1,0:T(8,128)(2,1)}, bf16[1024,512]{1,0:T(8,128)(2,1)}, u32[]{:S(2)}, u32[]{:S(2)}) collective-permute-start(bf16[1024,512]{1,0:T(8,128)(2,1)} %collective-permute-done.4), channel_id=1, source_target_pairs={{120,0},{0,8},{8,16},{16,24},{24,32},{32,40},{40,48},{48,56},{56,6... | collective-permute-start | bytes 3145736 | tf_op jit(solution)/shard_map/ppermute | solution.py:15
  155.2 22.5 %collective-permute-start.2 = (bf16[128,4096]{0,1:T(8,128)(2,1)}, bf16[128,4096]{0,1:T(8,128)(2,1)}, u32[]{:S(2)}, u32[]{:S(2)}) collective-permute-start(bf16[128,4096]{0,1:T(8,128)(2,1)} %collective-permute-done.1), channel_id=1, source_target_pairs={{120,0},{0,8},{8,16},{16,24},{24,32},{32,40},{40,48},{48,56},{56,6... | collective-permute-start | bytes 3145736 | tf_op jit(solution)/shard_map/ppermute | solution.py:15
  188.2 123.5 %all-gather.12.cloned.1.call-start = ((), (), s32[]{:S(2)}) async-start(), calls=%async_computation.4 | async-start | bytes 4718592 | tf_op jit(solution)/shard_map/all_gather | solution.py:45
  188.9 189.1 %all-gather.8.cloned.1.call-start = ((), (), s32[]{:S(2)}) async-start(), calls=%async_computation.2 | async-start | bytes 4718592 | tf_op jit(solution)/shard_map/all_gather | solution.py:45
  189.5 239.2 %all-gather.10.cloned.1.call-start = ((), (), s32[]{:S(2)}) async-start(), calls=%async_computation.3 | async-start | bytes 4718592 | tf_op jit(solution)/shard_map/all_gather | solution.py:45
  215.3 26.5 %copy-start.1 = (bf16[1024,512]{1,0:T(8,128)(2,1)S(1)}, bf16[1024,512]{1,0:T(8,128)(2,1)}, u32[]{:S(2)}) copy-start(bf16[1024,512]{1,0:T(8,128)(2,1)} %param.4) | copy-start | bytes 3145732
  249.2 62.5 %collective-permute-start.6 = (f32[1024,512]{1,0:T(8,128)}, f32[1024,512]{1,0:T(8,128)}, u32[]{:S(2)}, u32[]{:S(2)}) collective-permute-start(f32[1024,512]{1,0:T(8,128)} %fusion.39), channel_id=1, source_target_pairs={{8,0},{16,8},{24,16},{32,24},{40,32},{48,40},{56,48},{64,56},{72,6... | collective-permute-start | bytes 6291464 | tf_op jit(solution)/shard_map/ppermute | solution.py:15
  250.6 127.4 %copy-start = (bf16[1024,512]{1,0:T(8,128)(2,1)S(1)}, bf16[1024,512]{1,0:T(8,128)(2,1)}, u32[]{:S(2)}) copy-start(bf16[1024,512]{1,0:T(8,128)(2,1)} %param.5) | copy-start | bytes 3145732
  319.8 114.3 %collective-permute-start.7 = (f32[1024,512]{1,0:T(8,128)}, f32[1024,512]{1,0:T(8,128)S(1)}, u32[]{:S(2)}, u32[]{:S(2)}) collective-permute-start(f32[1024,512]{1,0:T(8,128)} %convolution_add_fusion), channel_id=1, source_target_pairs={{8,0},{16,8},{24,16},{32,24},{40,32},{48,40},{56,48},{64,56},{72,6... | collective-permute-start | bytes 6291464 | tf_op jit(solution)/shard_map/ppermute | solution.py:15
  378.0 7.7 %copy-start.7 = (f32[1024,1024]{0,1:T(8,128)S(1)}, f32[1024,1024]{0,1:T(8,128)}, u32[]{:S(2)}) copy-start(f32[1024,1024]{0,1:T(8,128)} %all-gather.12.cloned.1.call-done) | copy-start | bytes 12582916
  385.7 43.0 %copy-start.2 = (bf16[1024,512]{1,0:T(8,128)(2,1)S(1)}, bf16[1024,512]{1,0:T(8,128)(2,1)}, u32[]{:S(2)}) copy-start(bf16[1024,512]{1,0:T(8,128)(2,1)} %param.4) | copy-start | bytes 3145732
  428.7 10.6 %copy-start.5 = (f32[1024,1024]{0,1:T(8,128)S(1)}, f32[1024,1024]{0,1:T(8,128)}, u32[]{:S(2)}) copy-start(f32[1024,1024]{0,1:T(8,128)} %all-gather.8.cloned.1.call-done) | copy-start | bytes 12582916
  428.7 15.5 %slice-start = ((s8[16777216]{0:T(1024)(128)(4,1)}), s8[4194304]{0:T(1024)(128)(4,1)S(1)}, s32[]{:S(2)}) async-start(s8[16777216]{0:T(1024)(128)(4,1)} %bitcast.21), calls=%async_computation.6 | async-start | bytes 8388608
  428.7 15.5 %slice-start.1 = ((s8[16777216]{0:T(1024)(128)(4,1)}), s8[4194304]{0:T(1024)(128)(4,1)S(1)}, s32[]{:S(2)}) async-start(s8[16777216]{0:T(1024)(128)(4,1)} %bitcast.21), calls=%async_computation.7 | async-start | bytes 8388608
  434.1 10.1 %slice-start.2 = ((s8[16777216]{0:T(1024)(128)(4,1)}), s8[4194304]{0:T(1024)(128)(4,1)S(1)}, s32[]{:S(2)}) async-start(s8[16777216]{0:T(1024)(128)(4,1)} %bitcast.21), calls=%async_computation.8 | async-start | bytes 8388608
  434.6 9.7 %slice-start.3 = ((s8[16777216]{0:T(1024)(128)(4,1)}), s8[4194304]{0:T(1024)(128)(4,1)S(1)}, s32[]{:S(2)}) async-start(s8[16777216]{0:T(1024)(128)(4,1)} %bitcast.21), calls=%async_computation.9 | async-start | bytes 8388608
  434.6 9.7 %copy-start.6 = (f32[1024,1024]{0,1:T(8,128)S(1)}, f32[1024,1024]{0,1:T(8,128)}, u32[]{:S(2)}) copy-start(f32[1024,1024]{0,1:T(8,128)} %all-gather.10.cloned.1.call-done) | copy-start | bytes 12582916
  434.6 9.7 %copy-start.9 = (bf16[1024,512]{1,0:T(8,128)(2,1)S(1)}, bf16[1024,512]{1,0:T(8,128)(2,1)}, u32[]{:S(2)}) copy-start(bf16[1024,512]{1,0:T(8,128)(2,1)} %copy-done.8) | copy-start | bytes 3145732
  434.6 28.2 %collective-permute-start.8 = (f32[1024,512]{1,0:T(8,128)S(1)}, f32[1024,512]{1,0:T(8,128)S(1)}, u32[]{:S(2)}, u32[]{:S(2)}) collective-permute-start(f32[1024,512]{1,0:T(8,128)S(1)} %add.108), channel_id=1, source_target_pairs={{8,0},{16,8},{24,16},{32,24},{40,32},{48,40},{56,48},{64,56},{72,6... | collective-permute-start | bytes 6291464 | tf_op jit(solution)/shard_map/ppermute | solution.py:15
  444.2 4.2 copy-start.4
Sparse Core Ops, SparseCore 0:
  9.6 98.7 all-gather.5
  188.3 50.3 all-gather.13
  241.0 70.7 all-gather.11
  313.2 64.7 all-gather.7
  379.5 49.1 all-gather.9

commit v14 on v11

--- a/solution.py
+++ b/solution.py
@@ -43,16 +43,17 @@
     scores = SCALE * raw
 
     index = positives[:, None]
-    teach = teacher.astype(jnp.float32)
-    column = lax.broadcasted_iota(jnp.int32, teach.shape, 1)
-    t_pos = jnp.sum(jnp.where(column == index, teach, 0.0), 1, keepdims=True)
+    column = lax.broadcasted_iota(jnp.int32, teacher.shape, 1)
+    t_pos = jnp.sum(
+        jnp.where(column == index, teacher.astype(jnp.float32), 0.0), 1, keepdims=True
+    )
 
     local = lax.broadcasted_iota(jnp.int32, (1, STEPS * sub), 1)
     wcol = (local // sub) * rows + me * sub + local % sub
     hit = wcol == index
     teach_cols = lax.dynamic_slice_in_dim(
-        teach.reshape(rows, STEPS, width, sub), me, 1, 2
-    ).reshape(rows, STEPS * sub)
+        teacher.reshape(rows, STEPS, width, sub), me, 1, 2
+    ).reshape(rows, STEPS * sub).astype(jnp.float32)
 
     pos_part = jnp.sum(jnp.where(hit, scores, 0.0), 1)
     row_part = jnp.sum(scores, 1) - jnp.sum(teach_cols, 1)
@@ -67,7 +68,7 @@
     terms = []
     for k in range(STEPS):
         block_scores = SCALE * gathered[k]
-        errors = (s_pos - block_scores) - (t_pos - teach[:, k * rows : (k + 1) * rows])
+        errors = (s_pos - block_scores) - (t_pos - teacher[:, k * rows : (k + 1) * rows].astype(jnp.float32))
         block_hit = (block_col + k * rows == index).astype(jnp.float32)
         block_slopes = coef * (block_hit * total - errors)
         gq = wide_dot(block_slopes, held[k].astype(jnp.float32))

time: 452 us -> 444 us (0.982)
  local copies, waits for them, and re-layouts: 14.1 us -> 31.9 us
  starting transfers between devices: 19.1 us -> 9.9 us
  matrix products: 61.6 us -> 53.6 us
  waiting for transfers between devices: 269 us -> 264 us
    unnamed x25 -> x29, local copies, waits for them, and re-layouts: 12.1 us -> 23.9 us
    convert_element_type x1 -> x0, other arithmetic: 11.3 us -> none  [per_device(): teach = teacher.astype(jnp.float32)]
    ppermute x9, starting transfers between devices: 18.9 us -> 9.54 us  [shifted(): return lax.ppermute(block, axis, route)]
    all_gather x4, waiting for transfers between devices: 112 us -> 103 us  [per_device(): lax.all_gather(raw[:, k * sub:(k + 1) * sub], 'width', axis=1, tiled=True)]
    dot_general x8, matrix products: 53.1 us -> 45.1 us  [wide_dot(): jnp.dot(a, b, precision=lax.Precision.HIGH, preferred_element_type=jnp.fl...]
    slice x0 -> x1, local copies, waits for them, and re-layouts: none -> 5.92 us  [per_device(): teacher[:, k * rows:(k + 1) * rows].astype(jnp.float32)]
    reduce_sum x1, other arithmetic: 1.77 us -> 7.63 us  [per_device(): row_part = jnp.sum(scores, 1) - jnp.sum(teach_cols, 1)]
  transfers between devices with their start and end apart: 14 -> 14, of which waited for: 8 -> 8; matrix products, arithmetic and copies ran while one was open for 19% -> 21% of each run, Pallas kernels for 0% -> 0%
where the time goes in v14:
time: 444 us; the launch traced here: 439 us
  waiting for transfers between devices  264 us (59%)
  matrix products  53.6 us (12%)
  blocking collectives  46.4 us (10%)
  local copies, waits for them, and re-layouts  31.9 us (7%)
  other arithmetic  18.1 us (4%)
  between operations  14.6 us (3%)
  starting transfers between devices  9.9 us (2%)
    ppermute x9, waiting for transfers between devices, shifted(): return lax.ppermute(block, axis, route)  159 us
    all_gather x4, waiting for transfers between devices, per_device(): lax.all_gather(raw[:, k * sub:(k + 1) * sub], 'width', axis=1, tiled=True)  103 us
    dot_general x8, matrix products, wide_dot(): jnp.dot(a, b, precision=lax.Precision.HIGH, preferred_element_type=jnp.fl...  45.1 us
    all_to_all x1, blocking collectives, per_device(): p_cols = lax.all_to_all(passages, 'width', 0, 1, tiled=True)  26.1 us
    unnamed x29, local copies, waits for them, and re-layouts  23.9 us
    psum x1, blocking collectives, per_device(): stats = lax.psum(jnp.stack([pos_part, row_part], 0), 'width')  20.3 us
    ppermute x9, starting transfers between devices, shifted(): return lax.ppermute(block, axis, route)  9.54 us
  transfers between devices with their start and end apart: 14, of which 8 were waited for; matrix products, arithmetic and copies ran while one was open for 21% of the time, Pallas kernels for 0%

profile of v14, /device:TPU:0, one launch (start us, length us, event | category | flops | bytes accessed | tf_op | source)
XLA Modules:
  0.0 438.5 jit_solution(10185207552571837070)
XLA Ops:
  7.2 0.0 copy-start.6
  7.2 0.0 all-gather.6.cloned.1.call-start
  7.2 0.7 all-gather.6.cloned.1.call-update
  7.9 0.0 all-gather.14.cloned.1.call-start
  8.0 26.1 %all_to_all.19 = bf16[8,128,512]{2,1,0:T(8,128)(2,1)S(1)} all-to-all(bf16[8,128,512]{2,1,0:T(8,128)(2,1)} %bitcast.24), channel_id=1, replica_groups=mesh['loop'=16,'width'=8] {'width'}, dimensions={0} | all-to-all | bytes 2097152 | tf_op jit(solution)/shard_map/all_to_all | solution.py:30
  34.1 0.7 copy.14
  34.7 0.1 collective-permute-start
  34.8 40.4 %collective-permute-done = bf16[128,4096]{0,1:T(8,128)(2,1)S(1)} collective-permute-done((bf16[128,4096]{0,1:T(8,128)(2,1)S(1)}, bf16[128,4096]{0,1:T(8,128)(2,1)S(1)}, u32[]{:S(2)}, u32[]{:S(2)}) %collective-permute-start) | collective-permute-done | bytes 1048608 | tf_op jit(solution)/shard_map/ppermute | solution.py:15
  75.2 0.0 collective-permute-start.1
  75.2 40.4 %collective-permute-done.1 = bf16[128,4096]{0,1:T(8,128)(2,1)S(1)} collective-permute-done((bf16[128,4096]{0,1:T(8,128)(2,1)S(1)}, bf16[128,4096]{0,1:T(8,128)(2,1)S(1)}, u32[]{:S(2)}, u32[]{:S(2)}) %collective-permute-start.1) | collective-permute-done | bytes 1048608 | tf_op jit(solution)/shard_map/ppermute | solution.py:15
  115.7 0.0 collective-permute-start.2
  115.7 28.3 %collective-permute-done.2 = bf16[128,4096]{0,1:T(8,128)(2,1)} collective-permute-done((bf16[128,4096]{0,1:T(8,128)(2,1)S(1)}, bf16[128,4096]{0,1:T(8,128)(2,1)}, u32[]{:S(2)}, u32[]{:S(2)}) %collective-permute-start.2) | collective-permute-done | bytes 1048608 | tf_op jit(solution)/shard_map/ppermute | solution.py:15
  144.0 0.0 copy-done.6
  144.0 8.5 %select_reduce_fusion.1 = (f32[1024]{0:T(1024)S(1)}, f32[1024]{0:T(1024)S(1)}, f32[1024,512]{0,1:T(8,128)S(1)}) fusion(s32[1024]{0:T(1024)S(1)} %copy-done.6, s32[512]{0:T(512)S(1)} %fusion.23, bf16[1024,4096]{1,0:T(8,128)(2,1)} %all-gather.6.cloned.1.call-done, bf16[128,4096]{0,1:T(8,128)(2,1)} %collective-permute-done.2, ...), kind=kOutput, calls=%fused_computation.17 | convolution fusion | flops 4314363904 | bytes 14694400 | tf_op jit(solution)/shard_map/qd,cd->qc/dot_general | solution.py:38
  152.5 1.4 fusion.53
  153.8 0.0 all-gather.14.cloned.1.call-update
  153.9 0.0 all-gather.12.cloned.1.call-start
  153.9 0.7 all-gather.12.cloned.1.call-update
  154.6 0.0 all-gather.8.cloned.1.call-start
  154.7 0.5 all-gather.8.cloned.1.call-update
  155.2 0.2 all-gather.10.cloned.1.call-start
  155.4 0.4 all-gather.10.cloned.1.call-update
  155.8 9.5 %copy.23 = bf16[128,8,32,128]{3,2,1,0:T(8,128)(2,1)} copy(bf16[128,8,32,128]{3,1,2,0:T(8,128)(2,1)} %bitcast.21) | data formatting | bytes 16777216
  165.3 5.9 %fusion.52 = (bf16[1024,1024]{1,0:T(8,128)(2,1)}, bf16[1024,1024]{1,0:T(8,128)(2,1)}, bf16[1024,1024]{1,0:T(8,128)(2,1)}, bf16[1024,1024]{1,0:T(8,128)(2,1)S(1)}) fusion(bf16[1024,4096]{1,0:T(8,128)(2,1)} %param.6), kind=kLoop, calls=%fused_computation.71 | loop fusion | bytes 16777216 | tf_op jit(solution)/shard_map/slice | solution.py:71
  171.2 4.0 copy.22
  175.1 7.6 %convert_reduce_fusion = f32[1024]{0:T(1024)S(1)} fusion(bf16[1024,4,8,128]{3,2,1,0:T(8,128)(2,1)} %bitcast.22, s32[]{:T(128)S(6)} %select_n.36), kind=kLoop, calls=%fused_computation.16 | loop fusion | flops 1047552 | bytes 1052676 | tf_op jit(solution)/shard_map/reduce_sum | solution.py:59
  182.8 0.0 copy-start.3
  182.8 6.4 %select_reduce_fusion = f32[1024]{0:T(1024)S(1)} fusion(bf16[1024,4096]{1,0:T(8,128)(2,1)} %param.6, s32[1024]{0:T(1024)S(1)} %copy-done.6), kind=kLoop, calls=%fused_computation | loop fusion | flops 16776192 | bytes 8396800 | tf_op jit(solution)/shard_map/reduce_sum | solution.py:47
  189.2 20.3 %psum.7 = f32[2,1024]{1,0:T(2,128)S(1)} all-reduce(f32[2,1024]{1,0:T(2,128)S(1)} %pad_maximum_fusion), channel_id=1, replica_groups=mesh['loop'=16,'width'=8] {'width'}, use_global_device_ids=true, to_apply=%region_3.4 | all-reduce | flops 2048 | bytes 16384 | tf_op jit(solution)/shard_map/psum | solution.py:60
  209.6 0.0 all-gather.14.cloned.1.call-done
  209.6 0.0 copy-done.3
  209.6 0.0 copy-start.4
  209.6 7.1 %fusion.16 = f32[1024,512]{1,0:T(8,128)} fusion(bf16[1024,512]{1,0:T(8,128)(2,1)S(1)} %copy-done.3, bf16[1024,1024]{0,1:T(8,128)(2,1)} %copy.22, f32[1024,1024]{0,1:T(8,128)} %all-gather.14.cloned.1.call-done, f32[1024]{0:T(1024)S(1)} %select_reduce_fusion, f32[1024]{0:T(1024)S(1)} %bitcast.29, f32[1024]{0:T(1024)S(1)} %multiply_subtract_fusion, ...), kind=kOutput, calls=%fused_computation.26 | convolution fusion | flops 3230662656 | bytes 9457664 | tf_op jit(solution)/shard_map/dot_general | solution.py:19
  216.7 0.2 collective-permute-start.6
  216.9 0.0 copy-done.4
  216.9 0.5 collective-permute-start.3
  217.4 39.8 %collective-permute-done.3 = bf16[1024,512]{1,0:T(8,128)(2,1)} collective-permute-done((bf16[1024,512]{1,0:T(8,128)(2,1)S(1)}, bf16[1024,512]{1,0:T(8,128)(2,1)}, u32[]{:S(2)}, u32[]{:S(2)}) %collective-permute-start.3) | collective-permute-done | bytes 1048608 | tf_op jit(solution)/shard_map/ppermute | solution.py:15
  257.1 0.0 collective-permute-start.4
  257.1 3.9 copy.21
  261.1 3.9 copy.20
  265.0 2.5 copy.19
  267.6 9.1 %all-gather.12.cloned.1.call-done = f32[1024,1024]{0,1:T(8,128)} async-done(((f32[1024,128]{0,1:T(8,128)}), f32[1024,1024]{0,1:T(8,128)}) %all-gather.12.cloned.1.call-update) | async-done | bytes 4194320 | tf_op jit(solution)/shard_map/all_gather | solution.py:40
  276.7 0.0 collective-permute-done.6
  276.7 7.6 %convolution_add_fusion = f32[1024,512]{1,0:T(8,128)} fusion(f32[1024,512]{1,0:T(8,128)} %collective-permute-done.6, bf16[1024,512]{1,0:T(8,128)(2,1)S(1)} %copy-done.3, bf16[1024,1024]{0,1:T(8,128)(2,1)} %copy.21, f32[1024,1024]{0,1:T(8,128)} %all-gather.12.cloned.1.call-done, f32[1024]{0:T(1024)S(1)} %select_reduce_fusion, f32[1024]{0:T(1024)S(1)} %bitcast.30, ...), kind=kOutput, calls=%fused_computation.20 | convolution fusion | flops 3231186944 | bytes 11554816 | tf_op jit(solution)/shard_map/dot_general | solution.py:19
  284.3 3.8 collective-permute-start.7
  288.1 0.0 collective-permute-done.4
  288.1 0.2 collective-permute-start.5
  288.4 55.0 %all-gather.8.cloned.1.call-done = f32[1024,1024]{0,1:T(8,128)} async-done(((f32[1024,128]{0,1:T(8,128)}), f32[1024,1024]{0,1:T(8,128)}) %all-gather.8.cloned.1.call-update) | async-done | bytes 4194320 | tf_op jit(solution)/shard_map/all_gather | solution.py:40
  343.4 5.8 %fusion.11 = f32[1024,512]{1,0:T(8,128)S(1)} fusion(bf16[1024,512]{1,0:T(8,128)(2,1)S(1)} %copy-done.3, bf16[1024,1024]{0,1:T(8,128)(2,1)} %copy.19, f32[1024,1024]{0,1:T(8,128)} %all-gather.8.cloned.1.call-done, f32[1024]{0:T(1024)S(1)} %select_reduce_fusion, f32[1024]{0:T(1024)S(1)} %bitcast.31, f32[1024]{0:T(1024)S(1)} %multiply_subtract_fusion, ...), kind=kOutput, calls=%fused_computation.21 | convolution fusion | flops 3230662656 | bytes 9453568 | tf_op jit(solution)/shard_map/dot_general | solution.py:19
  349.2 6.3 %fusion.15 = f32[1024,512]{1,0:T(8,128)} fusion(bf16[1024,512]{1,0:T(8,128)(2,1)} %collective-permute-done.4, bf16[1024,1024]{0,1:T(8,128)(2,1)} %copy.21, f32[1024,1024]{0,1:T(8,128)S(1)} %copy-done.10, f32[1024]{0:T(1024)S(1)} %select_reduce_fusion, f32[1024]{0:T(1024)S(1)} %bitcast.32, f32[1024]{0:T(1024)S(1)} %multiply_subtract_fusion, ...), kind=kOutput, calls=%fused_computation.25 | convolution fusion | flops 3230662656 | bytes 9457664 | tf_op jit(solution)/shard_map/dot_general | solution.py:19
  355.5 38.5 %all-gather.10.cloned.1.call-done = f32[1024,1024]{0,1:T(8,128)} async-done(((f32[1024,128]{0,1:T(8,128)}), f32[1024,1024]{0,1:T(8,128)}) %all-gather.10.cloned.1.call-update) | async-done | bytes 4194320 | tf_op jit(solution)/shard_map/all_gather | solution.py:40
  394.0 5.1 %fusion.13 = f32[1024,512]{1,0:T(8,128)S(1)} fusion(bf16[1024,512]{1,0:T(8,128)(2,1)S(1)} %copy-done.3, bf16[1024,1024]{0,1:T(8,128)(2,1)} %copy.20, f32[1024,1024]{0,1:T(8,128)} %all-gather.10.cloned.1.call-done, f32[1024]{0:T(1024)S(1)} %select_reduce_fusion, f32[1024]{0:T(1024)S(1)} %bitcast.33, f32[1024]{0:T(1024)S(1)} %multiply_subtract_fusion, ...), kind=kOutput, calls=%fused_computation.23 | convolution fusion | flops 3230662656 | bytes 9457664 | tf_op jit(solution)/shard_map/dot_general | solution.py:19
  399.2 0.0 copy-start.5
  399.2 0.0 collective-permute-done.7
  399.2 2.2 add.95
  401.4 4.7 %collective-permute-start.8 = (f32[1024,512]{1,0:T(8,128)S(1)}, f32[1024,512]{1,0:T(8,128)S(1)}, u32[]{:S(2)}, u32[]{:S(2)}) collective-permute-start(f32[1024,512]{1,0:T(8,128)S(1)} %add.95), channel_id=1, source_target_pairs={{8,0},{16,8},{24,16},{32,24},{40,32},{48,40},{56,48},{64,56},{72,6... | collective-permute-start | bytes 6291464 | tf_op jit(solution)/shard_map/ppermute | solution.py:15
  406.1 0.0 copy-done.2
  406.1 3.0 fusion.12
  409.1 0.0 copy-start.11
  409.2 4.4 fusion.14
  413.5 0.0 collective-permute-done.5
  413.6 5.8 %add_add_fusion = f32[1024,512]{1,0:T(8,128)} fusion(f32[1024,512]{1,0:T(8,128)S(1)} %copy-done.11, f32[1024,512]{1,0:T(8,128)S(1)} %fusion.12, f32[1024,512]{1,0:T(8,128)S(1)} %fusion.14, bf16[1024,512]{1,0:T(8,128)(2,1)} %collective-permute-done.5, bf16[1024,1024]{0,1:T(8,128)(2,1)S(1)} %copy-done, f32[1024,1024]{0,1:T(8,128)S(1)} %copy-done.7, ...), kind=kOutput, calls=%fused_computation.15 | convolution fusion | flops 3232235520 | bytes 15749120 | tf_op jit(solution)/shard_map/dot_general | solution.py:19
  419.4 10.3 %collective-permute-done.8 = f32[1024,512]{1,0:T(8,128)S(1)} collective-permute-done((f32[1024,512]{1,0:T(8,128)S(1)}, f32[1024,512]{1,0:T(8,128)S(1)}, u32[]{:S(2)}, u32[]{:S(2)}) %collective-permute-start.8) | collective-permute-done | bytes 2097184 | tf_op jit(solution)/shard_map/ppermute | solution.py:15
  429.7 1.8 add.96
  (24 shorter events, 0.1 us)
Async XLA Ops:
  7.2 136.8 %copy-start.6 = (s32[1024]{0:T(1024)S(1)}, s32[1024]{0:T(1024)}, u32[]{:S(2)}) copy-start(s32[1024]{0:T(1024)} %param.7) | copy-start | bytes 12292
  7.2 136.8 %all-gather.6.cloned.1.call-start = ((), (), s32[]{:S(2)}) async-start(), calls=%async_computation.1 | async-start | bytes 9437184 | tf_op jit(solution)/shard_map/all_gather | solution.py:29
  7.9 201.7 %all-gather.14.cloned.1.call-start = ((), (), s32[]{:S(2)}) async-start(), calls=%async_computation.5 | async-start | bytes 4718592 | tf_op jit(solution)/shard_map/all_gather | solution.py:40
  34.7 40.5 %collective-permute-start = (bf16[128,4096]{0,1:T(8,128)(2,1)S(1)}, bf16[128,4096]{0,1:T(8,128)(2,1)S(1)}, u32[]{:S(2)}, u32[]{:S(2)}) collective-permute-start(bf16[128,4096]{0,1:T(8,128)(2,1)S(1)} %bitcast.25), channel_id=1, source_target_pairs={{120,0},{0,8},{8,16},{16,24},{24,32},{32,40},{40,48},{48,56},{56,6... | collective-permute-start | bytes 3145736 | tf_op jit(solution)/shard_map/ppermute | solution.py:15
  75.2 40.4 %collective-permute-start.1 = (bf16[128,4096]{0,1:T(8,128)(2,1)S(1)}, bf16[128,4096]{0,1:T(8,128)(2,1)S(1)}, u32[]{:S(2)}, u32[]{:S(2)}) collective-permute-start(bf16[128,4096]{0,1:T(8,128)(2,1)S(1)} %collective-permute-done), channel_id=1, source_target_pairs={{120,0},{0,8},{8,16},{16,24},{24,32},{32,40},{40,48},{48,56},{56,6... | collective-permute-start | bytes 3145736 | tf_op jit(solution)/shard_map/ppermute | solution.py:15
  115.7 28.3 %collective-permute-start.2 = (bf16[128,4096]{0,1:T(8,128)(2,1)S(1)}, bf16[128,4096]{0,1:T(8,128)(2,1)}, u32[]{:S(2)}, u32[]{:S(2)}) collective-permute-start(bf16[128,4096]{0,1:T(8,128)(2,1)S(1)} %collective-permute-done.1), channel_id=1, source_target_pairs={{120,0},{0,8},{8,16},{16,24},{24,32},{32,40},{40,48},{48,56},{56,6... | collective-permute-start | bytes 3145736 | tf_op jit(solution)/shard_map/ppermute | solution.py:15
  153.9 122.8 %all-gather.12.cloned.1.call-start = ((), (), s32[]{:S(2)}) async-start(), calls=%async_computation.4 | async-start | bytes 4718592 | tf_op jit(solution)/shard_map/all_gather | solution.py:40
  154.6 188.8 %all-gather.8.cloned.1.call-start = ((), (), s32[]{:S(2)}) async-start(), calls=%async_computation.2 | async-start | bytes 4718592 | tf_op jit(solution)/shard_map/all_gather | solution.py:40
  155.2 238.8 %all-gather.10.cloned.1.call-start = ((), (), s32[]{:S(2)}) async-start(), calls=%async_computation.3 | async-start | bytes 4718592 | tf_op jit(solution)/shard_map/all_gather | solution.py:40
  182.8 26.8 %copy-start.3 = (bf16[1024,512]{1,0:T(8,128)(2,1)S(1)}, bf16[1024,512]{1,0:T(8,128)(2,1)}, u32[]{:S(2)}) copy-start(bf16[1024,512]{1,0:T(8,128)(2,1)} %param.4) | copy-start | bytes 3145732
  209.6 7.3 %copy-start.4 = (bf16[1024,512]{1,0:T(8,128)(2,1)S(1)}, bf16[1024,512]{1,0:T(8,128)(2,1)}, u32[]{:S(2)}) copy-start(bf16[1024,512]{1,0:T(8,128)(2,1)} %param.5) | copy-start | bytes 3145732
  216.7 60.0 %collective-permute-start.6 = (f32[1024,512]{1,0:T(8,128)}, f32[1024,512]{1,0:T(8,128)}, u32[]{:S(2)}, u32[]{:S(2)}) collective-permute-start(f32[1024,512]{1,0:T(8,128)} %fusion.16), channel_id=1, source_target_pairs={{8,0},{16,8},{24,16},{32,24},{40,32},{48,40},{56,48},{64,56},{72,6... | collective-permute-start | bytes 6291464 | tf_op jit(solution)/shard_map/ppermute | solution.py:15
  216.9 40.3 %collective-permute-start.3 = (bf16[1024,512]{1,0:T(8,128)(2,1)S(1)}, bf16[1024,512]{1,0:T(8,128)(2,1)}, u32[]{:S(2)}, u32[]{:S(2)}) collective-permute-start(bf16[1024,512]{1,0:T(8,128)(2,1)S(1)} %copy-done.4), channel_id=1, source_target_pairs={{120,0},{0,8},{8,16},{16,24},{24,32},{32,40},{40,48},{48,56},{56,6... | collective-permute-start | bytes 3145736 | tf_op jit(solution)/shard_map/ppermute | solution.py:15
  257.1 31.0 %collective-permute-start.4 = (bf16[1024,512]{1,0:T(8,128)(2,1)}, bf16[1024,512]{1,0:T(8,128)(2,1)}, u32[]{:S(2)}, u32[]{:S(2)}) collective-permute-start(bf16[1024,512]{1,0:T(8,128)(2,1)} %collective-permute-done.3), channel_id=1, source_target_pairs={{120,0},{0,8},{8,16},{16,24},{24,32},{32,40},{40,48},{48,56},{56,6... | collective-permute-start | bytes 3145736 | tf_op jit(solution)/shard_map/ppermute | solution.py:15
  284.3 114.9 %collective-permute-start.7 = (f32[1024,512]{1,0:T(8,128)}, f32[1024,512]{1,0:T(8,128)}, u32[]{:S(2)}, u32[]{:S(2)}) collective-permute-start(f32[1024,512]{1,0:T(8,128)} %convolution_add_fusion), channel_id=1, source_target_pairs={{8,0},{16,8},{24,16},{32,24},{40,32},{48,40},{56,48},{64,56},{72,6... | collective-permute-start | bytes 6291464 | tf_op jit(solution)/shard_map/ppermute | solution.py:15
  288.1 125.4 %collective-permute-start.5 = (bf16[1024,512]{1,0:T(8,128)(2,1)}, bf16[1024,512]{1,0:T(8,128)(2,1)}, u32[]{:S(2)}, u32[]{:S(2)}) collective-permute-start(bf16[1024,512]{1,0:T(8,128)(2,1)} %collective-permute-done.4), channel_id=1, source_target_pairs={{120,0},{0,8},{8,16},{16,24},{24,32},{32,40},{40,48},{48,56},{56,6... | collective-permute-start | bytes 3145736 | tf_op jit(solution)/shard_map/ppermute | solution.py:15
  343.4 5.8 %copy-start.10 = (f32[1024,1024]{0,1:T(8,128)S(1)}, f32[1024,1024]{0,1:T(8,128)}, u32[]{:S(2)}) copy-start(f32[1024,1024]{0,1:T(8,128)} %all-gather.12.cloned.1.call-done) | copy-start | bytes 12582916
  394.0 12.1 %copy-start.8 = (f32[1024,1024]{0,1:T(8,128)S(1)}, f32[1024,1024]{0,1:T(8,128)}, u32[]{:S(2)}) copy-start(f32[1024,1024]{0,1:T(8,128)} %all-gather.8.cloned.1.call-done) | copy-start | bytes 12582916
  399.2 7.0 %copy-start.2 = (bf16[1024,1024]{0,1:T(8,128)(2,1)S(1)}, bf16[1024,1024]{0,1:T(8,128)(2,1)}, u32[]{:S(2)}) copy-start(bf16[1024,1024]{0,1:T(8,128)(2,1)} %copy.19) | copy-start | bytes 6291460
  399.2 7.0 %copy-start.5 = (bf16[1024,512]{1,0:T(8,128)(2,1)S(1)}, bf16[1024,512]{1,0:T(8,128)(2,1)}, u32[]{:S(2)}) copy-start(bf16[1024,512]{1,0:T(8,128)(2,1)} %param.5) | copy-start | bytes 3145732
  401.4 7.7 %copy-start.1 = (bf16[1024,1024]{0,1:T(8,128)(2,1)S(1)}, bf16[1024,1024]{0,1:T(8,128)(2,1)}, u32[]{:S(2)}) copy-start(bf16[1024,1024]{0,1:T(8,128)(2,1)} %copy.20) | copy-start | bytes 6291460
  401.4 7.7 %copy-start.9 = (f32[1024,1024]{0,1:T(8,128)S(1)}, f32[1024,1024]{0,1:T(8,128)}, u32[]{:S(2)}) copy-start(f32[1024,1024]{0,1:T(8,128)} %all-gather.10.cloned.1.call-done) | copy-start | bytes 12582916
  401.4 28.3 %collective-permute-start.8 = (f32[1024,512]{1,0:T(8,128)S(1)}, f32[1024,512]{1,0:T(8,128)S(1)}, u32[]{:S(2)}, u32[]{:S(2)}) collective-permute-start(f32[1024,512]{1,0:T(8,128)S(1)} %add.95), channel_id=1, source_target_pairs={{8,0},{16,8},{24,16},{32,24},{40,32},{48,40},{56,48},{64,56},{72,6... | collective-permute-start | bytes 6291464 | tf_op jit(solution)/shard_map/ppermute | solution.py:15
  409.1 4.4 %copy-start = (bf16[1024,1024]{0,1:T(8,128)(2,1)S(1)}, bf16[1024,1024]{0,1:T(8,128)(2,1)}, u32[]{:S(2)}) copy-start(bf16[1024,1024]{0,1:T(8,128)(2,1)} %copy.22) | copy-start | bytes 6291460
  409.1 4.4 %copy-start.7 = (f32[1024,1024]{0,1:T(8,128)S(1)}, f32[1024,1024]{0,1:T(8,128)}, u32[]{:S(2)}) copy-start(f32[1024,1024]{0,1:T(8,128)} %all-gather.14.cloned.1.call-done) | copy-start | bytes 12582916
  409.1 4.4 %copy-start.11 = (f32[1024,512]{1,0:T(8,128)S(1)}, f32[1024,512]{1,0:T(8,128)}, u32[]{:S(2)}) copy-start(f32[1024,512]{1,0:T(8,128)} %fusion.15) | copy-start | bytes 6291460
Sparse Core Ops, SparseCore 0:
  9.6 98.8 all-gather.5
  154.0 50.4 all-gather.13
  206.2 70.4 all-gather.11
  278.2 65.1 all-gather.7
  344.9 49.0 all-gather.9
